TPU v7x, 32 devices: a whole 2x2x4 slice. The times are simulated.
32 devices in a mesh: blk: 4 (over x, core), st: 8 (over z, y).
Axes of the slice: x: 2, y: 2, z: 4, core: 2. Of those that a mesh axis runs over, the one named last changes fastest.
Arguments:
- voltages: bfloat16 [2, 4, 512, 34176], P(None, 'blk', 'st'), may hold values from -6 to 6
- filter_coeffs: float32 [12, 128], replicated, may hold values from -1.75 to 1.75
- station_gain: float32 [512], P('st'), may hold values from 0.5 to 5
- flags: int32 [4, 512], P('blk', 'st'), may hold values 0 or 1
- steer_index: int32 [512, 128], replicated, may hold values from 0 to 4095
Outputs:
- beams: bfloat16 [2, 128, 4, 256, 128], P(None, 'st', 'blk')
All inputs are finite; a program needn't handle non-finite values. No bound on the sum of `flags` on one device may be relied on, other than what follows from the above.
Results may differ from a plain program's by a relative error of at most 0.0074.
Values may be sent and summed in bfloat16 or wider, within the bound.
No kernel may reach another device: no remote copies, remote signals or barrier semaphores. Data moves between devices by JAX's collectives and lax.ppermute only.
A program may use at most 320 MiB of HBM per device.

v0:
```python
import math

import jax
import jax.numpy as jnp
from jax import lax
from jax.sharding import PartitionSpec as P

PHASES = 4096


def dft_tables(width):
    counter = jnp.arange(width, dtype=jnp.int32)
    product = counter[:, None] * counter[None, :] % width
    angle = product.astype(jnp.float32) * (2.0 * math.pi / width)
    factor = 1.0 / math.sqrt(width)
    return (
        (jnp.cos(angle) * factor).astype(jnp.bfloat16),
        (jnp.sin(angle) * factor).astype(jnp.bfloat16),
    )


def polyphase(samples, filter_coeffs, row_gain):
    ntaps = filter_coeffs.shape[0]
    width = filter_coeffs.shape[1]
    grid = samples.astype(jnp.float32).reshape(2, samples.shape[1], -1, width)
    count = grid.shape[2] - ntaps + 1
    filtered = filter_coeffs[0][None, None, None, :] * grid[:, :, 0:count, :]
    for tap_no in range(1, ntaps):
        filtered = (
            filtered
            + filter_coeffs[tap_no][None, None, None, :] * grid[:, :, tap_no : tap_no + count, :]
        )
    return (filtered * row_gain[None, :, None, None]).astype(jnp.bfloat16)


def transform(filtered, cos_table, sin_table):
    width = cos_table.shape[0]
    flat_re = filtered[0].reshape(-1, width)
    flat_im = filtered[1].reshape(-1, width)
    out_re = jnp.dot(flat_re, cos_table, preferred_element_type=jnp.float32) + jnp.dot(
        flat_im, sin_table, preferred_element_type=jnp.float32
    )
    out_im = jnp.dot(flat_im, cos_table, preferred_element_type=jnp.float32) - jnp.dot(
        flat_re, sin_table, preferred_element_type=jnp.float32
    )
    return jnp.stack([out_re, out_im]).astype(jnp.bfloat16).reshape(filtered.shape)


def batched(matrix, vectors):
    return jnp.einsum("ksu,kub->ksb", matrix, vectors, precision=lax.Precision.HIGHEST)


def iterate(rows_re, rows_im, steer_re, steer_im, diag_total, load, collect, combine):
    weight_re = steer_re / diag_total
    weight_im = steer_im / diag_total
    for sweep_no in range(2):
        full_re, full_im = collect(weight_re, weight_im)
        prod_re = batched(rows_re, full_re) - batched(rows_im, full_im)
        prod_im = batched(rows_re, full_im) + batched(rows_im, full_re)
        prod_re, prod_im = combine(prod_re, prod_im)
        next_re = weight_re + 0.5 * (steer_re - prod_re - load * weight_re) / diag_total
        next_im = weight_im + 0.5 * (steer_im - prod_im - load * weight_im) / diag_total
        weight_re, weight_im = (next_re, next_im)
    return collect(weight_re, weight_im)


def unchanged(part_re, part_im):
    return (part_re, part_im)


def local(voltages, filter_coeffs, station_gain, flags, steer_index):
    cos_table, sin_table = dft_tables(filter_coeffs.shape[1])
    row_gain = station_gain * flags[0].astype(jnp.float32)
    filtered = polyphase(voltages[:, 0], filter_coeffs, row_gain)
    local_spec = transform(filtered, cos_table, sin_table)
    spectra = lax.all_to_all(local_spec, "st", split_axis=3, concat_axis=1, tiled=True)
    stations = spectra.shape[1]
    chans = spectra.shape[3]
    counted = lax.axis_size("blk") * spectra.shape[2]
    spec_re = spectra[0]
    spec_im = spectra[1]
    cov_re = jnp.einsum(
        "stk,utk->ksu", spec_re, spec_re, preferred_element_type=jnp.float32
    ) + jnp.einsum("stk,utk->ksu", spec_im, spec_im, preferred_element_type=jnp.float32)
    cov_im = jnp.einsum(
        "stk,utk->ksu", spec_im, spec_re, preferred_element_type=jnp.float32
    ) - jnp.einsum("stk,utk->ksu", spec_re, spec_im, preferred_element_type=jnp.float32)
    channel_ids = lax.axis_index("st") * chans + jnp.arange(chans, dtype=jnp.int32)
    total_re, total_im = lax.psum((cov_re, cov_im), "blk")
    rows_re = total_re / counted
    rows_im = total_im / counted
    diag_part = jnp.diagonal(rows_re, axis1=1, axis2=2)
    load = jnp.sum(diag_part, axis=1) / stations + 1e-05
    phase_int = steer_index[None, :, :] * (channel_ids + 1)[:, None, None] % PHASES
    angle = phase_int.astype(jnp.float32) * (2.0 * math.pi / PHASES)
    steer_re = jnp.cos(angle)
    steer_im = jnp.sin(angle)
    load_full = load[:, None, None]
    diag_total = (diag_part + load[:, None])[:, :, None]
    weight_re, weight_im = iterate(
        rows_re, rows_im, steer_re, steer_im, diag_total, load_full, unchanged, unchanged
    )
    half_re = weight_re.astype(jnp.bfloat16)
    half_im = weight_im.astype(jnp.bfloat16)
    beam_re = jnp.einsum(
        "ksb,stk->btk", half_re, spec_re, preferred_element_type=jnp.float32
    ) + jnp.einsum("ksb,stk->btk", half_im, spec_im, preferred_element_type=jnp.float32)
    beam_im = jnp.einsum(
        "ksb,stk->btk", half_re, spec_im, preferred_element_type=jnp.float32
    ) - jnp.einsum("ksb,stk->btk", half_im, spec_re, preferred_element_type=jnp.float32)
    factor = 1.0 / math.sqrt(stations)
    beam_local = (jnp.stack([beam_re, beam_im]) * factor).astype(jnp.bfloat16)
    owned = lax.all_to_all(beam_local, "st", split_axis=1, concat_axis=3, tiled=True)
    return owned[:, :, None]


def solution(mesh):
    return jax.shard_map(
        local,
        mesh=mesh,
        in_specs=(P(None, "blk", "st", None), P(), P("st"), P("blk", "st"), P()),
        out_specs=P(None, "st", "blk", None, None),
        check_vma=False,
    )
```

profile of v0, /device:TPU:0, one launch (start us, length us, event | category | flops | bytes accessed | tf_op | source)
XLA Modules:
  0.0 1414.6 jit_solution(12180792529698045729)
XLA Ops:
  6.5 14.9 %reshape.61 = f32[2,64,267,128]{3,2,1,0:T(8,128)} reshape(bf16[2,1,64,34176]{3,2,1,0:T(8,128)(2,1)} %param.5) | data formatting | bytes 26247168 | tf_op jit(solution)/shard_map/convert_element_type | solution.py:25
  21.5 71.6 %fusion.4 = bf16[2,64,256,128]{3,2,1,0:T(8,128)(2,1)} fusion(f32[2,64,267,128]{3,2,1,0:T(8,128)} %reshape.61, f32[64]{0:T(128)S(1)} %bitcast_multiply_fusion, f32[128]{0:T(128)S(1)} %get-tuple-element.21, f32[128]{0:T(128)S(1)} %get-tuple-element.22, f32[128]{0:T(128)S(1)} %get-tuple-element.12, f32[128]{0:T(128)S(1)} %get-tuple-element.13, ...), kind=kLoop, calls=%fused_computation.8 | loop fusion | flops 104857600 | bytes 209721600 | tf_op jit(solution)/shard_map/convert_element_type | solution.py:33
  93.1 3.9 fusion.110
  97.0 1.5 fusion.56
  98.5 0.4 copy-done.4
  98.9 4.8 fusion.57
  103.7 3.4 fusion.1
  107.1 6.8 copy.28
  113.9 8.1 fusion
  122.0 6.8 copy.27
  128.8 7.5 pad_maximum_fusion
  136.3 190.7 %all_to_all.30 = bf16[2,64,256,128]{2,1,0,3:T(8,128)(2,1)} all-to-all(bf16[2,64,256,128]{2,1,0,3:T(8,128)(2,1)} %pad_maximum_fusion), channel_id=1, replica_groups=mesh['blk'=4,'st'=8] {'st'}, dimensions={3} | all-to-all | bytes 16777216 | tf_op jit(solution)/shard_map/all_to_all | solution.py:76
  327.0 11.4 copy.29
  338.5 4.0 fusion.109
  342.5 2.4 copy.31
  344.9 2.4 copy.30
  347.3 8.1 fusion.111
  355.5 8.1 fusion.112
  363.6 27.7 %convolution_subtract_fusion.1 = f32[16,512,512]{2,1,0:T(8,128)} fusion(f32[16,512,512]{2,1,0:T(8,128)} %fusion.112, bf16[512,256,16]{1,0,2:T(8,128)(2,1)} %bitcast.84, bf16[512,256,16]{1,0,2:T(8,128)(2,1)} %bitcast.78), kind=kOutput, calls=%fused_computation.38 | convolution fusion | flops 2151677952 | bytes 41943040 | tf_op jit(solution)/shard_map/stk,utk->ksu/dot_general | solution.py:87
  391.3 16.4 %convolution_add_fusion.1 = f32[16,512,512]{2,1,0:T(8,128)} fusion(f32[16,512,512]{2,1,0:T(8,128)} %fusion.111, bf16[512,256,16]{1,0,2:T(8,128)(2,1)} %bitcast.79), kind=kOutput, calls=%fused_computation.39 | convolution fusion | flops 2151677952 | bytes 37748736 | tf_op jit(solution)/shard_map/stk,utk->ksu/dot_general | solution.py:84
  407.7 0.0 all-reduce.3.cloned.1.call-update
  407.7 558.2 %all-reduce.3.cloned.1.call-done = (f32[16,512,512]{2,1,0:T(8,128)}, f32[16,512,512]{2,1,0:T(8,128)}) async-done(((f32[16,512,512]{2,1,0:T(8,128)}, f32[16,512,512]{2,1,0:T(8,128)}), (f32[16,512,512]{2,1,0:T(8,128)}, f32[16,512,512]{2,1,0:T(8,128)})) %all-reduce.3.cloned.1.call-update) | async-done | bytes 33554448 | tf_op jit(solution)/shard_map/psum | solution.py:89
  966.0 11.7 broadcast_multiply_fusion
  977.7 62.3 %copy.32 = f32[16,512,512]{0,2,1:T(8,128)} copy(f32[16,512,512]{2,1,0:T(8,128)} %broadcast_multiply_fusion) | data formatting | bytes 33554432 | tf_op jit(solution)/shard_map/div | solution.py:90
  1040.1 5.5 gather_fusion
  1045.6 0.1 reduce_sum.9
  1045.7 0.1 copy.33
  1045.8 15.7 %fusion.145 = f32[16,512,128]{2,1,0:T(8,128)S(1)} fusion(f32[16,512]{1,0:T(8,128)S(1)} %copy.33, s32[16]{0:T(128)S(1)} %add_add_fusion, s32[512,128]{1,0:T(8,128)S(1)} %copy-done.10), kind=kLoop, calls=%fused_computation.61.clone.2 | loop fusion | flops 15728640 | bytes 4489280 | tf_op jit(solution)/shard_map/ksu,kub->ksb/dot_general | solution.py:50
  1061.6 0.0 copy-start.11
  1061.6 34.4 %fusion.49 = f32[16,512,128]{2,1,0:T(8,128)S(1)} fusion(f32[16,512]{1,0:T(8,128)S(1)} %copy.33, s32[16]{0:T(128)S(1)} %add_add_fusion, s32[512,128]{1,0:T(8,128)} %param.9, f32[16,512,512]{2,1,0:T(8,128)} %get-tuple-element.6), kind=kOutput, calls=%fused_computation.75 | convolution fusion | flops 6462373888 | bytes 21266496 | tf_op jit(solution)/shard_map/ksu,kub->ksb/dot_general | solution.py:50
  1096.1 32.0 %fusion.21 = f32[16,512,128]{2,1,0:T(8,128)S(1)} fusion(f32[16,512,512]{2,1,0:T(8,128)S(1)} %bitcast.98, f32[16,512]{1,0:T(8,128)S(1)} %copy.33, s32[16]{0:T(128)S(1)} %add_add_fusion, s32[512,128]{1,0:T(8,128)S(1)} %copy-done.11), kind=kOutput, calls=%fused_computation.36 | convolution fusion | flops 6462373888 | bytes 21266496 | tf_op jit(solution)/shard_map/ksu,kub->ksb/dot_general | solution.py:50
  1128.2 32.6 %fusion.19 = f32[16,512,128]{2,1,0:T(8,128)} fusion(f32[16,512,512]{2,1,0:T(8,128)S(1)} %bitcast.98, f32[16,512]{1,0:T(8,128)S(1)} %copy.33, s32[16]{0:T(128)S(1)} %add_add_fusion, s32[512,128]{1,0:T(8,128)S(1)} %copy-done.11), kind=kOutput, calls=%fused_computation.34 | convolution fusion | flops 6462373888 | bytes 21266496 | tf_op jit(solution)/shard_map/ksu,kub->ksb/dot_general | solution.py:50
  1160.8 31.2 %divide_add_fusion.1 = f32[16,512,128]{2,1,0:T(8,128)} fusion(f32[16,512,128]{2,1,0:T(8,128)S(1)} %fusion.21, f32[16]{0:T(128)S(1)} %multiply_add_fusion, f32[16,512]{1,0:T(8,128)S(1)} %copy.33, s32[16]{0:T(128)S(1)} %add_add_fusion, s32[512,128]{1,0:T(8,128)S(1)} %copy-done.11, f32[16,512,512]{2,1,0:T(8,128)S(1)} %bitcast.88, f32[16,512,128]{2,1,0:T(8,128)S(1)} %fusion.145), kind=kOutput, calls=%fused_computation.59 | convolution fusion | flops 6469713920 | bytes 29655168 | tf_op jit(solution)/shard_map/ksu,kub->ksb/dot_general | solution.py:50
  1192.0 18.1 %fusion.108 = f32[16,512,128]{2,1,0:T(8,128)} fusion(f32[16,512,128]{2,1,0:T(8,128)} %divide_add_fusion.1, f32[16,512,512]{2,1,0:T(8,128)S(1)} %bitcast.88), kind=kOutput, calls=%fused_computation.156 | convolution fusion | flops 6446645248 | bytes 25165824 | tf_op jit(solution)/shard_map/ksu,kub->ksb/dot_general | solution.py:50
  1210.1 20.6 %fusion.15 = f32[16,512,128]{2,1,0:T(8,128)} fusion(f32[16,512,128]{2,1,0:T(8,128)} %divide_add_fusion.1, f32[16,512,512]{2,1,0:T(8,128)} %get-tuple-element.5), kind=kOutput, calls=%fused_computation.30 | convolution fusion | flops 6446645248 | bytes 25165824 | tf_op jit(solution)/shard_map/ksu,kub->ksb/dot_general | solution.py:50
  1230.7 19.3 %divide_add_fusion.13 = f32[16,512,128]{2,1,0:T(8,128)} fusion(f32[16,512,128]{2,1,0:T(8,128)S(1)} %fusion.49, f32[16,512,128]{2,1,0:T(8,128)} %fusion.19, f32[16]{0:T(128)S(1)} %multiply_add_fusion, f32[16,512]{1,0:T(8,128)S(1)} %copy.33, s32[16]{0:T(128)S(1)} %add_add_fusion, s32[512,128]{1,0:T(8,128)} %param.9), kind=kLoop, calls=%fused_computation.58.clone.2.clone.clone.clone.2 | loop fusion | flops 23068672 | bytes 12877952 | tf_op jit(solution)/shard_map/ksu,kub->ksb/dot_general | solution.py:50
  1250.0 18.0 %divide_add_fusion.12 = f32[16,512,128]{2,1,0:T(8,128)} fusion(f32[16,512,128]{2,1,0:T(8,128)S(1)} %fusion.49, f32[16,512,128]{2,1,0:T(8,128)S(1)} %copy-done.5, f32[16]{0:T(128)S(1)} %multiply_add_fusion, f32[16,512]{1,0:T(8,128)S(1)} %copy.33, s32[16]{0:T(128)S(1)} %add_add_fusion, s32[512,128]{1,0:T(8,128)S(1)} %copy-done.12), kind=kLoop, calls=%fused_computation.58.clone.1.clone.2 | loop fusion | flops 23068672 | bytes 12877952 | tf_op jit(solution)/shard_map/ksu,kub->ksb/dot_general | solution.py:50
  1268.0 33.9 %add_convert_fusion.1 = bf16[16,512,128]{2,1,0:T(8,128)(2,1)} fusion(f32[16,512,128]{2,1,0:T(8,128)S(1)} %copy-done.6, f32[16,512,128]{2,1,0:T(8,128)} %fusion.108, f32[16,512,512]{2,1,0:T(8,128)} %get-tuple-element.5, f32[16]{0:T(128)S(1)} %multiply_add_fusion, f32[16,512]{1,0:T(8,128)S(1)} %copy.33, s32[16]{0:T(128)S(1)} %add_add_fusion, ...), kind=kOutput, calls=%fused_computation.57 | convolution fusion | flops 6469713920 | bytes 31752320 | tf_op jit(solution)/shard_map/ksu,kub->ksb/dot_general | solution.py:50
  1301.9 4.5 fusion.114
  1306.4 2.7 fusion.113
  1309.1 33.4 %add_convert_fusion = bf16[16,512,128]{2,1,0:T(8,128)(2,1)} fusion(f32[16,512,128]{2,1,0:T(8,128)} %fusion.15, f32[16,512,128]{2,1,0:T(8,128)S(1)} %fusion.49, f32[16,512,128]{2,1,0:T(8,128)} %fusion.19, f32[16]{0:T(128)S(1)} %multiply_add_fusion, f32[16,512]{1,0:T(8,128)S(1)} %copy.33, s32[16]{0:T(128)S(1)} %add_add_fusion, s32[512,128]{1,0:T(8,128)S(1)} %copy-done.12, ...), kind=kOutput, calls=%fused_computation.56 | convolution fusion | flops 6478102528 | bytes 35946624 | tf_op jit(solution)/shard_map/ksu,kub->ksb/dot_general | solution.py:50
  1342.5 3.8 subtract_bitcast_fusion
  1346.3 1.4 add_bitcast_fusion
  1347.7 0.6 fusion.30
  1348.3 2.9 copy.38
  1351.2 53.7 %all_to_all.31 = bf16[2,128,256,16]{2,3,0,1:T(8,128)(2,1)S(1)} all-to-all(bf16[2,128,256,16]{2,3,0,1:T(8,128)(2,1)} %copy.38), channel_id=1, replica_groups=mesh['blk'=4,'st'=8] {'st'}, dimensions={1} | all-to-all | bytes 4194304 | tf_op jit(solution)/shard_map/all_to_all | solution.py:113
  1404.8 0.3 copy.40
  1405.1 2.4 copy.41
  (55 shorter events, 0.2 us)
Async XLA Ops:
  6.5 14.9 %copy-start.13 = (f32[12,128]{1,0:T(8,128)S(1)}, f32[12,128]{1,0:T(8,128)}, u32[]{:S(2)}) copy-start(f32[12,128]{1,0:T(8,128)} %param.6) | copy-start | bytes 18436
  6.5 14.9 %copy-start.14 = (f32[64]{0:T(128)S(1)}, f32[64]{0:T(128)}, u32[]{:S(2)}) copy-start(f32[64]{0:T(128)} %param.7) | copy-start | bytes 772
  6.5 14.9 %copy-start.15 = (s32[1,64]{1,0:T(1,128)S(1)}, s32[1,64]{1,0:T(1,128)}, u32[]{:S(2)}) copy-start(s32[1,64]{1,0:T(1,128)} %param.8) | copy-start | bytes 772
  6.5 959.4 %all-reduce.3.cloned.1.call-start = ((), (), s32[]{:S(2)}) async-start(), calls=%async_computation.2 | async-start | bytes 67108864 | tf_op jit(solution)/shard_map/psum | solution.py:89
  97.0 1.9 copy-start.4
  344.9 10.6 copy-start
  347.3 8.1 copy-start.2
  977.7 68.1 %copy-start.10 = (s32[512,128]{1,0:T(8,128)S(1)}, s32[512,128]{1,0:T(8,128)}, u32[]{:S(2)}) copy-start(s32[512,128]{1,0:T(8,128)} %param.9) | copy-start | bytes 786436
  1045.8 50.2 %slice-start.4 = ((s8[16777216]{0:T(1024)(128)(4,1)}), s8[4194304]{0:T(1024)(128)(4,1)S(1)}, s32[]{:S(2)}) async-start(s8[16777216]{0:T(1024)(128)(4,1)} %bitcast.97), calls=%async_computation.7 | async-start | bytes 8388608
  1061.5 34.5 %slice-start.5 = ((s8[16777216]{0:T(1024)(128)(4,1)}), s8[4194304]{0:T(1024)(128)(4,1)S(1)}, s32[]{:S(2)}) async-start(s8[16777216]{0:T(1024)(128)(4,1)} %bitcast.97), calls=%async_computation.8 | async-start | bytes 8388608
  1061.6 34.5 %slice-start.6 = ((s8[16777216]{0:T(1024)(128)(4,1)}), s8[4194304]{0:T(1024)(128)(4,1)S(1)}, s32[]{:S(2)}) async-start(s8[16777216]{0:T(1024)(128)(4,1)} %bitcast.97), calls=%async_computation.9 | async-start | bytes 8388608
  1061.6 34.5 %slice-start.7 = ((s8[16777216]{0:T(1024)(128)(4,1)}), s8[4194304]{0:T(1024)(128)(4,1)S(1)}, s32[]{:S(2)}) async-start(s8[16777216]{0:T(1024)(128)(4,1)} %bitcast.97), calls=%async_computation.10 | async-start | bytes 8388608
  1061.6 34.5 %copy-start.11 = (s32[512,128]{1,0:T(8,128)S(1)}, s32[512,128]{1,0:T(8,128)}, u32[]{:S(2)}) copy-start(s32[512,128]{1,0:T(8,128)} %param.9) | copy-start | bytes 786436
  1096.1 64.7 %slice-start = ((s8[16777216]{0:T(1024)(128)(4,1)}), s8[4194304]{0:T(1024)(128)(4,1)S(1)}, s32[]{:S(2)}) async-start(s8[16777216]{0:T(1024)(128)(4,1)} %bitcast.87), calls=%async_computation.3 | async-start | bytes 8388608
  1096.1 64.7 %slice-start.1 = ((s8[16777216]{0:T(1024)(128)(4,1)}), s8[4194304]{0:T(1024)(128)(4,1)S(1)}, s32[]{:S(2)}) async-start(s8[16777216]{0:T(1024)(128)(4,1)} %bitcast.87), calls=%async_computation.4 | async-start | bytes 8388608
  1128.1 32.7 %slice-start.2 = ((s8[16777216]{0:T(1024)(128)(4,1)}), s8[4194304]{0:T(1024)(128)(4,1)S(1)}, s32[]{:S(2)}) async-start(s8[16777216]{0:T(1024)(128)(4,1)} %bitcast.87), calls=%async_computation.5 | async-start | bytes 8388608
  1128.1 32.6 %slice-start.3 = ((s8[16777216]{0:T(1024)(128)(4,1)}), s8[4194304]{0:T(1024)(128)(4,1)S(1)}, s32[]{:S(2)}) async-start(s8[16777216]{0:T(1024)(128)(4,1)} %bitcast.87), calls=%async_computation.6 | async-start | bytes 8388608
  1230.7 19.3 %copy-start.5 = (f32[16,512,128]{2,1,0:T(8,128)S(1)}, f32[16,512,128]{2,1,0:T(8,128)}, u32[]{:S(2)}) copy-start(f32[16,512,128]{2,1,0:T(8,128)} %fusion.19) | copy-start | bytes 12582916
  1230.7 19.3 %copy-start.12 = (s32[512,128]{1,0:T(8,128)S(1)}, s32[512,128]{1,0:T(8,128)}, u32[]{:S(2)}) copy-start(s32[512,128]{1,0:T(8,128)} %param.9) | copy-start | bytes 786436
  1250.0 18.0 %copy-start.6 = (f32[16,512,128]{2,1,0:T(8,128)S(1)}, f32[16,512,128]{2,1,0:T(8,128)}, u32[]{:S(2)}) copy-start(f32[16,512,128]{2,1,0:T(8,128)} %divide_add_fusion.1) | copy-start | bytes 12582916
  1268.0 33.9 %copy-start.1 = (bf16[1,8,64,256,16]{3,2,1,4,0:T(8,128)(2,1)S(1)}, bf16[1,8,64,256,16]{3,2,1,4,0:T(8,128)(2,1)}, u32[]{:S(2)}) copy-start(bf16[1,8,64,256,16]{3,2,1,4,0:T(8,128)(2,1)} %copy-done) | copy-start | bytes 12582916
  1301.9 4.5 copy-start.3
  1301.9 4.5 copy-start.9
  1342.5 3.8 copy-start.7
  1342.5 3.8 copy-start.8
Sparse Core Ops, SparseCore 0:
  407.8 558.0 all-reduce.2
where the time goes:
time: 1420 us; the launch traced here: 1410 us
  waiting for transfers between devices  558 us (39%)
  matrix products  327 us (23%)
  blocking collectives  244 us (17%)
  other arithmetic  145 us (10%)
  local copies, waits for them, and re-layouts  127 us (9%)
    psum x1, waiting for transfers between devices, local(): total_re, total_im = lax.psum((cov_re, cov_im), 'blk')  558 us
    dot_general x8, matrix products, batched(): jnp.einsum('ksu,kub->ksb', matrix, vectors, precision=lax.Precision.HIGHEST)  236 us
    all_to_all x1, blocking collectives, local(): lax.all_to_all(local_spec, 'st', split_axis=3, concat_axis=1, tiled=True)  191 us
    convert_element_type x1, other arithmetic, polyphase(): return (filtered * row_gain[None, :, None, None]).astype(jnp.bfloat16)  71.6 us
    div x1, local copies, waits for them, and re-layouts, local(): rows_re = total_re / counted  62.3 us
    all_to_all x1, blocking collectives, local(): lax.all_to_all(beam_local, 'st', split_axis=1, concat_axis=3, tiled=True)  53.7 us
    dot_general x3, other arithmetic, batched(): jnp.einsum('ksu,kub->ksb', matrix, vectors, precision=lax.Precision.HIGHEST)  53 us
  transfers between devices with their start and end apart: 1, of which 1 were waited for; matrix products, arithmetic and copies ran while one was open for 0% of the time, Pallas kernels for 0%

commit v1 on v0

--- a/solution.py
+++ b/solution.py
@@ -6,6 +6,7 @@
 from jax.sharding import PartitionSpec as P
 
 PHASES = 4096
+AXES = ("blk", "st")
 
 
 def dft_tables(width):
@@ -34,6 +35,81 @@
 
 
 def transform(filtered, cos_table, sin_table):
+    flat_re = filtered[0]
+    flat_im = filtered[1]
+    dot = lambda a, b: jnp.einsum("stc,ck->stk", a, b, preferred_element_type=jnp.float32)
+    out_re = dot(flat_re, cos_table) + dot(flat_im, sin_table)
+    out_im = dot(flat_im, cos_table) - dot(flat_re, sin_table)
+    return jnp.stack([out_re, out_im]).astype(jnp.bfloat16)
+
+
+def batched(matrix, vectors):
+    return jnp.einsum("ksu,kub->ksb", matrix, vectors, precision=lax.Precision.HIGHEST)
+
+
+def iterate(rows_re, rows_im, steer_re, steer_im, diag_total, load):
+    weight_re = steer_re / diag_total
+    weight_im = steer_im / diag_total
+    for sweep_no in range(2):
+        prod_re = batched(rows_re, weight_re) - batched(rows_im, weight_im)
+        prod_im = batched(rows_re, weight_im) + batched(rows_im, weight_re)
+        next_re = weight_re + 0.5 * (steer_re - prod_re - load * weight_re) / diag_total
+        next_im = weight_im + 0.5 * (steer_im - prod_im - load * weight_im) / diag_total
+        weight_re, weight_im = (next_re, next_im)
+    return weight_re, weight_im
+
+
+def local(voltages, filter_coeffs, station_gain, flags, steer_index):
+    nblk = lax.axis_size("blk")
+    nst = lax.axis_size("st")
+    ndev = nblk * nst
+    cos_table, sin_table = dft_tables(filter_coeffs.shape[1])
+    row_gain = station_gain * flags[0].astype(jnp.float32)
+    filtered = polyphase(voltages[:, 0], filter_coeffs, row_gain)
+    local_spec = transform(filtered, cos_table, sin_table)
+    _, ls, nt, nk = local_spec.shape
+    kc = nk // ndev
+    send = local_spec.reshape(2, ls, nt, ndev, kc).transpose(3, 4, 0, 1, 2)
+    recv = lax.all_to_all(send, AXES, split_axis=0, concat_axis=0, tiled=True)
+    recv = recv.reshape(nblk, nst, kc, 2, ls, nt)
+    spec = recv.transpose(2, 3, 1, 4, 0, 5).reshape(kc, 2, nst * ls, nblk * nt)
+    stations = nst * ls
+    counted = nblk * nt
+    spec_re = spec[:, 0]
+    spec_im = spec[:, 1]
+    cdot = lambda a, b: jnp.einsum("kst,kut->ksu", a, b, preferred_element_type=jnp.float32)
+    cov_re = cdot(spec_re, spec_re) + cdot(spec_im, spec_im)
+    cov_im = cdot(spec_im, spec_re) - cdot(spec_re, spec_im)
+    me = lax.axis_index("blk") * nst + lax.axis_index("st")
+    channel_ids = me * kc + jnp.arange(kc, dtype=jnp.int32)
+    rows_re = cov_re / counted
+    rows_im = cov_im / counted
+    diag_part = jnp.diagonal(rows_re, axis1=1, axis2=2)
+    load = jnp.sum(diag_part, axis=1) / stations + 1e-05
+    phase_int = steer_index[None, :, :] * (channel_ids + 1)[:, None, None] % PHASES
+    angle = phase_int.astype(jnp.float32) * (2.0 * math.pi / PHASES)
+    steer_re = jnp.cos(angle)
+    steer_im = jnp.sin(angle)
+    load_full = load[:, None, None]
+    diag_total = (diag_part + load[:, None])[:, :, None]
+    weight_re, weight_im = iterate(rows_re, rows_im, steer_re, steer_im, diag_total, load_full)
+    half_re = weight_re.astype(jnp.bfloat16)
+    half_im = weight_im.astype(jnp.bfloat16)
+    bdot = lambda a, b: jnp.einsum("ksb,kst->kbt", a, b, preferred_element_type=jnp.float32)
+    beam_re = bdot(half_re, spec_re) + bdot(half_im, spec_im)
+    beam_im = bdot(half_re, spec_im) - bdot(half_im, spec_re)
+    factor = 1.0 / math.sqrt(stations)
+    beam = (jnp.stack([beam_re, beam_im]) * factor).astype(jnp.bfloat16)
+    nb = beam.shape[2]
+    bc = nb // nst
+    out = beam.reshape(2, kc, nst, bc, nblk, nt).transpose(4, 2, 0, 3, 5, 1)
+    out = out.reshape(ndev, 2, bc, nt, kc)
+    got = lax.all_to_all(out, AXES, split_axis=0, concat_axis=0, tiled=True)
+    got = got.transpose(1, 2, 3, 0, 4).reshape(2, bc, nt, ndev * kc)
+    return got[:, :, None]
+
+
+def fb_transform(filtered, cos_table, sin_table):
     width = cos_table.shape[0]
     flat_re = filtered[0].reshape(-1, width)
     flat_im = filtered[1].reshape(-1, width)
@@ -46,17 +122,17 @@
     return jnp.stack([out_re, out_im]).astype(jnp.bfloat16).reshape(filtered.shape)
 
 
-def batched(matrix, vectors):
+def fb_batched(matrix, vectors):
     return jnp.einsum("ksu,kub->ksb", matrix, vectors, precision=lax.Precision.HIGHEST)
 
 
-def iterate(rows_re, rows_im, steer_re, steer_im, diag_total, load, collect, combine):
+def fb_iterate(rows_re, rows_im, steer_re, steer_im, diag_total, load, collect, combine):
     weight_re = steer_re / diag_total
     weight_im = steer_im / diag_total
     for sweep_no in range(2):
         full_re, full_im = collect(weight_re, weight_im)
-        prod_re = batched(rows_re, full_re) - batched(rows_im, full_im)
-        prod_im = batched(rows_re, full_im) + batched(rows_im, full_re)
+        prod_re = fb_batched(rows_re, full_re) - fb_batched(rows_im, full_im)
+        prod_im = fb_batched(rows_re, full_im) + fb_batched(rows_im, full_re)
         prod_re, prod_im = combine(prod_re, prod_im)
         next_re = weight_re + 0.5 * (steer_re - prod_re - load * weight_re) / diag_total
         next_im = weight_im + 0.5 * (steer_im - prod_im - load * weight_im) / diag_total
@@ -68,11 +144,11 @@
     return (part_re, part_im)
 
 
-def local(voltages, filter_coeffs, station_gain, flags, steer_index):
+def fb_local(voltages, filter_coeffs, station_gain, flags, steer_index):
     cos_table, sin_table = dft_tables(filter_coeffs.shape[1])
     row_gain = station_gain * flags[0].astype(jnp.float32)
     filtered = polyphase(voltages[:, 0], filter_coeffs, row_gain)
-    local_spec = transform(filtered, cos_table, sin_table)
+    local_spec = fb_transform(filtered, cos_table, sin_table)
     spectra = lax.all_to_all(local_spec, "st", split_axis=3, concat_axis=1, tiled=True)
     stations = spectra.shape[1]
     chans = spectra.shape[3]
@@ -97,7 +173,7 @@
     steer_im = jnp.sin(angle)
     load_full = load[:, None, None]
     diag_total = (diag_part + load[:, None])[:, :, None]
-    weight_re, weight_im = iterate(
+    weight_re, weight_im = fb_iterate(
         rows_re, rows_im, steer_re, steer_im, diag_total, load_full, unchanged, unchanged
     )
     half_re = weight_re.astype(jnp.bfloat16)
@@ -114,9 +190,15 @@
     return owned[:, :, None]
 
 
+def body(voltages, filter_coeffs, station_gain, flags, steer_index):
+    ndev = lax.axis_size("blk") * lax.axis_size("st")
+    plan = local if filter_coeffs.shape[1] % ndev == 0 else fb_local
+    return plan(voltages, filter_coeffs, station_gain, flags, steer_index)
+
+
 def solution(mesh):
     return jax.shard_map(
-        local,
+        body,
         mesh=mesh,
         in_specs=(P(None, "blk", "st", None), P(), P("st"), P("blk", "st"), P()),
         out_specs=P(None, "st", "blk", None, None),

time: 1420 us -> 589 us (0.41)
  waiting for transfers between devices: 558 us -> 189 us
  matrix products: 327 us -> 112 us
  blocking collectives: 244 us -> 51.8 us
  other arithmetic: 145 us -> 80.1 us
    psum x1 -> x0, waiting for transfers between devices: 558 us -> none  [local(): total_re, total_im = lax.psum((cov_re, cov_im), 'blk')]
    all_to_all x2 -> x1, blocking collectives: 244 us -> 51.8 us  [local(): got = lax.all_to_all(out, AXES, split_axis=0, concat_axis=0, tiled=True)]
    all_to_all x0 -> x1, waiting for transfers between devices: none -> 189 us  [local(): recv = lax.all_to_all(send, AXES, split_axis=0, concat_axis=0, tiled=True)]
    dot_general x8, matrix products: 236 us -> 65.3 us  [batched(): jnp.einsum('ksu,kub->ksb', matrix, vectors, precision=lax.Precision.HIGHEST)]
    dot_general x3 -> x0, other arithmetic: 53 us -> none  [batched(): jnp.einsum('ksu,kub->ksb', matrix, vectors, precision=lax.Precision.HIGHEST)]
    dot_general x12, matrix products: 90.5 us -> 46.9 us  [the longest x4 19.9 us: transform(): jnp.einsum('stc,ck->stk', a, b, preferred_element_type=jnp.float32)]
    reshape x0 -> x2, local copies, waits for them, and re-layouts: none -> 26.5 us  [the longest x1 14.3 us: local(): spec = recv.transpose(2, 3, 1, 4, 0, 5).reshape(kc, 2, nst * ls, nblk * nt)]
    another operation x2 -> x7, local copies, waits for them, and re-layouts: 13.6 us -> 28.6 us  [the longest x2 13.8 us: transform(): return jnp.stack([out_re, out_im]).astype(jnp.bfloat16)]
where the time goes in v1:
time: 589 us; the launch traced here: 579 us
  waiting for transfers between devices  189 us (32%)
  local copies, waits for them, and re-layouts  138 us (23%)
  matrix products  112 us (19%)
  other arithmetic  80.1 us (14%)
  blocking collectives  51.8 us (9%)
  starting transfers between devices  7.65 us (1%)
    all_to_all x1, waiting for transfers between devices, local(): recv = lax.all_to_all(send, AXES, split_axis=0, concat_axis=0, tiled=True)  189 us
    convert_element_type x1, other arithmetic, polyphase(): return (filtered * row_gain[None, :, None, None]).astype(jnp.bfloat16)  70.9 us
    dot_general x8, matrix products, batched(): jnp.einsum('ksu,kub->ksb', matrix, vectors, precision=lax.Precision.HIGHEST)  65.3 us
    div x1, local copies, waits for them, and re-layouts, local(): rows_re = cov_re / counted  60.2 us
    all_to_all x1, blocking collectives, local(): got = lax.all_to_all(out, AXES, split_axis=0, concat_axis=0, tiled=True)  51.8 us
    dot_general x4, matrix products, transform(): jnp.einsum('stc,ck->stk', a, b, preferred_element_type=jnp.float32)  19.9 us
    dot_general x4, matrix products, local(): jnp.einsum('kst,kut->ksu', a, b, preferred_element_type=jnp.float32)  18.9 us
    convert_element_type x1, local copies, waits for them, and re-layouts, polyphase(): grid = samples.astype(jnp.float32).reshape(2, samples.shape[1], -1, width)  14.9 us
  transfers between devices with their start and end apart: 1, of which 1 were waited for; matrix products, arithmetic and copies ran while one was open for 0% of the time, Pallas kernels for 0%

profile of v1, /device:TPU:0, one launch (start us, length us, event | category | flops | bytes accessed | tf_op | source)
XLA Modules:
  0.0 579.5 jit_solution(16330924746540539322)
XLA Ops:
  0.0 1.0 slice_bitcast_fusion.43
  1.0 0.0 copy-start.5
  1.0 0.0 copy-start.6
  1.0 14.9 %reshape.73 = f32[2,64,267,128]{3,2,1,0:T(8,128)} reshape(bf16[2,1,64,34176]{3,2,1,0:T(8,128)(2,1)} %param.5) | data formatting | bytes 26247168 | tf_op jit(solution)/shard_map/convert_element_type | solution.py:26
  15.9 0.0 copy-done.5
  15.9 70.9 %fusion.2 = bf16[2,64,256,128]{3,2,1,0:T(8,128)(2,1)} fusion(f32[2,64,267,128]{3,2,1,0:T(8,128)} %reshape.73, f32[64]{0:T(128)S(1)} %bitcast_multiply_fusion, f32[128]{0:T(128)S(1)} %get-tuple-element.15, f32[128]{0:T(128)S(1)} %get-tuple-element.16, f32[128]{0:T(128)S(1)} %get-tuple-element.6, f32[128]{0:T(128)S(1)} %get-tuple-element.7, ...), kind=kLoop, calls=%fused_computation.4 | loop fusion | flops 104857600 | bytes 209721600 | tf_op jit(solution)/shard_map/convert_element_type | solution.py:34
  86.8 3.8 fusion.15
  90.6 0.8 copy-done
  91.5 4.7 fusion.14
  96.2 3.4 add_convert_fusion
  99.6 6.9 %stack.18 = bf16[1,64,256,32,4]{2,4,3,1,0:T(4,128)(2,1)} reshape(bf16[64,256,128]{1,2,0:T(8,128)(2,1)} %add_convert_fusion) | data formatting | bytes 8388608 | tf_op jit(solution)/shard_map/stack | solution.py:43
  106.5 8.1 %subtract_convert_fusion = bf16[64,256,128]{1,2,0:T(8,128)(2,1)} fusion(f32[64,256,128]{1,2,0:T(8,128)} %fusion.14, bf16[2,64,256,128]{3,2,1,0:T(8,128)(2,1)} %fusion.2), kind=kOutput, calls=%fused_computation.29 | convolution fusion | flops 541327360 | bytes 16777216 | tf_op jit(solution)/shard_map/stc,ck->stk/dot_general | solution.py:40
  114.5 6.9 %stack.19 = bf16[1,64,256,32,4]{2,4,3,1,0:T(4,128)(2,1)} reshape(bf16[64,256,128]{1,2,0:T(8,128)(2,1)} %subtract_convert_fusion) | data formatting | bytes 8388608 | tf_op jit(solution)/shard_map/stack | solution.py:43
  121.4 8.4 %copy_bitcast_fusion = bf16[32,4,2,64,256]{4,1,3,2,0:T(4,128)(2,1)} fusion(bf16[1,64,256,32,4]{2,4,3,1,0:T(4,128)(2,1)} %stack.19, bf16[1,64,256,32,4]{2,4,3,1,0:T(4,128)(2,1)} %stack.18), kind=kLoop, calls=%fused_computation.27 | loop fusion | flops 4194304 | bytes 16777216 | tf_op jit(solution)/shard_map/transpose | solution.py:72
  129.8 7.6 %all-to-all-start = ((bf16[32,4,2,64,256]{4,1,3,2,0:T(4,128)(2,1)}), bf16[32,4,2,64,256]{4,1,3,2,0:T(4,128)(2,1)}, u32[]{:S(2)}, u32[]{:S(2)}) async-start(bf16[32,4,2,64,256]{4,1,3,2,0:T(4,128)(2,1)} %copy_bitcast_fusion), calls=%async_computation | async-start | bytes 16777216 | tf_op jit(solution)/shard_map/all_to_all | solution.py:73
  137.5 189.2 %all-to-all-done = bf16[32,4,2,64,256]{4,1,3,2,0:T(4,128)(2,1)} async-done(((bf16[32,4,2,64,256]{4,1,3,2,0:T(4,128)(2,1)}), bf16[32,4,2,64,256]{4,1,3,2,0:T(4,128)(2,1)}, u32[]{:S(2)}, u32[]{:S(2)}) %all-to-all-start) | async-done | bytes 8388640 | tf_op jit(solution)/shard_map/all_to_all | solution.py:73
  326.7 12.2 %copy.44 = bf16[4,8,4,2,64,256]{5,0,4,1,2,3:T(4,128)(2,1)} copy(bf16[4,8,4,2,64,256]{5,2,4,3,1,0:T(4,128)(2,1)} %bitcast.18) | data formatting | bytes 16777216 | tf_op jit(solution)/shard_map/reshape | solution.py:74
  338.9 14.3 %reshape.71 = bf16[4,2,512,1024]{3,2,0,1:T(8,128)(2,1)} reshape(bf16[4,2,8,64,4,256]{5,4,3,2,0,1:T(4,128)(2,1)} %bitcast.111) | data formatting | bytes 16777216 | tf_op jit(solution)/shard_map/reshape | solution.py:75
  353.2 6.0 %fusion.22 = f32[4,512,512]{2,1,0:T(8,128)S(1)} fusion(bf16[4,2,512,1024]{3,2,0,1:T(8,128)(2,1)} %reshape.71), kind=kOutput, calls=%fused_computation.47 | convolution fusion | flops 2147483648 | bytes 8388608 | tf_op jit(solution)/shard_map/kst,kut->ksu/dot_general | solution.py:80
  359.2 4.3 fusion.20
  363.5 4.3 add_multiply_fusion
  367.8 60.2 %copy.27 = f32[4,512,512]{0,2,1:T(8,128)} copy(f32[4,512,512]{2,1,0:T(8,128)} %add_multiply_fusion) | data formatting | bytes 8388608 | tf_op jit(solution)/shard_map/div | solution.py:85
  428.0 5.5 gather_fusion
  433.5 0.1 reduce_sum.9
  433.7 0.1 copy.28
  433.8 9.9 %fusion.55 = f32[4,512,128]{2,1,0:T(8,128)S(1)} fusion(f32[4,512,512]{2,1,0:T(8,128)} %add_multiply_fusion, f32[4,512]{1,0:T(4,128)S(1)} %copy.28, s32[4]{0:T(128)S(1)} %add_add_fusion, s32[512,128]{1,0:T(8,128)S(1)} %copy-done.4), kind=kOutput, calls=%fused_computation.91 | convolution fusion | flops 1614544896 | bytes 5513232 | tf_op jit(solution)/shard_map/ksu,kub->ksb/dot_general | solution.py:47
  443.7 0.0 slice-start.1
  443.7 0.0 copy-start.7
  443.7 7.6 %fusion.56 = f32[4,512,128]{2,1,0:T(8,128)S(1)} fusion(f32[4,512,512]{2,1,0:T(8,128)S(1)} %copy-done.2, f32[4,512]{1,0:T(4,128)S(1)} %copy.28, s32[4]{0:T(128)S(1)} %add_add_fusion, s32[512,128]{1,0:T(8,128)S(1)} %copy-done.4), kind=kOutput, calls=%fused_computation.92 | convolution fusion | flops 1614544896 | bytes 5513232 | tf_op jit(solution)/shard_map/ksu,kub->ksb/dot_general | solution.py:47
  451.4 4.3 subtract_multiply_fusion
  455.7 13.0 %fusion.47 = f32[4,512,128]{2,1,0:T(8,128)S(1)} fusion(f32[4,512,128]{2,1,0:T(8,128)S(1)} %fusion.55, f32[4,512,512]{2,1,0:T(8,128)} %subtract_multiply_fusion, f32[4]{0:T(128)S(1)} %multiply_add_fusion, f32[4,512]{1,0:T(4,128)S(1)} %copy.28, s32[4]{0:T(128)S(1)} %add_add_fusion, s32[512,128]{1,0:T(8,128)S(1)} %copy-done.4), kind=kOutput, calls=%fused_computation.81 | convolution fusion | flops 1620312064 | bytes 6561824 | tf_op jit(solution)/shard_map/ksu,kub->ksb/dot_general | solution.py:47
  468.7 3.7 fusion.105
  472.5 11.5 %fusion.45 = f32[4,512,128]{2,1,0:T(8,128)S(1)} fusion(f32[4,512,128]{2,1,0:T(8,128)S(1)} %fusion.56, f32[4,512,512]{2,1,0:T(8,128)S(1)} %copy-done.8, f32[4]{0:T(128)S(1)} %multiply_add_fusion, f32[4,512]{1,0:T(4,128)S(1)} %copy.28, s32[4]{0:T(128)S(1)} %add_add_fusion, s32[512,128]{1,0:T(8,128)S(1)} %copy-done.4), kind=kOutput, calls=%fused_computation.79 | convolution fusion | flops 1620312064 | bytes 6561824 | tf_op jit(solution)/shard_map/ksu,kub->ksb/dot_general | solution.py:47
  483.9 3.7 fusion.106
  487.6 7.9 %fusion.48 = bf16[4,512,128]{2,1,0:T(8,128)(2,1)S(1)} fusion(f32[4,512,128]{2,1,0:T(8,128)S(1)} %fusion.47, f32[4,512,128]{2,1,0:T(8,128)S(1)} %fusion.105, f32[4,512,512]{2,1,0:T(8,128)S(1)} %copy-done.8, f32[4,512,128]{2,1,0:T(8,128)S(1)} %fusion.45, f32[4]{0:T(128)S(1)} %multiply_add_fusion, f32[4,512]{1,0:T(4,128)S(1)} %copy.28, s32[4]{0:T(128)S(1)} %add_add_fusion, ...), kind=kOutput, calls=%fused_computation.82 | convolution fusion | flops 1616379904 | bytes 8134688 | tf_op jit(solution)/shard_map/ksu,kub->ksb/dot_general | solution.py:47
  495.5 0.8 fusion.19
  496.3 8.0 %fusion.49 = bf16[4,512,128]{2,1,0:T(8,128)(2,1)S(1)} fusion(f32[4,512,128]{2,1,0:T(8,128)S(1)} %fusion.45, f32[4,512,128]{2,1,0:T(8,128)S(1)} %fusion.106, f32[4,512,512]{2,1,0:T(8,128)S(1)} %copy-done.8, f32[4,512,128]{2,1,0:T(8,128)S(1)} %fusion.47, f32[4]{0:T(128)S(1)} %multiply_add_fusion, f32[4,512]{1,0:T(4,128)S(1)} %copy.28, s32[4]{0:T(128)S(1)} %add_add_fusion, ...), kind=kOutput, calls=%fused_computation.83 | convolution fusion | flops 1616379904 | bytes 8134688 | tf_op jit(solution)/shard_map/ksu,kub->ksb/dot_general | solution.py:47
  504.3 0.8 fusion.18
  505.1 2.2 fusion.26
  507.3 3.2 stack.21
  510.5 3.3 copy.33
  513.8 4.3 fusion.27
  518.1 3.3 stack.22
  521.4 2.0 copy.34
  523.4 0.6 fusion.13
  524.1 51.8 %all_to_all.10 = bf16[32,2,16,256,4]{3,2,4,1,0:T(8,128)(2,1)S(1)} all-to-all(bf16[32,2,16,256,4]{3,2,4,1,0:T(8,128)(2,1)S(1)} %bitcast.112), channel_id=1, replica_groups=mesh['blk'=4,'st'=8] {'blk','st'}, dimensions={0} | all-to-all | bytes 4194304 | tf_op jit(solution)/shard_map/all_to_all | solution.py:107
  575.9 0.2 copy.35
  576.1 2.9 copy.36
  (22 shorter events, 0.1 us)
Async XLA Ops:
  1.0 14.9 %copy-start.5 = (f32[64]{0:T(128)S(1)}, f32[64]{0:T(128)}, u32[]{:S(2)}) copy-start(f32[64]{0:T(128)} %param.7) | copy-start | bytes 772
  1.0 14.9 %copy-start.6 = (s32[1,64]{1,0:T(1,128)S(1)}, s32[1,64]{1,0:T(1,128)}, u32[]{:S(2)}) copy-start(s32[1,64]{1,0:T(1,128)} %param.8) | copy-start | bytes 772
  86.8 4.6 copy-start
  129.8 196.9 %all-to-all-start = ((bf16[32,4,2,64,256]{4,1,3,2,0:T(4,128)(2,1)}), bf16[32,4,2,64,256]{4,1,3,2,0:T(4,128)(2,1)}, u32[]{:S(2)}, u32[]{:S(2)}) async-start(bf16[32,4,2,64,256]{4,1,3,2,0:T(4,128)(2,1)} %copy_bitcast_fusion), calls=%async_computation | async-start | bytes 16777216 | tf_op jit(solution)/shard_map/all_to_all | solution.py:73
  353.2 6.0 %copy-start.1 = (bf16[4,2,512,1024]{3,2,0,1:T(8,128)(2,1)S(1)}, bf16[4,2,512,1024]{3,2,0,1:T(8,128)(2,1)}, u32[]{:S(2)}) copy-start(bf16[4,2,512,1024]{3,2,0,1:T(8,128)(2,1)} %reshape.71) | copy-start | bytes 25165828
  367.8 66.0 %copy-start.4 = (s32[512,128]{1,0:T(8,128)S(1)}, s32[512,128]{1,0:T(8,128)}, u32[]{:S(2)}) copy-start(s32[512,128]{1,0:T(8,128)} %param.9) | copy-start | bytes 786436
  433.8 9.9 %copy-start.2 = (f32[4,512,512]{2,1,0:T(8,128)S(1)}, f32[4,512,512]{2,1,0:T(8,128)}, u32[]{:S(2)}) copy-start(f32[4,512,512]{2,1,0:T(8,128)} %add_multiply_fusion) | copy-start | bytes 12582916
  433.8 17.6 %slice-start = ((s8[8388608]{0:T(1024)(128)(4,1)}), s8[4194304]{0:T(1024)(128)(4,1)S(1)}, s32[]{:S(2)}) async-start(s8[8388608]{0:T(1024)(128)(4,1)} %bitcast.108), calls=%async_computation.2 | async-start | bytes 8388608
  443.7 7.7 %slice-start.1 = ((s8[8388608]{0:T(1024)(128)(4,1)}), s8[4194304]{0:T(1024)(128)(4,1)S(1)}, s32[]{:S(2)}) async-start(s8[8388608]{0:T(1024)(128)(4,1)} %bitcast.108), calls=%async_computation.3 | async-start | bytes 8388608
  443.7 7.7 %copy-start.7 = (f32[4,512,512]{2,1,0:T(8,128)S(1)}, f32[4,512,512]{2,1,0:T(8,128)}, u32[]{:S(2)}) copy-start(f32[4,512,512]{2,1,0:T(8,128)} %fusion.20) | copy-start | bytes 12582916
  468.7 3.7 copy-start.8
  518.1 5.3 copy-start.3

commit v2 on v1

--- a/solution.py
+++ b/solution.py
@@ -59,32 +59,55 @@
     return weight_re, weight_im
 
 
+def chunk_count(nt):
+    for n in (4, 2):
+        if nt % n == 0:
+            return n
+    return 1
+
+
 def local(voltages, filter_coeffs, station_gain, flags, steer_index):
     nblk = lax.axis_size("blk")
     nst = lax.axis_size("st")
     ndev = nblk * nst
-    cos_table, sin_table = dft_tables(filter_coeffs.shape[1])
+    ntaps, width = filter_coeffs.shape
+    cos_table, sin_table = dft_tables(width)
     row_gain = station_gain * flags[0].astype(jnp.float32)
-    filtered = polyphase(voltages[:, 0], filter_coeffs, row_gain)
-    local_spec = transform(filtered, cos_table, sin_table)
-    _, ls, nt, nk = local_spec.shape
+    samples = voltages[:, 0]
+    ls = samples.shape[1]
+    nt = samples.shape[2] // width - ntaps + 1
+    nk = width
     kc = nk // ndev
-    send = local_spec.reshape(2, ls, nt, ndev, kc).transpose(3, 4, 0, 1, 2)
-    recv = lax.all_to_all(send, AXES, split_axis=0, concat_axis=0, tiled=True)
-    recv = recv.reshape(nblk, nst, kc, 2, ls, nt)
-    spec = recv.transpose(2, 3, 1, 4, 0, 5).reshape(kc, 2, nst * ls, nblk * nt)
+    nch = chunk_count(nt)
+    tc = nt // nch
     stations = nst * ls
     counted = nblk * nt
-    spec_re = spec[:, 0]
-    spec_im = spec[:, 1]
     cdot = lambda a, b: jnp.einsum("kst,kut->ksu", a, b, preferred_element_type=jnp.float32)
-    cov_re = cdot(spec_re, spec_re) + cdot(spec_im, spec_im)
-    cov_im = cdot(spec_im, spec_re) - cdot(spec_re, spec_im)
+    specs = []
+    cov_re = None
+    cov_im = None
+    for ch in range(nch):
+        t0 = ch * tc
+        piece = samples[:, :, t0 * width : (t0 + tc + ntaps - 1) * width]
+        filtered = polyphase(piece, filter_coeffs, row_gain)
+        local_spec = transform(filtered, cos_table, sin_table)
+        send = local_spec.reshape(2, ls, tc, ndev, kc).transpose(3, 4, 0, 1, 2)
+        recv = lax.all_to_all(send, AXES, split_axis=0, concat_axis=0, tiled=True)
+        recv = recv.reshape(nblk, nst, kc, 2, ls, tc)
+        spec = recv.transpose(2, 3, 1, 4, 0, 5).reshape(kc, 2, stations, nblk * tc)
+        specs.append(spec)
+        spec_re = spec[:, 0]
+        spec_im = spec[:, 1]
+        part_re = cdot(spec_re, spec_re) + cdot(spec_im, spec_im)
+        part_im = cdot(spec_im, spec_re) - cdot(spec_re, spec_im)
+        cov_re = part_re if cov_re is None else cov_re + part_re
+        cov_im = part_im if cov_im is None else cov_im + part_im
     me = lax.axis_index("blk") * nst + lax.axis_index("st")
     channel_ids = me * kc + jnp.arange(kc, dtype=jnp.int32)
     rows_re = cov_re / counted
     rows_im = cov_im / counted
-    diag_part = jnp.diagonal(rows_re, axis1=1, axis2=2)
+    eye = jnp.eye(stations, dtype=jnp.float32)
+    diag_part = jnp.sum(rows_re * eye[None], axis=2)
     load = jnp.sum(diag_part, axis=1) / stations + 1e-05
     phase_int = steer_index[None, :, :] * (channel_ids + 1)[:, None, None] % PHASES
     angle = phase_int.astype(jnp.float32) * (2.0 * math.pi / PHASES)
@@ -96,14 +119,19 @@
     half_re = weight_re.astype(jnp.bfloat16)
     half_im = weight_im.astype(jnp.bfloat16)
     bdot = lambda a, b: jnp.einsum("ksb,kst->kbt", a, b, preferred_element_type=jnp.float32)
-    beam_re = bdot(half_re, spec_re) + bdot(half_im, spec_im)
-    beam_im = bdot(half_re, spec_im) - bdot(half_im, spec_re)
     factor = 1.0 / math.sqrt(stations)
-    beam = (jnp.stack([beam_re, beam_im]) * factor).astype(jnp.bfloat16)
-    nb = beam.shape[2]
+    nb = half_re.shape[2]
     bc = nb // nst
-    out = beam.reshape(2, kc, nst, bc, nblk, nt).transpose(4, 2, 0, 3, 5, 1)
-    out = out.reshape(ndev, 2, bc, nt, kc)
+    outs = []
+    for spec in specs:
+        spec_re = spec[:, 0]
+        spec_im = spec[:, 1]
+        beam_re = bdot(half_re, spec_re) + bdot(half_im, spec_im)
+        beam_im = bdot(half_re, spec_im) - bdot(half_im, spec_re)
+        beam = (jnp.stack([beam_re, beam_im]) * factor).astype(jnp.bfloat16)
+        outs.append(beam.reshape(2, kc, nst, bc, nblk, tc))
+    beam = jnp.stack(outs, axis=5)
+    out = beam.transpose(4, 2, 0, 3, 5, 6, 1).reshape(ndev, 2, bc, nt, kc)
     got = lax.all_to_all(out, AXES, split_axis=0, concat_axis=0, tiled=True)
     got = got.transpose(1, 2, 3, 0, 4).reshape(2, bc, nt, ndev * kc)
     return got[:, :, None]

time: 589 us -> 632 us (1.073)
  waiting for transfers between devices: 189 us -> 0.8 us
  local copies, waits for them, and re-layouts: 138 us -> 235 us
  matrix products: 112 us -> 185 us
  other arithmetic: 80.1 us -> 117 us
  starting transfers between devices: 7.65 us -> 25.9 us
    all_to_all x1 -> x4, waiting for transfers between devices: 189 us -> 0.8 us  [local(): recv = lax.all_to_all(send, AXES, split_axis=0, concat_axis=0, tiled=True)]
    reshape x2 -> x13, local copies, waits for them, and re-layouts: 26.5 us -> 104 us  [the longest x4 50 us: local(): recv = recv.reshape(nblk, nst, kc, 2, ls, tc)]
    unnamed x22 -> x48, local copies, waits for them, and re-layouts: 0.89 us -> 65 us
    div x1 -> x0, local copies, waits for them, and re-layouts: 60.2 us -> none  [local(): rows_re = cov_re / counted]
    dot_general x4 -> x16, matrix products: 18.9 us -> 63.8 us  [local(): jnp.einsum('kst,kut->ksu', a, b, preferred_element_type=jnp.float32)]
    dot_general x8, matrix products: 65.3 us -> 87.2 us  [batched(): jnp.einsum('ksu,kub->ksb', matrix, vectors, precision=lax.Precision.HIGHEST)]
    all_to_all x1 -> x4, starting transfers between devices: 7.65 us -> 25.9 us  [local(): recv = lax.all_to_all(send, AXES, split_axis=0, concat_axis=0, tiled=True)]
    convert_element_type x1 -> x4, other arithmetic: 70.9 us -> 87.3 us  [polyphase(): return (filtered * row_gain[None, :, None, None]).astype(jnp.bfloat16)]
  transfers between devices with their start and end apart: 1 -> 4, of which waited for: 1 -> 1; matrix products, arithmetic and copies ran while one was open for 0% -> 42% of each run, Pallas kernels for 0% -> 0%
where the time goes in v2:
time: 632 us; the launch traced here: 620 us
  local copies, waits for them, and re-layouts  235 us (37%)
  matrix products  185 us (29%)
  other arithmetic  117 us (19%)
  blocking collectives  55.8 us (9%)
  starting transfers between devices  25.9 us (4%)
    convert_element_type x4, other arithmetic, polyphase(): return (filtered * row_gain[None, :, None, None]).astype(jnp.bfloat16)  87.3 us
    dot_general x8, matrix products, batched(): jnp.einsum('ksu,kub->ksb', matrix, vectors, precision=lax.Precision.HIGHEST)  87.2 us
    unnamed x48, local copies, waits for them, and re-layouts  65 us
    dot_general x16, matrix products, local(): jnp.einsum('kst,kut->ksu', a, b, preferred_element_type=jnp.float32)  63.8 us
    all_to_all x1, blocking collectives, local(): got = lax.all_to_all(out, AXES, split_axis=0, concat_axis=0, tiled=True)  55.8 us
    reshape x4, local copies, waits for them, and re-layouts, local(): recv = recv.reshape(nblk, nst, kc, 2, ls, tc)  50 us
    another operation x8, local copies, waits for them, and re-layouts  29.8 us
    another operation x16, local copies, waits for them, and re-layouts, local(): beam = (jnp.stack([beam_re, beam_im]) * factor).astype(jnp.bfloat16)  27.8 us
  transfers between devices with their start and end apart: 4, of which 1 were waited for; matrix products, arithmetic and copies ran while one was open for 42% of the time, Pallas kernels for 0%

profile of v2, /device:TPU:0, one launch (start us, length us, event | category | flops | bytes accessed | tf_op | source)
XLA Modules:
  0.0 620.5 jit_solution(11082686384137678407)
XLA Ops:
  1.0 9.2 %slice_convert_fusion.3 = (f32[2,64,9600]{2,1,0:T(8,128)}, f32[2,64,9600]{2,1,0:T(8,128)}, f32[2,64,9600]{2,1,0:T(8,128)}, f32[2,64,9600]{2,1,0:T(8,128)}) fusion(bf16[2,64,34176]{2,1,0:T(8,128)(2,1)} %bitcast.231), kind=kLoop, calls=%fused_computation.124 | loop fusion | flops 4915200 | bytes 29491200 | tf_op jit(solution)/shard_map/reshape | solution.py:26
  10.2 5.5 reshape.286
  15.7 21.8 %fusion.41 = bf16[2,64,64,128]{3,2,1,0:T(8,128)(2,1)S(1)} fusion(f32[2,64,75,128]{3,2,1,0:T(8,128)} %reshape.286, f32[64]{0:T(128)S(1)} %bitcast_multiply_fusion, f32[128]{0:T(128)S(1)} %get-tuple-element.21, f32[128]{0:T(128)S(1)} %get-tuple-element.22, f32[128]{0:T(128)S(1)} %get-tuple-element.12, f32[128]{0:T(128)S(1)} %get-tuple-element.13, ...), kind=kLoop, calls=%fused_computation.78 | loop fusion | flops 26214400 | bytes 52435200 | tf_op jit(solution)/shard_map/convert_element_type | solution.py:34
  50.6 4.0 copy_bitcast_fusion.7
  54.6 7.9 %reshape.305 = bf16[32,2,16384]{2,1,0:T(2,128)(2,1)} reshape(bf16[32,2,4,64,64]{4,3,2,1,0:T(8,128)(2,1)} %copy_bitcast_fusion.7) | data formatting | bytes 4194304
  62.4 7.9 %all-to-all-start = ((bf16[32,2,16384]{2,1,0:T(2,128)(2,1)}), bf16[32,2,16384]{2,1,0:T(2,128)(2,1)}, u32[]{:S(2)}, u32[]{:S(2)}) async-start(bf16[32,2,16384]{2,1,0:T(2,128)(2,1)} %reshape.305), calls=%async_computation | async-start | bytes 4194304 | tf_op jit(solution)/shard_map/all_to_all | solution.py:95
  70.3 5.5 reshape.288
  75.8 21.8 %fusion.28 = bf16[2,64,64,128]{3,2,1,0:T(8,128)(2,1)S(1)} fusion(f32[2,64,75,128]{3,2,1,0:T(8,128)} %reshape.288, f32[64]{0:T(128)S(1)} %bitcast_multiply_fusion, f32[128]{0:T(128)S(1)} %get-tuple-element.21, f32[128]{0:T(128)S(1)} %get-tuple-element.22, f32[128]{0:T(128)S(1)} %get-tuple-element.12, f32[128]{0:T(128)S(1)} %get-tuple-element.13, ...), kind=kLoop, calls=%fused_computation.53 | loop fusion | flops 26214400 | bytes 52435200 | tf_op jit(solution)/shard_map/convert_element_type | solution.py:34
  107.8 4.0 copy_bitcast_fusion.6
  111.7 7.9 %reshape.303 = bf16[32,2,16384]{2,1,0:T(2,128)(2,1)} reshape(bf16[32,2,4,64,64]{4,3,2,1,0:T(8,128)(2,1)} %copy_bitcast_fusion.6) | data formatting | bytes 4194304
  120.4 5.5 all-to-all-start.1
  125.9 5.5 reshape.290
  131.3 21.8 %fusion.15 = bf16[2,64,64,128]{3,2,1,0:T(8,128)(2,1)S(1)} fusion(f32[2,64,75,128]{3,2,1,0:T(8,128)} %reshape.290, f32[64]{0:T(128)S(1)} %bitcast_multiply_fusion, f32[128]{0:T(128)S(1)} %get-tuple-element.21, f32[128]{0:T(128)S(1)} %get-tuple-element.22, f32[128]{0:T(128)S(1)} %get-tuple-element.12, f32[128]{0:T(128)S(1)} %get-tuple-element.13, ...), kind=kLoop, calls=%fused_computation.28 | loop fusion | flops 26214400 | bytes 52435200 | tf_op jit(solution)/shard_map/convert_element_type | solution.py:34
  163.3 4.0 copy_bitcast_fusion.5
  167.3 7.9 %reshape.301 = bf16[32,2,16384]{2,1,0:T(2,128)(2,1)} reshape(bf16[32,2,4,64,64]{4,3,2,1,0:T(8,128)(2,1)} %copy_bitcast_fusion.5) | data formatting | bytes 4194304
  175.2 5.4 reshape.292
  180.6 6.3 %all-to-all-start.2 = ((bf16[32,2,16384]{2,1,0:T(2,128)(2,1)}), bf16[32,2,16384]{2,1,0:T(2,128)(2,1)}, u32[]{:S(2)}, u32[]{:S(2)}) async-start(bf16[32,2,16384]{2,1,0:T(2,128)(2,1)} %reshape.301), calls=%async_computation.2 | async-start | bytes 4194304 | tf_op jit(solution)/shard_map/all_to_all | solution.py:95
  186.9 21.8 %fusion.2 = bf16[2,64,64,128]{3,2,1,0:T(8,128)(2,1)S(1)} fusion(f32[2,64,75,128]{3,2,1,0:T(8,128)} %reshape.292, f32[64]{0:T(128)S(1)} %bitcast_multiply_fusion, f32[128]{0:T(128)S(1)} %get-tuple-element.21, f32[128]{0:T(128)S(1)} %get-tuple-element.22, f32[128]{0:T(128)S(1)} %get-tuple-element.12, f32[128]{0:T(128)S(1)} %get-tuple-element.13, ...), kind=kLoop, calls=%fused_computation.3 | loop fusion | flops 26214400 | bytes 52435200 | tf_op jit(solution)/shard_map/convert_element_type | solution.py:34
  218.9 4.0 copy_bitcast_fusion.4
  222.9 7.9 %reshape.299 = bf16[32,2,16384]{2,1,0:T(2,128)(2,1)} reshape(bf16[32,2,4,64,64]{4,3,2,1,0:T(8,128)(2,1)} %copy_bitcast_fusion.4) | data formatting | bytes 4194304
  230.8 8.3 %reshape.306 = bf16[32,2,4,64,64]{4,3,2,1,0:T(8,128)(2,1)} reshape(bf16[32,2,16384]{2,1,0:T(2,128)(2,1)} %all-to-all-done) | data formatting | bytes 4194304
  239.2 12.5 %copy.307 = bf16[4,8,4,2,64,64]{5,0,4,1,2,3:T(4,128)(2,1)} copy(bf16[4,8,4,2,64,64]{5,4,2,3,1,0:T(8,128)(2,1)} %bitcast.223) | data formatting | bytes 4194304 | tf_op jit(solution)/shard_map/reshape | solution.py:96
  251.7 6.0 reshape.271
  257.7 8.4 %reshape.304 = bf16[32,2,4,64,64]{4,3,2,1,0:T(8,128)(2,1)} reshape(bf16[32,2,16384]{2,1,0:T(2,128)(2,1)} %all-to-all-done.1) | data formatting | bytes 4194304
  266.0 12.5 %copy.306 = bf16[4,8,4,2,64,64]{5,0,4,1,2,3:T(4,128)(2,1)} copy(bf16[4,8,4,2,64,64]{5,4,2,3,1,0:T(8,128)(2,1)} %bitcast.225) | data formatting | bytes 4194304 | tf_op jit(solution)/shard_map/reshape | solution.py:96
  278.6 7.0 %reshape.275 = bf16[4,2,512,256]{3,2,0,1:T(8,128)(2,1)} reshape(bf16[4,2,8,64,4,64]{5,4,3,2,0,1:T(4,128)(2,1)} %bitcast.226) | data formatting | bytes 4194304 | tf_op jit(solution)/shard_map/reshape | solution.py:97
  288.2 6.3 %all-to-all-start.3 = ((bf16[32,2,16384]{2,1,0:T(2,128)(2,1)}), bf16[32,2,16384]{2,1,0:T(2,128)(2,1)}, u32[]{:S(2)}, u32[]{:S(2)}) async-start(bf16[32,2,16384]{2,1,0:T(2,128)(2,1)} %reshape.299), calls=%async_computation.3 | async-start | bytes 4194304 | tf_op jit(solution)/shard_map/all_to_all | solution.py:95
  294.5 8.0 %reshape.302 = bf16[32,2,4,64,64]{4,3,2,1,0:T(8,128)(2,1)} reshape(bf16[32,2,16384]{2,1,0:T(2,128)(2,1)} %all-to-all-done.2) | data formatting | bytes 4194304
  302.5 12.5 %copy.305 = bf16[4,8,4,2,64,64]{5,0,4,1,2,3:T(4,128)(2,1)} copy(bf16[4,8,4,2,64,64]{5,4,2,3,1,0:T(8,128)(2,1)} %bitcast.227) | data formatting | bytes 4194304 | tf_op jit(solution)/shard_map/reshape | solution.py:96
  314.9 6.4 %reshape.279 = bf16[4,2,512,256]{3,2,0,1:T(8,128)(2,1)S(1)} reshape(bf16[4,2,8,64,4,64]{5,4,3,2,0,1:T(4,128)(2,1)} %bitcast.228) | data formatting | bytes 4194304 | tf_op jit(solution)/shard_map/reshape | solution.py:97
  321.3 4.4 fusion.169
  353.0 8.1 %reshape.300 = bf16[32,2,4,64,64]{4,3,2,1,0:T(8,128)(2,1)} reshape(bf16[32,2,16384]{2,1,0:T(2,128)(2,1)} %all-to-all-done.3) | data formatting | bytes 4194304
  361.1 12.5 %copy.304 = bf16[4,8,4,2,64,64]{5,0,4,1,2,3:T(4,128)(2,1)} copy(bf16[4,8,4,2,64,64]{5,4,2,3,1,0:T(8,128)(2,1)} %bitcast.229) | data formatting | bytes 4194304 | tf_op jit(solution)/shard_map/reshape | solution.py:96
  373.6 7.0 %reshape.283 = bf16[4,2,512,256]{3,2,0,1:T(8,128)(2,1)} reshape(bf16[4,2,8,64,4,64]{5,4,3,2,0,1:T(4,128)(2,1)} %bitcast.230) | data formatting | bytes 4194304 | tf_op jit(solution)/shard_map/reshape | solution.py:97
  380.6 4.4 fusion.184
  388.4 11.4 %multiply_reduce_fusion = (f32[4]{0:T(128)S(1)}, f32[4,512]{1,0:T(4,128)S(1)}, f32[4,512,512]{1,2,0:T(8,128)}) fusion(f32[512,512]{0,1:T(8,128)S(1)} %fusion.149, f32[4,512,512]{1,2,0:T(8,128)} %fusion.184, bf16[4,2,512,256]{3,2,0,1:T(8,128)(2,1)S(1)} %copy-done.5, f32[4,512,512]{1,2,0:T(8,128)} %fusion.179, f32[4,512,512]{1,2,0:T(8,128)} %fusion.181, ...), kind=kOutput, calls=%fused_computation.111 | convolution fusion | flops 547354624 | bytes 35659792 | tf_op jit(solution)/shard_map/kst,kut->ksu/dot_general | solution.py:85
  400.0 10.8 %add_multiply_fusion = f32[4,512,512]{1,2,0:T(8,128)S(1)} fusion(f32[4,512,512]{1,2,0:T(8,128)} %fusion.183, f32[4,512,512]{1,2,0:T(8,128)} %fusion.178, f32[4,512,512]{1,2,0:T(8,128)} %fusion.177, f32[4,512,512]{1,2,0:T(8,128)} %fusion.172, f32[4,512,512]{1,2,0:T(8,128)} %fusion.171, f32[4,512,512]{1,2,0:T(8,128)} %fusion.166, ...), kind=kOutput, calls=%fused_computation.109 | convolution fusion | flops 545259520 | bytes 35651584 | tf_op jit(solution)/shard_map/kst,kut->ksu/dot_general | solution.py:85
  410.7 10.3 %fusion.154 = f32[4,512,128]{2,1,0:T(8,128)S(1)} fusion(f32[4,512,512]{1,2,0:T(8,128)S(1)} %add_multiply_fusion, f32[4,512]{1,0:T(4,128)S(1)} %broadcast_add_fusion, s32[4]{0:T(128)S(1)} %add_add_fusion.1, s32[512,128]{1,0:T(8,128)S(1)} %copy-done.17), kind=kOutput, calls=%fused_computation.209 | convolution fusion | flops 1614544896 | bytes 5513232 | tf_op jit(solution)/shard_map/ksu,kub->ksb/dot_general | solution.py:47
  421.1 10.5 %fusion.151 = f32[4,512,128]{2,1,0:T(8,128)S(1)} fusion(f32[4,512,512]{1,2,0:T(8,128)S(1)} %add_multiply_fusion, f32[4,512]{1,0:T(4,128)S(1)} %broadcast_add_fusion, s32[4]{0:T(128)S(1)} %add_add_fusion.1, s32[512,128]{1,0:T(8,128)S(1)} %copy-done.17), kind=kOutput, calls=%fused_computation.206 | convolution fusion | flops 1614544896 | bytes 5513232 | tf_op jit(solution)/shard_map/ksu,kub->ksb/dot_general | solution.py:47
  431.6 14.8 %fusion.134 = f32[4,512,128]{2,1,0:T(8,128)S(1)} fusion(f32[4,512,128]{2,1,0:T(8,128)S(1)} %fusion.154, f32[4,512,512]{1,2,0:T(8,128)S(1)} %copy-done.16, f32[4]{0:T(128)S(1)} %multiply_add_fusion, f32[4,512]{1,0:T(4,128)S(1)} %broadcast_add_fusion, s32[4]{0:T(128)S(1)} %add_add_fusion.1, s32[512,128]{1,0:T(8,128)S(1)} %copy-done.17), kind=kOutput, calls=%fused_computation.180 | convolution fusion | flops 1621360640 | bytes 6561824 | tf_op jit(solution)/shard_map/ksu,kub->ksb/dot_general | solution.py:47
  446.4 7.1 %fusion.320 = f32[4,512,128]{2,1,0:T(8,128)S(1)} fusion(f32[4,512,512]{1,2,0:T(8,128)S(1)} %add_multiply_fusion, f32[4,512,128]{2,1,0:T(8,128)S(1)} %fusion.134), kind=kOutput, calls=%fused_computation.380 | convolution fusion | flops 1610612736 | bytes 6291456 | tf_op jit(solution)/shard_map/ksu,kub->ksb/dot_general | solution.py:47
  453.5 14.7 %fusion.119 = f32[4,512,128]{2,1,0:T(8,128)S(1)} fusion(f32[4,512,128]{2,1,0:T(8,128)S(1)} %fusion.151, f32[4,512,512]{1,2,0:T(8,128)S(1)} %copy-done.16, f32[4]{0:T(128)S(1)} %multiply_add_fusion, f32[4,512]{1,0:T(4,128)S(1)} %broadcast_add_fusion, s32[4]{0:T(128)S(1)} %add_add_fusion.1, s32[512,128]{1,0:T(8,128)S(1)} %copy-done.17), kind=kOutput, calls=%fused_computation.175 | convolution fusion | flops 1621360640 | bytes 6561824 | tf_op jit(solution)/shard_map/ksu,kub->ksb/dot_general | solution.py:47
  468.2 7.1 %fusion.321 = f32[4,512,128]{2,1,0:T(8,128)S(1)} fusion(f32[4,512,512]{1,2,0:T(8,128)S(1)} %add_multiply_fusion, f32[4,512,128]{2,1,0:T(8,128)S(1)} %fusion.119), kind=kOutput, calls=%fused_computation.381 | convolution fusion | flops 1610612736 | bytes 6291456 | tf_op jit(solution)/shard_map/ksu,kub->ksb/dot_general | solution.py:47
  475.4 11.2 %fusion.128 = bf16[4,512,128]{2,1,0:T(8,128)(2,1)S(1)} fusion(f32[4,512,128]{2,1,0:T(8,128)S(1)} %fusion.119, f32[4,512,128]{2,1,0:T(8,128)S(1)} %fusion.320, f32[4,512,512]{1,2,0:T(8,128)S(1)} %copy-done.16, f32[4]{0:T(128)S(1)} %multiply_add_fusion, f32[4,512]{1,0:T(4,128)S(1)} %broadcast_add_fusion, s32[4]{0:T(128)S(1)} %add_add_fusion.1, ...), kind=kOutput, calls=%fused_computation.178 | convolution fusion | flops 1617428480 | bytes 7086112 | tf_op jit(solution)/shard_map/ksu,kub->ksb/dot_general | solution.py:47
  495.1 11.4 %fusion.143 = bf16[4,512,128]{2,1,0:T(8,128)(2,1)S(1)} fusion(f32[4,512,128]{2,1,0:T(8,128)S(1)} %fusion.134, f32[4,512,128]{2,1,0:T(8,128)S(1)} %fusion.321, f32[4,512,512]{1,2,0:T(8,128)S(1)} %copy-done.16, f32[4]{0:T(128)S(1)} %multiply_add_fusion, f32[4,512]{1,0:T(4,128)S(1)} %broadcast_add_fusion, s32[4]{0:T(128)S(1)} %add_add_fusion.1, ...), kind=kOutput, calls=%fused_computation.183 | convolution fusion | flops 1617428480 | bytes 7086112 | tf_op jit(solution)/shard_map/ksu,kub->ksb/dot_general | solution.py:47
  550.9 4.4 copy.261
  555.3 6.0 reshape.284
  561.3 55.8 %all_to_all.25 = bf16[32,2,16,256,4]{3,2,4,1,0:T(8,128)(2,1)S(1)} all-to-all(bf16[32,2,16,256,4]{3,2,4,1,0:T(8,128)(2,1)S(1)} %reshape.284), channel_id=1, replica_groups=mesh['blk'=4,'st'=8] {'blk','st'}, dimensions={0} | all-to-all | bytes 4194304 | tf_op jit(solution)/shard_map/all_to_all | solution.py:135
  (123 shorter events, 134.8 us)
Async XLA Ops:
  10.2 5.5 copy-start.18
  10.2 5.5 copy-start.19
  46.9 3.7 copy-start.10
  62.4 57.9 %all-to-all-start = ((bf16[32,2,16384]{2,1,0:T(2,128)(2,1)}), bf16[32,2,16384]{2,1,0:T(2,128)(2,1)}, u32[]{:S(2)}, u32[]{:S(2)}) async-start(bf16[32,2,16384]{2,1,0:T(2,128)(2,1)} %reshape.305), calls=%async_computation | async-start | bytes 4194304 | tf_op jit(solution)/shard_map/all_to_all | solution.py:95
  104.1 3.7 copy-start.7
  120.4 60.2 %all-to-all-start.1 = ((bf16[32,2,16384]{2,1,0:T(2,128)(2,1)}), bf16[32,2,16384]{2,1,0:T(2,128)(2,1)}, u32[]{:S(2)}, u32[]{:S(2)}) async-start(bf16[32,2,16384]{2,1,0:T(2,128)(2,1)} %reshape.303), calls=%async_computation.1 | async-start | bytes 4194304 | tf_op jit(solution)/shard_map/all_to_all | solution.py:95
  159.6 3.7 copy-start.8
  180.6 107.6 %all-to-all-start.2 = ((bf16[32,2,16384]{2,1,0:T(2,128)(2,1)}), bf16[32,2,16384]{2,1,0:T(2,128)(2,1)}, u32[]{:S(2)}, u32[]{:S(2)}) async-start(bf16[32,2,16384]{2,1,0:T(2,128)(2,1)} %reshape.301), calls=%async_computation.2 | async-start | bytes 4194304 | tf_op jit(solution)/shard_map/all_to_all | solution.py:95
  215.2 3.7 copy-start.9
  257.7 27.9 %copy-start = (bf16[4,2,512,256]{3,2,0,1:T(8,128)(2,1)}, bf16[4,2,512,256]{3,2,0,1:T(8,128)(2,1)S(1)}, u32[]{:S(2)}) copy-start(bf16[4,2,512,256]{3,2,0,1:T(8,128)(2,1)S(1)} %reshape.271) | copy-start | bytes 6291460
  288.2 64.8 %all-to-all-start.3 = ((bf16[32,2,16384]{2,1,0:T(2,128)(2,1)}), bf16[32,2,16384]{2,1,0:T(2,128)(2,1)}, u32[]{:S(2)}, u32[]{:S(2)}) async-start(bf16[32,2,16384]{2,1,0:T(2,128)(2,1)} %reshape.299), calls=%async_computation.3 | async-start | bytes 4194304 | tf_op jit(solution)/shard_map/all_to_all | solution.py:95
  321.3 4.4 copy-start.3
  331.1 5.5 copy-start.1
  380.6 4.4 copy-start.5
  385.0 3.4 copy-start.6
  400.0 10.8 %copy-start.17 = (s32[512,128]{1,0:T(8,128)S(1)}, s32[512,128]{1,0:T(8,128)}, u32[]{:S(2)}) copy-start(s32[512,128]{1,0:T(8,128)} %param.9) | copy-start | bytes 786436
  421.1 10.6 %copy-start.16 = (f32[4,512,512]{1,2,0:T(8,128)S(1)}, f32[4,512,512]{1,2,0:T(8,128)}, u32[]{:S(2)}) copy-start(f32[4,512,512]{1,2,0:T(8,128)} %get-tuple-element.23) | copy-start | bytes 12582916
  475.4 11.2 %copy-start.4 = (bf16[4,2,512,256]{3,2,0,1:T(8,128)(2,1)S(1)}, bf16[4,2,512,256]{3,2,0,1:T(8,128)(2,1)}, u32[]{:S(2)}) copy-start(bf16[4,2,512,256]{3,2,0,1:T(8,128)(2,1)} %reshape.275) | copy-start | bytes 6291460
  486.6 1.6 copy-start.2
  545.1 1.8 copy-start.11
  545.1 1.8 copy-start.12
  546.7 2.5 copy-start.13
  546.7 2.5 copy-start.14
  546.7 2.5 copy-start.15

commit v3 on v1

--- a/solution.py
+++ b/solution.py
@@ -69,44 +69,45 @@
     local_spec = transform(filtered, cos_table, sin_table)
     _, ls, nt, nk = local_spec.shape
     kc = nk // ndev
-    send = local_spec.reshape(2, ls, nt, ndev, kc).transpose(3, 4, 0, 1, 2)
-    recv = lax.all_to_all(send, AXES, split_axis=0, concat_axis=0, tiled=True)
-    recv = recv.reshape(nblk, nst, kc, 2, ls, nt)
-    spec = recv.transpose(2, 3, 1, 4, 0, 5).reshape(kc, 2, nst * ls, nblk * nt)
     stations = nst * ls
     counted = nblk * nt
-    spec_re = spec[:, 0]
-    spec_im = spec[:, 1]
-    cdot = lambda a, b: jnp.einsum("kst,kut->ksu", a, b, preferred_element_type=jnp.float32)
-    cov_re = cdot(spec_re, spec_re) + cdot(spec_im, spec_im)
-    cov_im = cdot(spec_im, spec_re) - cdot(spec_re, spec_im)
+    send = local_spec.reshape(2, ls, nt, ndev, kc).transpose(4, 3, 0, 1, 2)
     me = lax.axis_index("blk") * nst + lax.axis_index("st")
-    channel_ids = me * kc + jnp.arange(kc, dtype=jnp.int32)
-    rows_re = cov_re / counted
-    rows_im = cov_im / counted
-    diag_part = jnp.diagonal(rows_re, axis1=1, axis2=2)
-    load = jnp.sum(diag_part, axis=1) / stations + 1e-05
-    phase_int = steer_index[None, :, :] * (channel_ids + 1)[:, None, None] % PHASES
-    angle = phase_int.astype(jnp.float32) * (2.0 * math.pi / PHASES)
-    steer_re = jnp.cos(angle)
-    steer_im = jnp.sin(angle)
-    load_full = load[:, None, None]
-    diag_total = (diag_part + load[:, None])[:, :, None]
-    weight_re, weight_im = iterate(rows_re, rows_im, steer_re, steer_im, diag_total, load_full)
-    half_re = weight_re.astype(jnp.bfloat16)
-    half_im = weight_im.astype(jnp.bfloat16)
-    bdot = lambda a, b: jnp.einsum("ksb,kst->kbt", a, b, preferred_element_type=jnp.float32)
-    beam_re = bdot(half_re, spec_re) + bdot(half_im, spec_im)
-    beam_im = bdot(half_re, spec_im) - bdot(half_im, spec_re)
+    eye = jnp.eye(stations, dtype=jnp.float32)
     factor = 1.0 / math.sqrt(stations)
-    beam = (jnp.stack([beam_re, beam_im]) * factor).astype(jnp.bfloat16)
-    nb = beam.shape[2]
-    bc = nb // nst
-    out = beam.reshape(2, kc, nst, bc, nblk, nt).transpose(4, 2, 0, 3, 5, 1)
-    out = out.reshape(ndev, 2, bc, nt, kc)
-    got = lax.all_to_all(out, AXES, split_axis=0, concat_axis=0, tiled=True)
-    got = got.transpose(1, 2, 3, 0, 4).reshape(2, bc, nt, ndev * kc)
-    return got[:, :, None]
+    cdot = lambda a, b: jnp.einsum("st,ut->su", a, b, preferred_element_type=jnp.float32)
+    bdot = lambda a, b: jnp.einsum("sb,st->bt", a, b, preferred_element_type=jnp.float32)
+    got = []
+    for c in range(kc):
+        recv = lax.all_to_all(send[c], AXES, split_axis=0, concat_axis=0, tiled=True)
+        recv = recv.reshape(nblk, nst, 2, ls, nt)
+        spec = recv.transpose(2, 1, 3, 0, 4).reshape(2, stations, counted)
+        spec_re = spec[0]
+        spec_im = spec[1]
+        rows_re = (cdot(spec_re, spec_re) + cdot(spec_im, spec_im)) / counted
+        rows_im = (cdot(spec_im, spec_re) - cdot(spec_re, spec_im)) / counted
+        diag_part = jnp.sum(rows_re * eye, axis=1)
+        load = jnp.sum(diag_part) / stations + 1e-05
+        channel_no = me * kc + c
+        phase_int = steer_index * (channel_no + 1) % PHASES
+        angle = phase_int.astype(jnp.float32) * (2.0 * math.pi / PHASES)
+        steer_re = jnp.cos(angle)
+        steer_im = jnp.sin(angle)
+        diag_total = (diag_part + load)[:, None]
+        weight_re, weight_im = iterate(
+            rows_re[None], rows_im[None], steer_re[None], steer_im[None], diag_total[None], load
+        )
+        half_re = weight_re[0].astype(jnp.bfloat16)
+        half_im = weight_im[0].astype(jnp.bfloat16)
+        beam_re = bdot(half_re, spec_re) + bdot(half_im, spec_im)
+        beam_im = bdot(half_re, spec_im) - bdot(half_im, spec_re)
+        beam = (jnp.stack([beam_re, beam_im]) * factor).astype(jnp.bfloat16)
+        nb = beam.shape[1]
+        bc = nb // nst
+        out = beam.reshape(2, nst, bc, nblk, nt).transpose(3, 1, 0, 2, 4).reshape(ndev, 2, bc, nt)
+        got.append(lax.all_to_all(out, AXES, split_axis=0, concat_axis=0, tiled=True))
+    res = jnp.stack(got, axis=4).transpose(1, 2, 3, 0, 4).reshape(2, bc, nt, ndev * kc)
+    return res[:, :, None]
 
 
 def fb_transform(filtered, cos_table, sin_table):

time: 589 us -> 534 us (0.907)
  waiting for transfers between devices: 189 us -> 58.4 us
  matrix products: 112 us -> 180 us
  local copies, waits for them, and re-layouts: 138 us -> 91.8 us
  starting transfers between devices: 7.65 us -> 31.6 us
  blocking collectives: 51.8 us -> 75.6 us
    all_to_all x1 -> x6, waiting for transfers between devices: 189 us -> 58.4 us  [the longest x3 44.3 us: local(): lax.all_to_all(send[c], AXES, split_axis=0, concat_axis=0, tiled=True)]
    div x1 -> x0, local copies, waits for them, and re-layouts: 60.2 us -> none  [local(): rows_re = cov_re / counted]
    dot_general x8 -> x32, matrix products: 65.3 us -> 109 us  [batched(): jnp.einsum('ksu,kub->ksb', matrix, vectors, precision=lax.Precision.HIGHEST)]
    all_to_all x1 -> x6, starting transfers between devices: 7.65 us -> 31.6 us  [the longest x3 18.2 us: local(): lax.all_to_all(out, AXES, split_axis=0, concat_axis=0, tiled=True)]
    all_to_all x1 -> x2, blocking collectives: 51.8 us -> 75.6 us  [the longest x1 57.2 us: local(): lax.all_to_all(send[c], AXES, split_axis=0, concat_axis=0, tiled=True)]
    dot_general x8 -> x32, matrix products: 27 us -> 50.4 us  [the longest x16 28 us: local(): jnp.einsum('st,ut->su', a, b, preferred_element_type=jnp.float32)]
    reshape x2 -> x4, local copies, waits for them, and re-layouts: 26.5 us -> 12 us  [local(): recv = recv.reshape(nblk, nst, 2, ls, nt)]
    another operation x2 -> x4, local copies, waits for them, and re-layouts: 13.8 us -> 27.2 us  [transform(): return jnp.stack([out_re, out_im]).astype(jnp.bfloat16)]
  transfers between devices with their start and end apart: 1 -> 6, of which waited for: 1 -> 2; matrix products, arithmetic and copies ran while one was open for 0% -> 32% of each run, Pallas kernels for 0% -> 0%
where the time goes in v3:
time: 534 us; the launch traced here: 525 us
  matrix products  180 us (34%)
  local copies, waits for them, and re-layouts  91.8 us (17%)
  other arithmetic  84 us (16%)
  blocking collectives  75.6 us (14%)
  waiting for transfers between devices  58.4 us (11%)
  starting transfers between devices  31.6 us (6%)
    dot_general x32, matrix products, batched(): jnp.einsum('ksu,kub->ksb', matrix, vectors, precision=lax.Precision.HIGHEST)  109 us
    convert_element_type x1, other arithmetic, polyphase(): return (filtered * row_gain[None, :, None, None]).astype(jnp.bfloat16)  71 us
    all_to_all x1, blocking collectives, local(): lax.all_to_all(send[c], AXES, split_axis=0, concat_axis=0, tiled=True)  57.2 us
    all_to_all x3, waiting for transfers between devices, local(): lax.all_to_all(send[c], AXES, split_axis=0, concat_axis=0, tiled=True)  44.3 us
    dot_general x16, matrix products, local(): jnp.einsum('st,ut->su', a, b, preferred_element_type=jnp.float32)  28 us
    another operation x4, local copies, waits for them, and re-layouts, transform(): return jnp.stack([out_re, out_im]).astype(jnp.bfloat16)  27.2 us
    dot_general x16, matrix products, local(): jnp.einsum('sb,st->bt', a, b, preferred_element_type=jnp.float32)  22.4 us
    another operation x16, local copies, waits for them, and re-layouts, local(): beam = (jnp.stack([beam_re, beam_im]) * factor).astype(jnp.bfloat16)  20.9 us
  transfers between devices with their start and end apart: 6, of which 2 were waited for; matrix products, arithmetic and copies ran while one was open for 32% of the time, Pallas kernels for 0%

profile of v3, /device:TPU:0, one launch (start us, length us, event | category | flops | bytes accessed | tf_op | source)
XLA Modules:
  0.0 525.1 jit_solution(5239286948181572614)
XLA Ops:
  1.0 14.9 %reshape.429 = f32[2,64,267,128]{3,2,1,0:T(8,128)} reshape(bf16[2,1,64,34176]{3,2,1,0:T(8,128)(2,1)} %param.5) | data formatting | bytes 26247168 | tf_op jit(solution)/shard_map/convert_element_type | solution.py:26
  15.9 71.0 %fusion.2 = bf16[2,64,256,128]{3,2,1,0:T(8,128)(2,1)} fusion(f32[2,64,267,128]{3,2,1,0:T(8,128)} %reshape.429, f32[64]{0:T(128)S(1)} %bitcast_multiply_fusion, f32[128]{0:T(128)S(1)} %get-tuple-element.35, f32[128]{0:T(128)S(1)} %get-tuple-element.36, f32[128]{0:T(128)S(1)} %get-tuple-element.26, f32[128]{0:T(128)S(1)} %get-tuple-element.27, ...), kind=kLoop, calls=%fused_computation.3 | loop fusion | flops 104857600 | bytes 209721600 | tf_op jit(solution)/shard_map/convert_element_type | solution.py:34
  86.9 3.8 fusion.14
  91.5 4.7 fusion.13
  96.3 3.5 add_convert_fusion
  99.8 7.1 %stack.60 = bf16[1,64,256,32,4]{2,4,3,1,0:T(4,128)(2,1)} reshape(bf16[64,256,128]{1,2,0:T(8,128)(2,1)} %add_convert_fusion) | data formatting | bytes 8388608 | tf_op jit(solution)/shard_map/stack | solution.py:43
  106.9 6.6 %copy.14 = bf16[1,64,256,32,4]{2,1,0,3,4:T(8,128)(2,1)} copy(bf16[1,64,256,32,4]{2,4,3,1,0:T(4,128)(2,1)} %stack.60) | data formatting | bytes 8388608 | tf_op jit(solution)/shard_map/stack | solution.py:43
  113.5 8.1 %subtract_convert_fusion = bf16[64,256,128]{1,2,0:T(8,128)(2,1)} fusion(f32[64,256,128]{1,2,0:T(8,128)} %fusion.13, bf16[2,64,256,128]{3,2,1,0:T(8,128)(2,1)} %fusion.2), kind=kOutput, calls=%fused_computation.26 | convolution fusion | flops 541327360 | bytes 16777216 | tf_op jit(solution)/shard_map/stc,ck->stk/dot_general | solution.py:40
  121.5 6.9 %stack.61 = bf16[1,64,256,32,4]{2,4,3,1,0:T(4,128)(2,1)} reshape(bf16[64,256,128]{1,2,0:T(8,128)(2,1)} %subtract_convert_fusion) | data formatting | bytes 8388608 | tf_op jit(solution)/shard_map/stack | solution.py:43
  128.4 6.6 %copy.15 = bf16[1,64,256,32,4]{2,1,0,3,4:T(8,128)(2,1)} copy(bf16[1,64,256,32,4]{2,4,3,1,0:T(4,128)(2,1)} %stack.61) | data formatting | bytes 8388608 | tf_op jit(solution)/shard_map/stack | solution.py:43
  135.1 6.4 %maximum_bitcast_fusion = bf16[4,32,2,64,256]{4,3,2,1,0:T(8,128)(2,1)} fusion(bf16[1,64,256,32,4]{2,1,0,3,4:T(8,128)(2,1)} %copy.15, bf16[1,64,256,32,4]{2,1,0,3,4:T(8,128)(2,1)S(1)} %copy-done.3), kind=kLoop, calls=%fused_computation.25 | loop fusion | flops 4194304 | bytes 16777216 | tf_op jit(solution)/shard_map/transpose | solution.py:74
  141.4 5.7 %slice_bitcast_fusion.13 = (bf16[32,2,64,256]{3,2,1,0:T(8,128)(2,1)S(1)}, bf16[32,2,64,256]{3,2,1,0:T(8,128)(2,1)}, bf16[32,2,64,256]{3,2,1,0:T(8,128)(2,1)}, bf16[32,2,64,256]{3,2,1,0:T(8,128)(2,1)}) fusion(bf16[4,32,2,64,256]{4,3,2,1,0:T(8,128)(2,1)} %maximum_bitcast_fusion), kind=kLoop, calls=%fused_computation.37 | loop fusion | bytes 16777216 | tf_op jit(solution)/shard_map/squeeze | solution.py:82
  147.1 57.2 %all_to_all.40 = bf16[32,2,64,256]{3,2,1,0:T(8,128)(2,1)S(1)} all-to-all(bf16[32,2,64,256]{3,2,1,0:T(8,128)(2,1)S(1)} %get-tuple-element.13), channel_id=1, replica_groups=mesh['blk'=4,'st'=8] {'blk','st'}, dimensions={0} | all-to-all | bytes 4194304 | tf_op jit(solution)/shard_map/all_to_all | solution.py:82
  204.3 3.5 all-to-all-start.2
  213.5 44.3 %all-to-all-done.2 = bf16[32,2,64,256]{3,2,1,0:T(8,128)(2,1)} async-done(((bf16[32,2,64,256]{3,2,1,0:T(8,128)(2,1)}), bf16[32,2,64,256]{3,2,1,0:T(8,128)(2,1)}, u32[]{:S(2)}, u32[]{:S(2)}) %all-to-all-start.2) | async-done | bytes 2097184 | tf_op jit(solution)/shard_map/all_to_all | solution.py:82
  257.8 4.0 all-to-all-start.4
  261.8 3.5 copy.60
  271.2 3.6 fusion.123
  275.4 4.0 fusion.181
  283.3 3.7 fusion.104
  292.2 3.5 fusion.99
  298.2 3.0 fusion.183
  302.8 3.5 fusion.84
  311.5 4.4 fusion.79
  316.0 5.9 %all-to-all-start.6 = ((bf16[32,2,64,256]{3,2,1,0:T(8,128)(2,1)}), bf16[32,2,64,256]{3,2,1,0:T(8,128)(2,1)}, u32[]{:S(2)}, u32[]{:S(2)}) async-start(bf16[32,2,64,256]{3,2,1,0:T(8,128)(2,1)} %get-tuple-element.14), calls=%async_computation.6 | async-start | bytes 4194304 | tf_op jit(solution)/shard_map/all_to_all | solution.py:82
  321.8 3.4 copy.59
  334.4 4.3 fusion.185
  338.7 3.9 fusion.219
  342.6 5.0 fusion.64
  352.1 3.5 fusion.59
  358.2 2.8 fusion.105
  373.2 3.4 copy.58
  383.8 4.6 fusion.188
  388.4 4.6 fusion.187
  393.1 4.1 fusion.106
  409.3 6.1 %all-to-all-start.1 = ((bf16[32,2,16,256]{3,2,1,0:T(8,128)(2,1)}), bf16[32,2,16,256]{3,2,1,0:T(8,128)(2,1)}, u32[]{:S(2)}, u32[]{:S(2)}) async-start(bf16[32,2,16,256]{3,2,1,0:T(8,128)(2,1)} %bitcast.287), calls=%async_computation.1 | async-start | bytes 1048576 | tf_op jit(solution)/shard_map/all_to_all | solution.py:108
  415.4 4.1 fusion.108
  431.8 4.1 fusion.110
  442.4 3.5 fusion.39
  445.9 4.2 fusion.44
  450.1 6.1 %all-to-all-start.3 = ((bf16[32,2,16,256]{3,2,1,0:T(8,128)(2,1)}), bf16[32,2,16,256]{3,2,1,0:T(8,128)(2,1)}, u32[]{:S(2)}, u32[]{:S(2)}) async-start(bf16[32,2,16,256]{3,2,1,0:T(8,128)(2,1)} %bitcast.289), calls=%async_computation.3 | async-start | bytes 1048576 | tf_op jit(solution)/shard_map/all_to_all | solution.py:108
  456.3 3.5 fusion.229
  470.8 4.1 fusion.111
  474.9 4.1 fusion.112
  479.0 6.1 %all-to-all-start.5 = ((bf16[32,2,16,256]{3,2,1,0:T(8,128)(2,1)}), bf16[32,2,16,256]{3,2,1,0:T(8,128)(2,1)}, u32[]{:S(2)}, u32[]{:S(2)}) async-start(bf16[32,2,16,256]{3,2,1,0:T(8,128)(2,1)} %bitcast.288), calls=%async_computation.5 | async-start | bytes 1048576 | tf_op jit(solution)/shard_map/all_to_all | solution.py:108
  487.3 14.1 %all-to-all-done.5 = bf16[32,2,16,256]{3,2,1,0:T(8,128)(2,1)} async-done(((bf16[32,2,16,256]{3,2,1,0:T(8,128)(2,1)}), bf16[32,2,16,256]{3,2,1,0:T(8,128)(2,1)}, u32[]{:S(2)}, u32[]{:S(2)}) %all-to-all-start.5) | async-done | bytes 524320 | tf_op jit(solution)/shard_map/all_to_all | solution.py:108
  501.4 18.4 %all_to_all.41 = bf16[32,2,16,256]{3,2,1,0:T(8,128)(2,1)S(1)} all-to-all(bf16[32,2,16,256]{3,2,1,0:T(8,128)(2,1)S(1)} %bitcast.290), channel_id=1, replica_groups=mesh['blk'=4,'st'=8] {'blk','st'}, dimensions={0} | all-to-all | bytes 1048576 | tf_op jit(solution)/shard_map/all_to_all | solution.py:108
  521.8 2.9 copy.37
  (175 shorter events, 111.1 us)
Async XLA Ops:
  1.0 14.9 %copy-start.39 = (f32[64]{0:T(128)S(1)}, f32[64]{0:T(128)}, u32[]{:S(2)}) copy-start(f32[64]{0:T(128)} %param.7) | copy-start | bytes 772
  1.0 14.9 %copy-start.40 = (s32[1,64]{1,0:T(1,128)S(1)}, s32[1,64]{1,0:T(1,128)}, u32[]{:S(2)}) copy-start(s32[1,64]{1,0:T(1,128)} %param.8) | copy-start | bytes 772
  86.9 4.6 copy-start
  128.4 6.6 %copy-start.3 = (bf16[1,64,256,32,4]{2,1,0,3,4:T(8,128)(2,1)S(1)}, bf16[1,64,256,32,4]{2,1,0,3,4:T(8,128)(2,1)}, u32[]{:S(2)}) copy-start(bf16[1,64,256,32,4]{2,1,0,3,4:T(8,128)(2,1)} %copy.14) | copy-start | bytes 12582916
  204.3 53.6 %all-to-all-start.2 = ((bf16[32,2,64,256]{3,2,1,0:T(8,128)(2,1)}), bf16[32,2,64,256]{3,2,1,0:T(8,128)(2,1)}, u32[]{:S(2)}, u32[]{:S(2)}) async-start(bf16[32,2,64,256]{3,2,1,0:T(8,128)(2,1)} %get-tuple-element.16), calls=%async_computation.2 | async-start | bytes 4194304 | tf_op jit(solution)/shard_map/all_to_all | solution.py:82
  257.8 58.1 %all-to-all-start.4 = ((bf16[32,2,64,256]{3,2,1,0:T(8,128)(2,1)}), bf16[32,2,64,256]{3,2,1,0:T(8,128)(2,1)}, u32[]{:S(2)}, u32[]{:S(2)}) async-start(bf16[32,2,64,256]{3,2,1,0:T(8,128)(2,1)} %get-tuple-element.15), calls=%async_computation.4 | async-start | bytes 4194304 | tf_op jit(solution)/shard_map/all_to_all | solution.py:82
  261.8 6.5 %copy-start.6 = (bf16[64,8,4,256]{3,1,2,0:T(8,128)(2,1)S(1)}, bf16[64,8,4,256]{3,1,2,0:T(8,128)(2,1)}, u32[]{:S(2)}) copy-start(bf16[64,8,4,256]{3,1,2,0:T(8,128)(2,1)} %copy.47) | copy-start | bytes 3145732
  261.8 6.5 %copy-start.41 = (f32[512,512]{0,1:T(8,128)S(1)}, f32[512,512]{0,1:T(8,128)}, u32[]{:S(2)}) copy-start(f32[512,512]{0,1:T(8,128)} %fusion.209) | copy-start | bytes 3145732
  266.1 9.3 %copy-start.35 = (s32[512,128]{1,0:T(8,128)S(1)}, s32[512,128]{1,0:T(8,128)}, u32[]{:S(2)}) copy-start(s32[512,128]{1,0:T(8,128)} %param.9) | copy-start | bytes 786436
  268.3 33.7 %copy-start.4 = (bf16[64,8,4,256]{3,1,2,0:T(8,128)(2,1)}, bf16[64,8,4,256]{3,1,2,0:T(8,128)(2,1)S(1)}, u32[]{:S(2)}) copy-start(bf16[64,8,4,256]{3,1,2,0:T(8,128)(2,1)S(1)} %copy.49) | copy-start | bytes 3145732
  275.3 11.7 %copy-start.14 = (f32[512,512]{0,1:T(8,128)S(1)}, f32[512,512]{0,1:T(8,128)}, u32[]{:S(2)}) copy-start(f32[512,512]{0,1:T(8,128)} %get-tuple-element.40) | copy-start | bytes 3145732
  283.3 18.0 %copy-start.19 = (f32[512,512]{0,1:T(8,128)}, f32[512,512]{0,1:T(8,128)S(1)}, u32[]{:S(2)}) copy-start(f32[512,512]{0,1:T(8,128)S(1)} %fusion.23) | copy-start | bytes 3145732
  283.3 14.9 %copy-start.13 = (f32[512,512]{0,1:T(8,128)S(1)}, f32[512,512]{0,1:T(8,128)}, u32[]{:S(2)}) copy-start(f32[512,512]{0,1:T(8,128)} %get-tuple-element.39) | copy-start | bytes 3145732
  287.0 14.3 %copy-start.25 = (f32[512,128]{1,0:T(8,128)}, f32[512,128]{1,0:T(8,128)S(1)}, u32[]{:S(2)}) copy-start(f32[512,128]{1,0:T(8,128)S(1)} %fusion.104) | copy-start | bytes 786436
  292.2 10.6 %copy-start.36 = (s32[512,128]{1,0:T(8,128)S(1)}, s32[512,128]{1,0:T(8,128)}, u32[]{:S(2)}) copy-start(s32[512,128]{1,0:T(8,128)} %param.9) | copy-start | bytes 786436
  295.7 5.6 %copy-start.27 = (f32[512,128]{1,0:T(8,128)}, f32[512,128]{1,0:T(8,128)S(1)}, u32[]{:S(2)}) copy-start(f32[512,128]{1,0:T(8,128)S(1)} %fusion.99) | copy-start | bytes 786436
  302.8 8.7 %copy-start.17 = (f32[512,512]{0,1:T(8,128)}, f32[512,512]{0,1:T(8,128)S(1)}, u32[]{:S(2)}) copy-start(f32[512,512]{0,1:T(8,128)S(1)} %fusion.21) | copy-start | bytes 3145732
  316.0 57.2 %all-to-all-start.6 = ((bf16[32,2,64,256]{3,2,1,0:T(8,128)(2,1)}), bf16[32,2,64,256]{3,2,1,0:T(8,128)(2,1)}, u32[]{:S(2)}, u32[]{:S(2)}) async-start(bf16[32,2,64,256]{3,2,1,0:T(8,128)(2,1)} %get-tuple-element.14), calls=%async_computation.6 | async-start | bytes 4194304 | tf_op jit(solution)/shard_map/all_to_all | solution.py:82
  326.2 44.6 %copy-start.1 = (bf16[64,8,4,256]{3,1,2,0:T(8,128)(2,1)}, bf16[64,8,4,256]{3,1,2,0:T(8,128)(2,1)S(1)}, u32[]{:S(2)}) copy-start(bf16[64,8,4,256]{3,1,2,0:T(8,128)(2,1)S(1)} %copy.50) | copy-start | bytes 3145732
  331.9 15.6 %copy-start.15 = (f32[512,512]{0,1:T(8,128)S(1)}, f32[512,512]{0,1:T(8,128)}, u32[]{:S(2)}) copy-start(f32[512,512]{0,1:T(8,128)} %get-tuple-element.38) | copy-start | bytes 3145732
  331.9 17.5 %copy-start.37 = (s32[512,128]{1,0:T(8,128)S(1)}, s32[512,128]{1,0:T(8,128)}, u32[]{:S(2)}) copy-start(s32[512,128]{1,0:T(8,128)} %param.9) | copy-start | bytes 786436
  334.3 33.9 %copy-start.21 = (f32[512,512]{0,1:T(8,128)}, f32[512,512]{0,1:T(8,128)S(1)}, u32[]{:S(2)}) copy-start(f32[512,512]{0,1:T(8,128)S(1)} %fusion.19) | copy-start | bytes 3145732
  338.7 19.5 %copy-start.20 = (f32[512,512]{0,1:T(8,128)S(1)}, f32[512,512]{0,1:T(8,128)}, u32[]{:S(2)}) copy-start(f32[512,512]{0,1:T(8,128)} %copy-done.19) | copy-start | bytes 3145732
  338.7 19.5 %copy-start.26 = (f32[512,128]{1,0:T(8,128)S(1)}, f32[512,128]{1,0:T(8,128)}, u32[]{:S(2)}) copy-start(f32[512,128]{1,0:T(8,128)} %copy-done.25) | copy-start | bytes 786436
  338.7 19.5 %copy-start.28 = (f32[512,128]{1,0:T(8,128)S(1)}, f32[512,128]{1,0:T(8,128)}, u32[]{:S(2)}) copy-start(f32[512,128]{1,0:T(8,128)} %copy-done.27) | copy-start | bytes 786436
  338.7 19.5 %copy-start.32 = (f32[512,128]{1,0:T(8,128)S(1)}, f32[512,128]{1,0:T(8,128)}, u32[]{:S(2)}) copy-start(f32[512,128]{1,0:T(8,128)} %fusion.211) | copy-start | bytes 786436
  347.6 20.6 %copy-start.29 = (f32[512,128]{1,0:T(8,128)}, f32[512,128]{1,0:T(8,128)S(1)}, u32[]{:S(2)}) copy-start(f32[512,128]{1,0:T(8,128)S(1)} %fusion.64) | copy-start | bytes 786436
  347.6 14.6 %copy-start.7 = (bf16[64,8,4,256]{3,1,2,0:T(8,128)(2,1)S(1)}, bf16[64,8,4,256]{3,1,2,0:T(8,128)(2,1)}, u32[]{:S(2)}) copy-start(bf16[64,8,4,256]{3,1,2,0:T(8,128)(2,1)} %copy.47) | copy-start | bytes 3145732
  347.6 15.7 %copy-start.18 = (f32[512,512]{0,1:T(8,128)S(1)}, f32[512,512]{0,1:T(8,128)}, u32[]{:S(2)}) copy-start(f32[512,512]{0,1:T(8,128)} %copy-done.17) | copy-start | bytes 3145732
  347.6 15.7 %copy-start.24 = (f32[512,128]{1,0:T(8,128)S(1)}, f32[512,128]{1,0:T(8,128)}, u32[]{:S(2)}) copy-start(f32[512,128]{1,0:T(8,128)} %fusion.79) | copy-start | bytes 786436
  347.6 15.7 %copy-start.33 = (f32[512,128]{1,0:T(8,128)S(1)}, f32[512,128]{1,0:T(8,128)}, u32[]{:S(2)}) copy-start(f32[512,128]{1,0:T(8,128)} %fusion.217) | copy-start | bytes 786436
  352.1 15.0 %copy-start.5 = (bf16[64,8,4,256]{3,1,2,0:T(8,128)(2,1)S(1)}, bf16[64,8,4,256]{3,1,2,0:T(8,128)(2,1)}, u32[]{:S(2)}) copy-start(bf16[64,8,4,256]{3,1,2,0:T(8,128)(2,1)} %copy-done.4) | copy-start | bytes 3145732
  355.6 16.4 %copy-start.31 = (f32[512,128]{1,0:T(8,128)}, f32[512,128]{1,0:T(8,128)S(1)}, u32[]{:S(2)}) copy-start(f32[512,128]{1,0:T(8,128)S(1)} %fusion.59) | copy-start | bytes 786436
  358.2 13.8 %copy-start.11 = (bf16[64,8,4,256]{3,1,2,0:T(8,128)(2,1)S(1)}, bf16[64,8,4,256]{3,1,2,0:T(8,128)(2,1)}, u32[]{:S(2)}) copy-start(bf16[64,8,4,256]{3,1,2,0:T(8,128)(2,1)} %copy-done.10) | copy-start | bytes 3145732
  409.3 29.1 %copy-start.2 = (bf16[64,8,4,256]{3,1,2,0:T(8,128)(2,1)S(1)}, bf16[64,8,4,256]{3,1,2,0:T(8,128)(2,1)}, u32[]{:S(2)}) copy-start(bf16[64,8,4,256]{3,1,2,0:T(8,128)(2,1)} %copy-done.1) | copy-start | bytes 3145732
  409.3 40.8 %all-to-all-start.1 = ((bf16[32,2,16,256]{3,2,1,0:T(8,128)(2,1)}), bf16[32,2,16,256]{3,2,1,0:T(8,128)(2,1)}, u32[]{:S(2)}, u32[]{:S(2)}) async-start(bf16[32,2,16,256]{3,2,1,0:T(8,128)(2,1)} %bitcast.287), calls=%async_computation.1 | async-start | bytes 1048576 | tf_op jit(solution)/shard_map/all_to_all | solution.py:108
  419.5 12.3 %copy-start.30 = (f32[512,128]{1,0:T(8,128)S(1)}, f32[512,128]{1,0:T(8,128)}, u32[]{:S(2)}) copy-start(f32[512,128]{1,0:T(8,128)} %copy-done.29) | copy-start | bytes 786436
  428.3 13.3 %copy-start.9 = (bf16[64,8,4,256]{3,1,2,0:T(8,128)(2,1)S(1)}, bf16[64,8,4,256]{3,1,2,0:T(8,128)(2,1)}, u32[]{:S(2)}) copy-start(bf16[64,8,4,256]{3,1,2,0:T(8,128)(2,1)} %copy-done.8) | copy-start | bytes 3145732
  430.5 10.2 %copy-start.16 = (f32[1,8,16,4,256]{4,2,0,1,3:T(8,128)S(1)}, f32[1,8,16,4,256]{4,2,0,1,3:T(8,128)}, u32[]{:S(2)}) copy-start(f32[1,8,16,4,256]{4,2,0,1,3:T(8,128)} %copy.24) | copy-start | bytes 1572868
  430.5 11.1 %copy-start.22 = (f32[512,512]{0,1:T(8,128)S(1)}, f32[512,512]{0,1:T(8,128)}, u32[]{:S(2)}) copy-start(f32[512,512]{0,1:T(8,128)} %fusion.228) | copy-start | bytes 3145732
  430.5 11.9 %copy-start.38 = (s32[512,128]{1,0:T(8,128)S(1)}, s32[512,128]{1,0:T(8,128)}, u32[]{:S(2)}) copy-start(s32[512,128]{1,0:T(8,128)} %param.9) | copy-start | bytes 786436
  430.5 11.9 %copy-start.43 = (f32[512,128]{1,0:T(8,128)S(1)}, f32[512,128]{1,0:T(8,128)}, u32[]{:S(2)}) copy-start(f32[512,128]{1,0:T(8,128)} %fusion.188) | copy-start | bytes 786436
  435.9 10.0 %copy-start.42 = (f32[512,128]{1,0:T(8,128)S(1)}, f32[512,128]{1,0:T(8,128)}, u32[]{:S(2)}) copy-start(f32[512,128]{1,0:T(8,128)} %fusion.187) | copy-start | bytes 786436
  440.6 15.6 %copy-start.12 = (f32[512,512]{0,1:T(8,128)S(1)}, f32[512,512]{0,1:T(8,128)}, u32[]{:S(2)}) copy-start(f32[512,512]{0,1:T(8,128)} %get-tuple-element.37) | copy-start | bytes 3145732
  442.4 3.5 copy-start.23
  445.9 23.1 %copy-start.34 = (f32[512,128]{1,0:T(8,128)}, f32[512,128]{1,0:T(8,128)S(1)}, u32[]{:S(2)}) copy-start(f32[512,128]{1,0:T(8,128)S(1)} %fusion.39) | copy-start | bytes 786436
  450.1 28.9 %all-to-all-start.3 = ((bf16[32,2,16,256]{3,2,1,0:T(8,128)(2,1)}), bf16[32,2,16,256]{3,2,1,0:T(8,128)(2,1)}, u32[]{:S(2)}, u32[]{:S(2)}) async-start(bf16[32,2,16,256]{3,2,1,0:T(8,128)(2,1)} %bitcast.289), calls=%async_computation.3 | async-start | bytes 1048576 | tf_op jit(solution)/shard_map/all_to_all | solution.py:108
  479.0 22.4 %all-to-all-start.5 = ((bf16[32,2,16,256]{3,2,1,0:T(8,128)(2,1)}), bf16[32,2,16,256]{3,2,1,0:T(8,128)(2,1)}, u32[]{:S(2)}, u32[]{:S(2)}) async-start(bf16[32,2,16,256]{3,2,1,0:T(8,128)(2,1)} %bitcast.288), calls=%async_computation.5 | async-start | bytes 1048576 | tf_op jit(solution)/shard_map/all_to_all | solution.py:108
  (2 other events, 3.5 us)

commit v4 on v3

--- a/solution.py
+++ b/solution.py
@@ -75,17 +75,20 @@
     me = lax.axis_index("blk") * nst + lax.axis_index("st")
     eye = jnp.eye(stations, dtype=jnp.float32)
     factor = 1.0 / math.sqrt(stations)
-    cdot = lambda a, b: jnp.einsum("st,ut->su", a, b, preferred_element_type=jnp.float32)
-    bdot = lambda a, b: jnp.einsum("sb,st->bt", a, b, preferred_element_type=jnp.float32)
+    hi = lax.Precision.HIGHEST
     got = []
     for c in range(kc):
         recv = lax.all_to_all(send[c], AXES, split_axis=0, concat_axis=0, tiled=True)
         recv = recv.reshape(nblk, nst, 2, ls, nt)
-        spec = recv.transpose(2, 1, 3, 0, 4).reshape(2, stations, counted)
-        spec_re = spec[0]
-        spec_im = spec[1]
-        rows_re = (cdot(spec_re, spec_re) + cdot(spec_im, spec_im)) / counted
-        rows_im = (cdot(spec_im, spec_re) - cdot(spec_re, spec_im)) / counted
+        spec = recv.transpose(2, 1, 3, 0, 4).reshape(2 * stations, counted)
+        gram = jnp.dot(spec, spec.T, preferred_element_type=jnp.float32)
+        g00 = gram[:stations, :stations]
+        g01 = gram[:stations, stations:]
+        g10 = gram[stations:, :stations]
+        g11 = gram[stations:, stations:]
+        rows_re = (g00 + g11) / counted
+        rows_im = (g10 - g01) / counted
+        rows = jnp.concatenate([rows_re, rows_im], axis=0)
         diag_part = jnp.sum(rows_re * eye, axis=1)
         load = jnp.sum(diag_part) / stations + 1e-05
         channel_no = me * kc + c
@@ -94,15 +97,25 @@
         steer_re = jnp.cos(angle)
         steer_im = jnp.sin(angle)
         diag_total = (diag_part + load)[:, None]
-        weight_re, weight_im = iterate(
-            rows_re[None], rows_im[None], steer_re[None], steer_im[None], diag_total[None], load
+        weight_re = steer_re / diag_total
+        weight_im = steer_im / diag_total
+        nb = weight_re.shape[1]
+        for sweep_no in range(2):
+            both = jnp.concatenate([weight_re, weight_im], axis=1)
+            prod = jnp.dot(rows, both, precision=hi)
+            prod_re = prod[:stations, :nb] - prod[stations:, nb:]
+            prod_im = prod[:stations, nb:] + prod[stations:, :nb]
+            next_re = weight_re + 0.5 * (steer_re - prod_re - load * weight_re) / diag_total
+            next_im = weight_im + 0.5 * (steer_im - prod_im - load * weight_im) / diag_total
+            weight_re, weight_im = (next_re, next_im)
+        half_re = weight_re.astype(jnp.bfloat16)
+        half_im = weight_im.astype(jnp.bfloat16)
+        lhs = jnp.concatenate(
+            [jnp.concatenate([half_re, -half_im], axis=1), jnp.concatenate([half_im, half_re], axis=1)],
+            axis=0,
         )
-        half_re = weight_re[0].astype(jnp.bfloat16)
-        half_im = weight_im[0].astype(jnp.bfloat16)
-        beam_re = bdot(half_re, spec_re) + bdot(half_im, spec_im)
-        beam_im = bdot(half_re, spec_im) - bdot(half_im, spec_re)
-        beam = (jnp.stack([beam_re, beam_im]) * factor).astype(jnp.bfloat16)
-        nb = beam.shape[1]
+        beam = jnp.dot(lhs.T, spec, preferred_element_type=jnp.float32)
+        beam = (beam * factor).astype(jnp.bfloat16)
         bc = nb // nst
         out = beam.reshape(2, nst, bc, nblk, nt).transpose(3, 1, 0, 2, 4).reshape(ndev, 2, bc, nt)
         got.append(lax.all_to_all(out, AXES, split_axis=0, concat_axis=0, tiled=True))

time: 534 us -> 492 us (0.921)
  matrix products: 180 us -> 58.8 us
  blocking collectives: 75.6 us -> 180 us
  other arithmetic: 84 us -> 108 us
  starting transfers between devices: 31.6 us -> 12.2 us
  local copies, waits for them, and re-layouts: 91.8 us -> 75.2 us
  waiting for transfers between devices: 58.4 us -> 47.6 us
    dot_general x64 -> x16, matrix products: 160 us -> 38.7 us  [the longest x8 18.8 us: local(): prod = jnp.dot(rows, both, precision=hi)]
    all_to_all x1 -> x3, blocking collectives: 57.2 us -> 162 us  [local(): lax.all_to_all(send[c], AXES, split_axis=0, concat_axis=0, tiled=True)]
    all_to_all x3 -> x1, waiting for transfers between devices: 44.3 us -> 21.4 us  [local(): lax.all_to_all(send[c], AXES, split_axis=0, concat_axis=0, tiled=True)]
    another operation x16 -> x0, local copies, waits for them, and re-layouts: 20.9 us -> none  [local(): beam = (jnp.stack([beam_re, beam_im]) * factor).astype(jnp.bfloat16)]
    all_to_all x3, waiting for transfers between devices: 14.1 us -> 26.2 us  [local(): lax.all_to_all(out, AXES, split_axis=0, concat_axis=0, tiled=True)]
    all_to_all x3, starting transfers between devices: 18.2 us -> 8.54 us  [local(): lax.all_to_all(out, AXES, split_axis=0, concat_axis=0, tiled=True)]
    all_to_all x3 -> x1, starting transfers between devices: 13.3 us -> 3.65 us  [local(): lax.all_to_all(send[c], AXES, split_axis=0, concat_axis=0, tiled=True)]
    add x0 -> x3, other arithmetic: none -> 8.86 us  [local(): weight_im + 0.5 * (steer_im - prod_im - load * weight_im) / diag_total]
  transfers between devices with their start and end apart: 6 -> 4, of which waited for: 2 -> 4; matrix products, arithmetic and copies ran while one was open for 32% -> 10% of each run, Pallas kernels for 0% -> 0%
where the time goes in v4:
time: 492 us; the launch traced here: 485 us
  blocking collectives  180 us (37%)
  other arithmetic  108 us (22%)
  local copies, waits for them, and re-layouts  75.2 us (15%)
  matrix products  58.8 us (12%)
  waiting for transfers between devices  47.6 us (10%)
  starting transfers between devices  12.2 us (2%)
    all_to_all x3, blocking collectives, local(): lax.all_to_all(send[c], AXES, split_axis=0, concat_axis=0, tiled=True)  162 us
    convert_element_type x1, other arithmetic, polyphase(): return (filtered * row_gain[None, :, None, None]).astype(jnp.bfloat16)  71.8 us
    another operation x4, local copies, waits for them, and re-layouts, transform(): return jnp.stack([out_re, out_im]).astype(jnp.bfloat16)  27.4 us
    all_to_all x3, waiting for transfers between devices, local(): lax.all_to_all(out, AXES, split_axis=0, concat_axis=0, tiled=True)  26.2 us
    all_to_all x1, waiting for transfers between devices, local(): lax.all_to_all(send[c], AXES, split_axis=0, concat_axis=0, tiled=True)  21.4 us
    dot_general x4, matrix products, transform(): jnp.einsum('stc,ck->stk', a, b, preferred_element_type=jnp.float32)  20.1 us
    dot_general x8, matrix products, local(): prod = jnp.dot(rows, both, precision=hi)  18.8 us
    all_to_all x1, blocking collectives, local(): lax.all_to_all(out, AXES, split_axis=0, concat_axis=0, tiled=True)  18.3 us
  transfers between devices with their start and end apart: 4, of which 4 were waited for; matrix products, arithmetic and copies ran while one was open for 10% of the time, Pallas kernels for 0%

profile of v4, /device:TPU:0, one launch (start us, length us, event | category | flops | bytes accessed | tf_op | source)
XLA Modules:
  0.0 484.8 jit_solution(10691688567517130561)
XLA Ops:
  1.0 14.9 %reshape.101 = f32[2,64,267,128]{3,2,1,0:T(8,128)} reshape(bf16[2,1,64,34176]{3,2,1,0:T(8,128)(2,1)} %param.5) | data formatting | bytes 26247168 | tf_op jit(solution)/shard_map/convert_element_type | solution.py:26
  15.9 71.8 %fusion.2 = bf16[2,64,256,128]{3,2,1,0:T(8,128)(2,1)} fusion(f32[2,64,267,128]{3,2,1,0:T(8,128)} %reshape.101, f32[64]{0:T(128)S(1)} %bitcast_multiply_fusion, f32[128]{0:T(128)S(1)} %get-tuple-element.75, f32[128]{0:T(128)S(1)} %get-tuple-element.76, f32[128]{0:T(128)S(1)} %get-tuple-element.66, f32[128]{0:T(128)S(1)} %get-tuple-element.67, ...), kind=kLoop, calls=%fused_computation.3 | loop fusion | flops 104857600 | bytes 209721600 | tf_op jit(solution)/shard_map/convert_element_type | solution.py:34
  87.8 3.8 fusion.14
  92.4 4.7 fusion.13
  97.1 3.4 add_convert_fusion
  100.6 7.3 %stack.24 = bf16[1,64,256,32,4]{2,4,3,1,0:T(4,128)(2,1)} reshape(bf16[64,256,128]{1,2,0:T(8,128)(2,1)} %add_convert_fusion) | data formatting | bytes 8388608 | tf_op jit(solution)/shard_map/stack | solution.py:43
  107.9 6.5 %copy.11 = bf16[1,64,256,32,4]{2,1,0,3,4:T(8,128)(2,1)} copy(bf16[1,64,256,32,4]{2,4,3,1,0:T(4,128)(2,1)} %stack.24) | data formatting | bytes 8388608 | tf_op jit(solution)/shard_map/stack | solution.py:43
  114.5 8.1 %subtract_convert_fusion = bf16[64,256,128]{1,2,0:T(8,128)(2,1)} fusion(f32[64,256,128]{1,2,0:T(8,128)} %fusion.13, bf16[2,64,256,128]{3,2,1,0:T(8,128)(2,1)} %fusion.2), kind=kOutput, calls=%fused_computation.26 | convolution fusion | flops 541327360 | bytes 16777216 | tf_op jit(solution)/shard_map/stc,ck->stk/dot_general | solution.py:40
  122.5 6.9 %stack.25 = bf16[1,64,256,32,4]{2,4,3,1,0:T(4,128)(2,1)} reshape(bf16[64,256,128]{1,2,0:T(8,128)(2,1)} %subtract_convert_fusion) | data formatting | bytes 8388608 | tf_op jit(solution)/shard_map/stack | solution.py:43
  129.4 6.7 %copy.12 = bf16[1,64,256,32,4]{2,1,0,3,4:T(8,128)(2,1)} copy(bf16[1,64,256,32,4]{2,4,3,1,0:T(4,128)(2,1)} %stack.25) | data formatting | bytes 8388608 | tf_op jit(solution)/shard_map/stack | solution.py:43
  136.1 6.3 %maximum_bitcast_fusion = bf16[4,32,2,64,256]{4,3,2,1,0:T(8,128)(2,1)} fusion(bf16[1,64,256,32,4]{2,1,0,3,4:T(8,128)(2,1)} %copy.12, bf16[1,64,256,32,4]{2,1,0,3,4:T(8,128)(2,1)S(1)} %copy-done.1), kind=kLoop, calls=%fused_computation.25 | loop fusion | flops 4194304 | bytes 16777216 | tf_op jit(solution)/shard_map/transpose | solution.py:74
  142.4 5.0 %slice_bitcast_fusion.13 = (bf16[32,2,64,256]{3,2,1,0:T(8,128)(2,1)S(1)}, bf16[32,2,64,256]{3,2,1,0:T(8,128)(2,1)S(1)}, bf16[32,2,64,256]{3,2,1,0:T(8,128)(2,1)}, bf16[32,2,64,256]{3,2,1,0:T(8,128)(2,1)S(1)}) fusion(bf16[4,32,2,64,256]{4,3,2,1,0:T(8,128)(2,1)} %maximum_bitcast_fusion), kind=kLoop, calls=%fused_computation.37 | loop fusion | bytes 16777216 | tf_op jit(solution)/shard_map/squeeze | solution.py:81
  147.4 57.3 %all_to_all.40 = bf16[32,2,64,256]{3,2,1,0:T(8,128)(2,1)} all-to-all(bf16[32,2,64,256]{3,2,1,0:T(8,128)(2,1)S(1)} %get-tuple-element.28), channel_id=1, replica_groups=mesh['blk'=4,'st'=8] {'blk','st'}, dimensions={0} | all-to-all | bytes 4194304 | tf_op jit(solution)/shard_map/all_to_all | solution.py:81
  204.7 52.1 %all_to_all.41 = bf16[32,2,64,256]{3,2,1,0:T(8,128)(2,1)S(1)} all-to-all(bf16[32,2,64,256]{3,2,1,0:T(8,128)(2,1)S(1)} %get-tuple-element.26), channel_id=1, replica_groups=mesh['blk'=4,'st'=8] {'blk','st'}, dimensions={0} | all-to-all | bytes 4194304 | tf_op jit(solution)/shard_map/all_to_all | solution.py:81
  256.8 52.6 %all_to_all.42 = bf16[32,2,64,256]{3,2,1,0:T(8,128)(2,1)} all-to-all(bf16[32,2,64,256]{3,2,1,0:T(8,128)(2,1)S(1)} %get-tuple-element.25), channel_id=1, replica_groups=mesh['blk'=4,'st'=8] {'blk','st'}, dimensions={0} | all-to-all | bytes 4194304 | tf_op jit(solution)/shard_map/all_to_all | solution.py:81
  309.4 3.7 all-to-all-start.4
  313.2 3.4 copy.16
  320.7 2.4 fusion.266
  324.7 4.6 fusion.268
  329.3 2.2 fusion.47
  332.1 3.4 copy.13
  336.0 2.6 fusion.265
  338.6 2.4 fusion.41
  341.5 21.4 %all-to-all-done.4 = bf16[32,2,64,256]{3,2,1,0:T(8,128)(2,1)} async-done(((bf16[32,2,64,256]{3,2,1,0:T(8,128)(2,1)}), bf16[32,2,64,256]{3,2,1,0:T(8,128)(2,1)}, u32[]{:S(2)}, u32[]{:S(2)}) %all-to-all-start.4) | async-done | bytes 2097184 | tf_op jit(solution)/shard_map/all_to_all | solution.py:81
  362.9 3.4 copy.19
  366.8 2.4 fusion.267
  369.2 2.4 fusion.45
  372.3 2.6 broadcast_divide_fusion.7
  374.9 3.6 fusion.20
  378.5 2.0 fusion.24
  380.5 5.2 %fusion.187 = (f32[512,128]{0,1:T(8,128)S(1)}, f32[512,128]{0,1:T(8,128)S(1)}, f32[512,128]{0,1:T(8,128)S(1)}, f32[512,128]{0,1:T(8,128)S(1)}, f32[512,128]{0,1:...) fusion(f32[1024,256]{0,1:T(8,128)S(1)} %fusion.24, f32[]{:T(128)S(6)} %add.243, ...), kind=kLoop, calls=%fused_computation.253 | loop fusion | flops 6029312 | bytes 4464664 | tf_op jit(solution)/shard_map/add | solution.py:109
  389.8 2.0 fusion.18
  391.9 2.4 fusion.127
  394.4 2.0 fusion.17
  396.4 3.8 fusion.253
  404.1 2.6 all-to-all-start.1
  406.7 3.0 fusion.22
  411.0 2.0 fusion.21
  414.1 3.7 fusion.195
  419.9 3.2 all-to-all-done.1
  423.1 3.3 all-to-all-start.3
  426.5 3.3 fusion.27
  432.0 10.7 %all-to-all-done.3 = bf16[32,2,16,256]{3,2,1,0:T(8,128)(2,1)} async-done(((bf16[32,2,16,256]{3,2,1,0:T(8,128)(2,1)}), bf16[32,2,16,256]{3,2,1,0:T(8,128)(2,1)}, u32[]{:S(2)}, u32[]{:S(2)}) %all-to-all-start.3) | async-done | bytes 524320 | tf_op jit(solution)/shard_map/all_to_all | solution.py:121
  442.8 2.6 all-to-all-start.5
  445.4 2.5 fusion.28
  449.4 12.3 %all-to-all-done.5 = bf16[32,2,16,256]{3,2,1,0:T(8,128)(2,1)S(1)} async-done(((bf16[32,2,16,256]{3,2,1,0:T(8,128)(2,1)}), bf16[32,2,16,256]{3,2,1,0:T(8,128)(2,1)S(1)}, u32[]{:S(2)}, u32[]{:S(2)}) %all-to-all-start.5) | async-done | bytes 524320 | tf_op jit(solution)/shard_map/all_to_all | solution.py:121
  461.7 18.3 %all_to_all.43 = bf16[32,2,16,256]{3,2,1,0:T(8,128)(2,1)S(1)} all-to-all(bf16[32,2,16,256]{3,2,1,0:T(8,128)(2,1)S(1)} %bitcast.129), channel_id=1, replica_groups=mesh['blk'=4,'st'=8] {'blk','st'}, dimensions={0} | all-to-all | bytes 1048576 | tf_op jit(solution)/shard_map/all_to_all | solution.py:121
  481.6 2.9 copy.25
  (83 shorter events, 25.9 us)
Async XLA Ops:
  1.0 14.9 %copy-start.26 = (f32[64]{0:T(128)S(1)}, f32[64]{0:T(128)}, u32[]{:S(2)}) copy-start(f32[64]{0:T(128)} %param.7) | copy-start | bytes 772
  1.0 14.9 %copy-start.27 = (s32[1,64]{1,0:T(1,128)S(1)}, s32[1,64]{1,0:T(1,128)}, u32[]{:S(2)}) copy-start(s32[1,64]{1,0:T(1,128)} %param.8) | copy-start | bytes 772
  87.8 4.6 copy-start
  129.4 6.7 %copy-start.1 = (bf16[1,64,256,32,4]{2,1,0,3,4:T(8,128)(2,1)S(1)}, bf16[1,64,256,32,4]{2,1,0,3,4:T(8,128)(2,1)}, u32[]{:S(2)}) copy-start(bf16[1,64,256,32,4]{2,1,0,3,4:T(8,128)(2,1)} %copy.11) | copy-start | bytes 12582916
  256.8 56.3 %copy-start.22 = (s32[512,128]{1,0:T(8,128)S(1)}, s32[512,128]{1,0:T(8,128)}, u32[]{:S(2)}) copy-start(s32[512,128]{1,0:T(8,128)} %param.9) | copy-start | bytes 786436
  309.4 53.6 %all-to-all-start.4 = ((bf16[32,2,64,256]{3,2,1,0:T(8,128)(2,1)}), bf16[32,2,64,256]{3,2,1,0:T(8,128)(2,1)}, u32[]{:S(2)}, u32[]{:S(2)}) async-start(bf16[32,2,64,256]{3,2,1,0:T(8,128)(2,1)} %get-tuple-element.27), calls=%async_computation.4 | async-start | bytes 4194304 | tf_op jit(solution)/shard_map/all_to_all | solution.py:81
  317.1 3.6 copy-start.16
  335.9 2.6 copy-start.19
  366.8 2.4 copy-start.18
  372.2 6.3 %copy-start.3 = (f32[512,512]{1,0:T(8,128)S(1)}, f32[512,512]{1,0:T(8,128)}, u32[]{:S(2)}) copy-start(f32[512,512]{1,0:T(8,128)} %get-tuple-element.15) | copy-start | bytes 3145732
  372.2 6.3 %copy-start.4 = (f32[512,512]{1,0:T(8,128)S(1)}, f32[512,512]{1,0:T(8,128)}, u32[]{:S(2)}) copy-start(f32[512,512]{1,0:T(8,128)} %get-tuple-element.29) | copy-start | bytes 3145732
  378.4 7.3 %copy-start.5 = (f32[512,512]{1,0:T(8,128)S(1)}, f32[512,512]{1,0:T(8,128)}, u32[]{:S(2)}) copy-start(f32[512,512]{1,0:T(8,128)} %get-tuple-element.21) | copy-start | bytes 3145732
  378.5 7.3 %copy-start.6 = (f32[512,512]{1,0:T(8,128)S(1)}, f32[512,512]{1,0:T(8,128)}, u32[]{:S(2)}) copy-start(f32[512,512]{1,0:T(8,128)} %get-tuple-element.31) | copy-start | bytes 3145732
  385.7 6.2 %copy-start.11 = (f32[512,128]{0,1:T(8,128)}, f32[512,128]{0,1:T(8,128)S(1)}, u32[]{:S(2)}) copy-start(f32[512,128]{0,1:T(8,128)S(1)} %get-tuple-element.54) | copy-start | bytes 786436
  385.7 4.1 copy-start.2
  387.8 8.6 %copy-start.7 = (f32[1024,256]{0,1:T(8,128)}, f32[1024,256]{0,1:T(8,128)S(1)}, u32[]{:S(2)}) copy-start(f32[1024,256]{0,1:T(8,128)S(1)} %fusion.19) | copy-start | bytes 3145732
  394.3 5.9 %copy-start.13 = (f32[512,128]{0,1:T(8,128)}, f32[512,128]{0,1:T(8,128)S(1)}, u32[]{:S(2)}) copy-start(f32[512,128]{0,1:T(8,128)S(1)} %get-tuple-element.40) | copy-start | bytes 786436
  394.3 5.9 %copy-start.20 = (bf16[128,8,4,256]{3,1,2,0:T(8,128)(2,1)S(1)}, bf16[128,8,4,256]{3,1,2,0:T(8,128)(2,1)}, u32[]{:S(2)}) copy-start(bf16[128,8,4,256]{3,1,2,0:T(8,128)(2,1)} %copy-done.19) | copy-start | bytes 6291460
  396.4 3.8 copy-start.9
  400.2 6.5 %copy-start.21 = (f32[512,128]{0,1:T(8,128)S(1)}, f32[512,128]{0,1:T(8,128)}, u32[]{:S(2)}) copy-start(f32[512,128]{0,1:T(8,128)} %get-tuple-element.58) | copy-start | bytes 786436
  404.1 19.0 %all-to-all-start.1 = ((bf16[32,2,16,256]{3,2,1,0:T(8,128)(2,1)}), bf16[32,2,16,256]{3,2,1,0:T(8,128)(2,1)S(1)}, u32[]{:S(2)}, u32[]{:S(2)}) async-start(bf16[32,2,16,256]{3,2,1,0:T(8,128)(2,1)} %bitcast.22), calls=%async_computation.1 | async-start | bytes 1048576 | tf_op jit(solution)/shard_map/all_to_all | solution.py:121
  409.7 4.4 copy-start.8
  409.7 4.4 copy-start.10
  409.7 4.4 copy-start.12
  409.7 4.4 copy-start.14
  411.0 6.9 %copy-start.17 = (bf16[128,8,4,256]{3,1,2,0:T(8,128)(2,1)S(1)}, bf16[128,8,4,256]{3,1,2,0:T(8,128)(2,1)}, u32[]{:S(2)}) copy-start(bf16[128,8,4,256]{3,1,2,0:T(8,128)(2,1)} %copy-done.16) | copy-start | bytes 6291460
  417.9 8.6 %copy-start.24 = (bf16[512,128]{0,1:T(8,128)(2,1)S(1)}, bf16[512,128]{0,1:T(8,128)(2,1)}, u32[]{:S(2)}) copy-start(bf16[512,128]{0,1:T(8,128)(2,1)} %get-tuple-element.51) | copy-start | bytes 393220
  417.9 8.6 %copy-start.25 = (bf16[512,128]{0,1:T(8,128)(2,1)S(1)}, bf16[512,128]{0,1:T(8,128)(2,1)}, u32[]{:S(2)}) copy-start(bf16[512,128]{0,1:T(8,128)(2,1)} %get-tuple-element.52) | copy-start | bytes 393220
  423.1 19.7 %all-to-all-start.3 = ((bf16[32,2,16,256]{3,2,1,0:T(8,128)(2,1)}), bf16[32,2,16,256]{3,2,1,0:T(8,128)(2,1)}, u32[]{:S(2)}, u32[]{:S(2)}) async-start(bf16[32,2,16,256]{3,2,1,0:T(8,128)(2,1)} %bitcast.28), calls=%async_computation.3 | async-start | bytes 1048576 | tf_op jit(solution)/shard_map/all_to_all | solution.py:121
  426.4 18.9 %copy-start.15 = (bf16[128,8,4,256]{3,1,2,0:T(8,128)(2,1)S(1)}, bf16[128,8,4,256]{3,1,2,0:T(8,128)(2,1)}, u32[]{:S(2)}) copy-start(bf16[128,8,4,256]{3,1,2,0:T(8,128)(2,1)} %copy.29) | copy-start | bytes 6291460
  426.4 18.9 %copy-start.23 = (bf16[512,128]{0,1:T(8,128)(2,1)S(1)}, bf16[512,128]{0,1:T(8,128)(2,1)}, u32[]{:S(2)}) copy-start(bf16[512,128]{0,1:T(8,128)(2,1)} %get-tuple-element.50) | copy-start | bytes 393220
  442.8 19.0 %all-to-all-start.5 = ((bf16[32,2,16,256]{3,2,1,0:T(8,128)(2,1)}), bf16[32,2,16,256]{3,2,1,0:T(8,128)(2,1)S(1)}, u32[]{:S(2)}, u32[]{:S(2)}) async-start(bf16[32,2,16,256]{3,2,1,0:T(8,128)(2,1)} %bitcast.34), calls=%async_computation.5 | async-start | bytes 1048576 | tf_op jit(solution)/shard_map/all_to_all | solution.py:121

commit v5 on v4

--- a/solution.py
+++ b/solution.py
@@ -63,24 +63,33 @@
     nblk = lax.axis_size("blk")
     nst = lax.axis_size("st")
     ndev = nblk * nst
-    cos_table, sin_table = dft_tables(filter_coeffs.shape[1])
+    ntaps, nk = filter_coeffs.shape
+    cos_table, sin_table = dft_tables(nk)
     row_gain = station_gain * flags[0].astype(jnp.float32)
-    filtered = polyphase(voltages[:, 0], filter_coeffs, row_gain)
-    local_spec = transform(filtered, cos_table, sin_table)
-    _, ls, nt, nk = local_spec.shape
+    samples = voltages[:, 0]
+    ls = samples.shape[1]
+    nt = samples.shape[2] // nk - ntaps + 1
     kc = nk // ndev
     stations = nst * ls
     counted = nblk * nt
-    send = local_spec.reshape(2, ls, nt, ndev, kc).transpose(4, 3, 0, 1, 2)
+    ngr = 4 if ls % 64 == 0 else 1
+    gs = ls // ngr
     me = lax.axis_index("blk") * nst + lax.axis_index("st")
     eye = jnp.eye(stations, dtype=jnp.float32)
     factor = 1.0 / math.sqrt(stations)
+    arrived = []
+    for g in range(ngr):
+        part = samples[:, g * gs : (g + 1) * gs]
+        filtered = polyphase(part, filter_coeffs, row_gain[g * gs : (g + 1) * gs])
+        local_spec = transform(filtered, cos_table, sin_table)
+        send = local_spec.reshape(2, gs, nt, ndev, kc).transpose(3, 4, 0, 1, 2)
+        arrived.append(lax.all_to_all(send, AXES, split_axis=0, concat_axis=0, tiled=True))
+    recv_all = jnp.stack(arrived, axis=3).reshape(nblk, nst, kc, 2, ngr, gs, nt)
     hi = lax.Precision.HIGHEST
     got = []
     for c in range(kc):
-        recv = lax.all_to_all(send[c], AXES, split_axis=0, concat_axis=0, tiled=True)
-        recv = recv.reshape(nblk, nst, 2, ls, nt)
-        spec = recv.transpose(2, 1, 3, 0, 4).reshape(2 * stations, counted)
+        recv = recv_all[:, :, c]
+        spec = recv.transpose(2, 1, 3, 4, 0, 5).reshape(2 * stations, counted)
         gram = jnp.dot(spec, spec.T, preferred_element_type=jnp.float32)
         g00 = gram[:stations, :stations]
         g01 = gram[:stations, stations:]

time: 492 us -> 434 us (0.88)
  blocking collectives: 180 us -> 18.3 us
  waiting for transfers between devices: 47.6 us -> 107 us
  other arithmetic: 108 us -> 138 us
  starting transfers between devices: 12.2 us -> 26.6 us
    all_to_all x3 -> x0, blocking collectives: 162 us -> none  [local(): lax.all_to_all(send[c], AXES, split_axis=0, concat_axis=0, tiled=True)]
    all_to_all x1 -> x4, waiting for transfers between devices: 21.4 us -> 81.2 us  [local(): lax.all_to_all(send, AXES, split_axis=0, concat_axis=0, tiled=True)]
    transpose x0 -> x5, local copies, waits for them, and re-layouts: none -> 18.2 us  [local(): spec = recv.transpose(2, 1, 3, 4, 0, 5).reshape(2 * stations, counted)]
    another operation x4 -> x8, local copies, waits for them, and re-layouts: 27.4 us -> 10.7 us  [transform(): return jnp.stack([out_re, out_im]).astype(jnp.bfloat16)]
    convert_element_type x1 -> x4, other arithmetic: 71.8 us -> 86.9 us  [polyphase(): return (filtered * row_gain[None, :, None, None]).astype(jnp.bfloat16)]
    convert_element_type x1 -> x0, local copies, waits for them, and re-layouts: 14.9 us -> none  [polyphase(): grid = samples.astype(jnp.float32).reshape(2, samples.shape[1], -1, width)]
    all_to_all x1 -> x4, starting transfers between devices: 3.65 us -> 18 us  [local(): lax.all_to_all(send, AXES, split_axis=0, concat_axis=0, tiled=True)]
    all_to_all x0 -> x4, local copies, waits for them, and re-layouts: none -> 10.4 us  [local(): lax.all_to_all(send, AXES, split_axis=0, concat_axis=0, tiled=True)]
  transfers between devices with their start and end apart: 4 -> 7, of which waited for: 4 -> 7; matrix products, arithmetic and copies ran while one was open for 10% -> 33% of each run, Pallas kernels for 0% -> 0%
where the time goes in v5:
time: 434 us; the launch traced here: 427 us
  other arithmetic  138 us (32%)
  waiting for transfers between devices  107 us (25%)
  local copies, waits for them, and re-layouts  75.2 us (17%)
  matrix products  57.3 us (13%)
  starting transfers between devices  26.6 us (6%)
  blocking collectives  18.3 us (4%)
    convert_element_type x4, other arithmetic, polyphase(): return (filtered * row_gain[None, :, None, None]).astype(jnp.bfloat16)  86.9 us
    all_to_all x4, waiting for transfers between devices, local(): lax.all_to_all(send, AXES, split_axis=0, concat_axis=0, tiled=True)  81.2 us
    all_to_all x3, waiting for transfers between devices, local(): lax.all_to_all(out, AXES, split_axis=0, concat_axis=0, tiled=True)  26.2 us
    dot_general x16, matrix products, transform(): jnp.einsum('stc,ck->stk', a, b, preferred_element_type=jnp.float32)  21.1 us
    reshape x4, local copies, waits for them, and re-layouts, polyphase(): grid = samples.astype(jnp.float32).reshape(2, samples.shape[1], -1, width)  20.2 us
    dot_general x8, matrix products, local(): prod = jnp.dot(rows, both, precision=hi)  18.8 us
    all_to_all x1, blocking collectives, local(): lax.all_to_all(out, AXES, split_axis=0, concat_axis=0, tiled=True)  18.3 us
    transpose x5, local copies, waits for them, and re-layouts, local(): spec = recv.transpose(2, 1, 3, 4, 0, 5).reshape(2 * stations, counted)  18.2 us
  transfers between devices with their start and end apart: 7, of which 7 were waited for; matrix products, arithmetic and copies ran while one was open for 33% of the time, Pallas kernels for 0%

profile of v5, /device:TPU:0, one launch (start us, length us, event | category | flops | bytes accessed | tf_op | source)
XLA Modules:
  0.0 426.6 jit_solution(6340207534801421521)
XLA Ops:
  1.0 9.9 %slice_convert_fusion.3 = (f32[2,16,34176]{2,1,0:T(8,128)}, f32[2,16,34176]{2,1,0:T(8,128)}, f32[2,16,34176]{2,1,0:T(8,128)}, f32[2,16,34176]{2,1,0:T(8,128)}) fusion(bf16[2,64,34176]{2,1,0:T(8,128)(2,1)} %bitcast.166), kind=kLoop, calls=%fused_computation.104 | loop fusion | flops 4374528 | bytes 26247168 | tf_op jit(solution)/shard_map/reshape | solution.py:26
  10.9 5.1 %reshape.147 = f32[2,16,267,128]{3,2,1,0:T(8,128)} reshape(f32[2,16,34176]{2,1,0:T(8,128)} %get-tuple-element.25) | data formatting | bytes 8749056 | tf_op jit(solution)/shard_map/reshape | solution.py:26
  16.0 21.7 %fusion.41 = bf16[2,16,256,128]{3,2,1,0:T(8,128)(2,1)S(1)} fusion(f32[2,16,267,128]{3,2,1,0:T(8,128)} %reshape.147, f32[16]{0:T(128)S(1)} %get-tuple-element.81, f32[128]{0:T(128)S(1)} %get-tuple-element.79, f32[128]{0:T(128)S(1)} %get-tuple-element.80, f32[128]{0:T(128)S(1)} %get-tuple-element.70, f32[128]{0:T(128)S(1)} %get-tuple-element.71, ...), kind=kLoop, calls=%fused_computation.79 | loop fusion | flops 26214400 | bytes 52435008 | tf_op jit(solution)/shard_map/convert_element_type | solution.py:34
  43.4 3.2 subtract_convert_fusion.3
  50.2 7.6 %all-to-all-start = ((bf16[32,4,2,16,256]{4,1,3,2,0:T(4,128)(2,1)}), bf16[32,4,2,16,256]{4,1,3,2,0:T(4,128)(2,1)}, u32[]{:S(2)}, u32[]{:S(2)}) async-start(bf16[32,4,2,16,256]{4,1,3,2,0:T(4,128)(2,1)} %copy_bitcast_fusion.3), calls=%async_computation | async-start | bytes 4194304 | tf_op jit(solution)/shard_map/all_to_all | solution.py:86
  57.9 5.0 %reshape.149 = f32[2,16,267,128]{3,2,1,0:T(8,128)} reshape(f32[2,16,34176]{2,1,0:T(8,128)} %get-tuple-element.28) | data formatting | bytes 8749056 | tf_op jit(solution)/shard_map/reshape | solution.py:26
  62.9 21.7 %fusion.28 = bf16[2,16,256,128]{3,2,1,0:T(8,128)(2,1)S(1)} fusion(f32[2,16,267,128]{3,2,1,0:T(8,128)} %reshape.149, f32[16]{0:T(128)S(1)} %get-tuple-element.84, f32[128]{0:T(128)S(1)} %get-tuple-element.79, f32[128]{0:T(128)S(1)} %get-tuple-element.80, f32[128]{0:T(128)S(1)} %get-tuple-element.70, f32[128]{0:T(128)S(1)} %get-tuple-element.71, ...), kind=kLoop, calls=%fused_computation.54 | loop fusion | flops 26214400 | bytes 52435008 | tf_op jit(solution)/shard_map/convert_element_type | solution.py:34
  94.1 13.8 %all-to-all-done = bf16[32,4,2,16,256]{4,1,3,2,0:T(4,128)(2,1)} async-done(((bf16[32,4,2,16,256]{4,1,3,2,0:T(4,128)(2,1)}), bf16[32,4,2,16,256]{4,1,3,2,0:T(4,128)(2,1)}, u32[]{:S(2)}, u32[]{:S(2)}) %all-to-all-start) | async-done | bytes 2097184 | tf_op jit(solution)/shard_map/all_to_all | solution.py:86
  107.9 3.7 all-to-all-start.1
  111.6 5.0 %reshape.151 = f32[2,16,267,128]{3,2,1,0:T(8,128)} reshape(f32[2,16,34176]{2,1,0:T(8,128)} %get-tuple-element.27) | data formatting | bytes 8749056 | tf_op jit(solution)/shard_map/reshape | solution.py:26
  116.7 21.7 %fusion.15 = bf16[2,16,256,128]{3,2,1,0:T(8,128)(2,1)S(1)} fusion(f32[2,16,267,128]{3,2,1,0:T(8,128)} %reshape.151, f32[16]{0:T(128)S(1)} %get-tuple-element.83, f32[128]{0:T(128)S(1)} %get-tuple-element.79, f32[128]{0:T(128)S(1)} %get-tuple-element.80, f32[128]{0:T(128)S(1)} %get-tuple-element.70, f32[128]{0:T(128)S(1)} %get-tuple-element.71, ...), kind=kLoop, calls=%fused_computation.29 | loop fusion | flops 26214400 | bytes 52435008 | tf_op jit(solution)/shard_map/convert_element_type | solution.py:34
  148.0 13.7 %all-to-all-done.1 = bf16[32,4,2,16,256]{4,1,3,2,0:T(4,128)(2,1)} async-done(((bf16[32,4,2,16,256]{4,1,3,2,0:T(4,128)(2,1)}), bf16[32,4,2,16,256]{4,1,3,2,0:T(4,128)(2,1)}, u32[]{:S(2)}, u32[]{:S(2)}) %all-to-all-start.1) | async-done | bytes 2097184 | tf_op jit(solution)/shard_map/all_to_all | solution.py:86
  161.7 3.9 all-to-all-start.2
  165.6 5.0 %reshape.153 = f32[2,16,267,128]{3,2,1,0:T(8,128)} reshape(f32[2,16,34176]{2,1,0:T(8,128)} %get-tuple-element.26) | data formatting | bytes 8749056 | tf_op jit(solution)/shard_map/reshape | solution.py:26
  170.7 21.7 %fusion.2 = bf16[2,16,256,128]{3,2,1,0:T(8,128)(2,1)S(1)} fusion(f32[2,16,267,128]{3,2,1,0:T(8,128)} %reshape.153, f32[16]{0:T(128)S(1)} %get-tuple-element.82, f32[128]{0:T(128)S(1)} %get-tuple-element.79, f32[128]{0:T(128)S(1)} %get-tuple-element.80, f32[128]{0:T(128)S(1)} %get-tuple-element.70, f32[128]{0:T(128)S(1)} %get-tuple-element.71, ...), kind=kLoop, calls=%fused_computation.4 | loop fusion | flops 26214400 | bytes 52435008 | tf_op jit(solution)/shard_map/convert_element_type | solution.py:34
  201.9 13.7 %all-to-all-done.2 = bf16[32,4,2,16,256]{4,1,3,2,0:T(4,128)(2,1)} async-done(((bf16[32,4,2,16,256]{4,1,3,2,0:T(4,128)(2,1)}), bf16[32,4,2,16,256]{4,1,3,2,0:T(4,128)(2,1)}, u32[]{:S(2)}, u32[]{:S(2)}) %all-to-all-start.2) | async-done | bytes 2097184 | tf_op jit(solution)/shard_map/all_to_all | solution.py:86
  215.7 2.7 all-to-all-start.3
  218.6 3.3 copy.31
  221.9 3.3 copy.34
  225.2 3.4 copy.37
  228.6 39.9 %all-to-all-done.3 = bf16[32,4,2,16,256]{4,1,3,2,0:T(4,128)(2,1)S(1)} async-done(((bf16[32,4,2,16,256]{4,1,3,2,0:T(4,128)(2,1)}), bf16[32,4,2,16,256]{4,1,3,2,0:T(4,128)(2,1)S(1)}, u32[]{:S(2)}, u32[]{:S(2)}) %all-to-all-start.3) | async-done | bytes 2097184 | tf_op jit(solution)/shard_map/all_to_all | solution.py:86
  270.7 2.9 pad_maximum_fusion
  273.7 2.9 slice_bitcast_fusion.3
  276.6 2.9 copy.44
  280.0 2.4 fusion.382
  283.4 2.9 copy.50
  286.9 2.4 fusion.384
  292.6 4.9 %copy.41 = bf16[2,8,4,16,4,256]{5,4,3,2,1,0:T(4,128)(2,1)S(1)} copy(bf16[2,8,4,16,4,256]{5,3,2,0,1,4:T(8,128)(2,1)} %get-tuple-element.29) | data formatting | bytes 4194304 | tf_op jit(solution)/shard_map/transpose | solution.py:92
  298.1 2.4 fusion.381
  300.4 2.4 fusion.76
  303.5 4.5 %copy.47 = bf16[2,8,4,16,4,256]{5,4,3,2,1,0:T(4,128)(2,1)S(1)} copy(bf16[2,8,4,16,4,256]{5,3,2,0,1,4:T(8,128)(2,1)} %get-tuple-element.31) | data formatting | bytes 4194304 | tf_op jit(solution)/shard_map/transpose | solution.py:92
  308.5 2.4 fusion.383
  310.9 2.5 fusion.80
  316.5 3.6 fusion.55
  322.1 5.2 %fusion.230 = (f32[512,128]{0,1:T(8,128)S(1)}, f32[512,128]{0,1:T(8,128)S(1)}, f32[512,128]{0,1:T(8,128)S(1)}, f32[512,128]{0,1:T(8,128)S(1)}, f32[512,128]{0,1:...) fusion(f32[1024,256]{0,1:T(8,128)S(1)} %fusion.59, f32[]{:T(128)S(6)} %add.411, ...), kind=kLoop, calls=%fused_computation.356 | loop fusion | flops 6029312 | bytes 4464664 | tf_op jit(solution)/shard_map/add | solution.py:118
  337.9 4.0 fusion.368
  345.8 2.6 all-to-all-start.4
  348.4 3.0 fusion.57
  355.8 3.7 fusion.238
  361.6 3.2 all-to-all-done.4
  364.8 3.3 all-to-all-start.5
  368.1 3.3 fusion.62
  373.7 10.7 %all-to-all-done.5 = bf16[32,2,16,256]{3,2,1,0:T(8,128)(2,1)} async-done(((bf16[32,2,16,256]{3,2,1,0:T(8,128)(2,1)}), bf16[32,2,16,256]{3,2,1,0:T(8,128)(2,1)}, u32[]{:S(2)}, u32[]{:S(2)}) %all-to-all-start.5) | async-done | bytes 524320 | tf_op jit(solution)/shard_map/all_to_all | solution.py:130
  384.4 2.6 all-to-all-start.6
  387.0 2.5 fusion.63
  391.1 12.3 %all-to-all-done.6 = bf16[32,2,16,256]{3,2,1,0:T(8,128)(2,1)S(1)} async-done(((bf16[32,2,16,256]{3,2,1,0:T(8,128)(2,1)}), bf16[32,2,16,256]{3,2,1,0:T(8,128)(2,1)S(1)}, u32[]{:S(2)}, u32[]{:S(2)}) %all-to-all-start.6) | async-done | bytes 524320 | tf_op jit(solution)/shard_map/all_to_all | solution.py:130
  403.4 18.3 %all_to_all.40 = bf16[32,2,16,256]{3,2,1,0:T(8,128)(2,1)S(1)} all-to-all(bf16[32,2,16,256]{3,2,1,0:T(8,128)(2,1)S(1)} %bitcast.184), channel_id=1, replica_groups=mesh['blk'=4,'st'=8] {'blk','st'}, dimensions={0} | all-to-all | bytes 1048576 | tf_op jit(solution)/shard_map/all_to_all | solution.py:130
  423.3 2.9 copy.53
  (120 shorter events, 76.7 us)
Async XLA Ops:
  10.9 5.1 %copy-start.27 = (f32[64]{0:T(128)S(1)}, f32[64]{0:T(128)}, u32[]{:S(2)}) copy-start(f32[64]{0:T(128)} %param.7) | copy-start | bytes 772
  10.9 5.1 %copy-start.28 = (s32[1,64]{1,0:T(1,128)S(1)}, s32[1,64]{1,0:T(1,128)}, u32[]{:S(2)}) copy-start(s32[1,64]{1,0:T(1,128)} %param.8) | copy-start | bytes 772
  50.2 57.7 %all-to-all-start = ((bf16[32,4,2,16,256]{4,1,3,2,0:T(4,128)(2,1)}), bf16[32,4,2,16,256]{4,1,3,2,0:T(4,128)(2,1)}, u32[]{:S(2)}, u32[]{:S(2)}) async-start(bf16[32,4,2,16,256]{4,1,3,2,0:T(4,128)(2,1)} %copy_bitcast_fusion.3), calls=%async_computation | async-start | bytes 4194304 | tf_op jit(solution)/shard_map/all_to_all | solution.py:86
  107.9 53.8 %all-to-all-start.1 = ((bf16[32,4,2,16,256]{4,1,3,2,0:T(4,128)(2,1)}), bf16[32,4,2,16,256]{4,1,3,2,0:T(4,128)(2,1)}, u32[]{:S(2)}, u32[]{:S(2)}) async-start(bf16[32,4,2,16,256]{4,1,3,2,0:T(4,128)(2,1)} %copy_bitcast_fusion.2), calls=%async_computation.1 | async-start | bytes 4194304 | tf_op jit(solution)/shard_map/all_to_all | solution.py:86
  161.7 54.0 %all-to-all-start.2 = ((bf16[32,4,2,16,256]{4,1,3,2,0:T(4,128)(2,1)}), bf16[32,4,2,16,256]{4,1,3,2,0:T(4,128)(2,1)}, u32[]{:S(2)}, u32[]{:S(2)}) async-start(bf16[32,4,2,16,256]{4,1,3,2,0:T(4,128)(2,1)} %copy_bitcast_fusion.1), calls=%async_computation.2 | async-start | bytes 4194304 | tf_op jit(solution)/shard_map/all_to_all | solution.py:86
  199.7 18.8 %copy-start.23 = (s32[512,128]{1,0:T(8,128)S(1)}, s32[512,128]{1,0:T(8,128)}, u32[]{:S(2)}) copy-start(s32[512,128]{1,0:T(8,128)} %param.9) | copy-start | bytes 786436
  215.7 52.8 %all-to-all-start.3 = ((bf16[32,4,2,16,256]{4,1,3,2,0:T(4,128)(2,1)}), bf16[32,4,2,16,256]{4,1,3,2,0:T(4,128)(2,1)S(1)}, u32[]{:S(2)}, u32[]{:S(2)}) async-start(bf16[32,4,2,16,256]{4,1,3,2,0:T(4,128)(2,1)} %copy_bitcast_fusion), calls=%async_computation.3 | async-start | bytes 4194304 | tf_op jit(solution)/shard_map/all_to_all | solution.py:86
  268.5 1.6 copy-start.5
  268.5 2.2 copy-start.6
  280.0 2.4 copy-start.17
  286.8 2.4 copy-start.15
  298.1 2.4 copy-start.20
  308.5 2.4 copy-start.19
  314.1 6.0 %copy-start.1 = (f32[512,512]{1,0:T(8,128)S(1)}, f32[512,512]{1,0:T(8,128)}, u32[]{:S(2)}) copy-start(f32[512,512]{1,0:T(8,128)} %get-tuple-element.15) | copy-start | bytes 3145732
  314.1 6.0 %copy-start.2 = (f32[512,512]{1,0:T(8,128)S(1)}, f32[512,512]{1,0:T(8,128)}, u32[]{:S(2)}) copy-start(f32[512,512]{1,0:T(8,128)} %get-tuple-element.33) | copy-start | bytes 3145732
  320.0 7.3 %copy-start.3 = (f32[512,512]{1,0:T(8,128)S(1)}, f32[512,512]{1,0:T(8,128)}, u32[]{:S(2)}) copy-start(f32[512,512]{1,0:T(8,128)} %get-tuple-element.21) | copy-start | bytes 3145732
  320.0 7.3 %copy-start.4 = (f32[512,512]{1,0:T(8,128)S(1)}, f32[512,512]{1,0:T(8,128)}, u32[]{:S(2)}) copy-start(f32[512,512]{1,0:T(8,128)} %get-tuple-element.35) | copy-start | bytes 3145732
  327.3 6.2 %copy-start.11 = (f32[512,128]{0,1:T(8,128)}, f32[512,128]{0,1:T(8,128)S(1)}, u32[]{:S(2)}) copy-start(f32[512,128]{0,1:T(8,128)S(1)} %get-tuple-element.58) | copy-start | bytes 786436
  327.3 4.1 copy-start
  329.4 8.5 %copy-start.7 = (f32[1024,256]{0,1:T(8,128)}, f32[1024,256]{0,1:T(8,128)S(1)}, u32[]{:S(2)}) copy-start(f32[1024,256]{0,1:T(8,128)S(1)} %fusion.54) | copy-start | bytes 3145732
  335.8 6.1 %copy-start.13 = (f32[512,128]{0,1:T(8,128)}, f32[512,128]{0,1:T(8,128)S(1)}, u32[]{:S(2)}) copy-start(f32[512,128]{0,1:T(8,128)S(1)} %get-tuple-element.44) | copy-start | bytes 786436
  335.8 6.1 %copy-start.21 = (bf16[128,8,4,256]{3,1,2,0:T(8,128)(2,1)S(1)}, bf16[128,8,4,256]{3,1,2,0:T(8,128)(2,1)}, u32[]{:S(2)}) copy-start(bf16[128,8,4,256]{3,1,2,0:T(8,128)(2,1)} %copy-done.20) | copy-start | bytes 6291460
  337.8 4.0 copy-start.9
  341.9 6.5 %copy-start.22 = (f32[512,128]{0,1:T(8,128)S(1)}, f32[512,128]{0,1:T(8,128)}, u32[]{:S(2)}) copy-start(f32[512,128]{0,1:T(8,128)} %get-tuple-element.62) | copy-start | bytes 786436
  345.8 19.0 %all-to-all-start.4 = ((bf16[32,2,16,256]{3,2,1,0:T(8,128)(2,1)}), bf16[32,2,16,256]{3,2,1,0:T(8,128)(2,1)S(1)}, u32[]{:S(2)}, u32[]{:S(2)}) async-start(bf16[32,2,16,256]{3,2,1,0:T(8,128)(2,1)} %bitcast.35), calls=%async_computation.4 | async-start | bytes 1048576 | tf_op jit(solution)/shard_map/all_to_all | solution.py:130
  351.4 4.4 %copy-start.8 = (f32[1024,256]{0,1:T(8,128)S(1)}, f32[1024,256]{0,1:T(8,128)}, u32[]{:S(2)}) copy-start(f32[1024,256]{0,1:T(8,128)} %copy-done.7) | copy-start | bytes 3145732
  351.4 4.4 %copy-start.10 = (f32[1024,256]{0,1:T(8,128)S(1)}, f32[1024,256]{0,1:T(8,128)}, u32[]{:S(2)}) copy-start(f32[1024,256]{0,1:T(8,128)} %copy-done.9) | copy-start | bytes 3145732
  351.4 4.4 %copy-start.12 = (f32[512,128]{0,1:T(8,128)S(1)}, f32[512,128]{0,1:T(8,128)}, u32[]{:S(2)}) copy-start(f32[512,128]{0,1:T(8,128)} %copy-done.11) | copy-start | bytes 786436
  351.4 4.4 %copy-start.14 = (f32[512,128]{0,1:T(8,128)S(1)}, f32[512,128]{0,1:T(8,128)}, u32[]{:S(2)}) copy-start(f32[512,128]{0,1:T(8,128)} %copy-done.13) | copy-start | bytes 786436
  352.7 6.9 %copy-start.18 = (bf16[128,8,4,256]{3,1,2,0:T(8,128)(2,1)S(1)}, bf16[128,8,4,256]{3,1,2,0:T(8,128)(2,1)}, u32[]{:S(2)}) copy-start(bf16[128,8,4,256]{3,1,2,0:T(8,128)(2,1)} %copy-done.17) | copy-start | bytes 6291460
  359.5 8.6 %copy-start.25 = (bf16[512,128]{0,1:T(8,128)(2,1)S(1)}, bf16[512,128]{0,1:T(8,128)(2,1)}, u32[]{:S(2)}) copy-start(bf16[512,128]{0,1:T(8,128)(2,1)} %get-tuple-element.55) | copy-start | bytes 393220
  359.5 8.6 %copy-start.26 = (bf16[512,128]{0,1:T(8,128)(2,1)S(1)}, bf16[512,128]{0,1:T(8,128)(2,1)}, u32[]{:S(2)}) copy-start(bf16[512,128]{0,1:T(8,128)(2,1)} %get-tuple-element.56) | copy-start | bytes 393220
  364.8 19.7 %all-to-all-start.5 = ((bf16[32,2,16,256]{3,2,1,0:T(8,128)(2,1)}), bf16[32,2,16,256]{3,2,1,0:T(8,128)(2,1)}, u32[]{:S(2)}, u32[]{:S(2)}) async-start(bf16[32,2,16,256]{3,2,1,0:T(8,128)(2,1)} %bitcast.40), calls=%async_computation.5 | async-start | bytes 1048576 | tf_op jit(solution)/shard_map/all_to_all | solution.py:130
  368.1 18.9 %copy-start.16 = (bf16[128,8,4,256]{3,1,2,0:T(8,128)(2,1)S(1)}, bf16[128,8,4,256]{3,1,2,0:T(8,128)(2,1)}, u32[]{:S(2)}) copy-start(bf16[128,8,4,256]{3,1,2,0:T(8,128)(2,1)} %copy-done.15) | copy-start | bytes 6291460
  368.1 18.9 %copy-start.24 = (bf16[512,128]{0,1:T(8,128)(2,1)S(1)}, bf16[512,128]{0,1:T(8,128)(2,1)}, u32[]{:S(2)}) copy-start(bf16[512,128]{0,1:T(8,128)(2,1)} %get-tuple-element.54) | copy-start | bytes 393220
  384.4 19.0 %all-to-all-start.6 = ((bf16[32,2,16,256]{3,2,1,0:T(8,128)(2,1)}), bf16[32,2,16,256]{3,2,1,0:T(8,128)(2,1)S(1)}, u32[]{:S(2)}, u32[]{:S(2)}) async-start(bf16[32,2,16,256]{3,2,1,0:T(8,128)(2,1)} %bitcast.45), calls=%async_computation.6 | async-start | bytes 1048576 | tf_op jit(solution)/shard_map/all_to_all | solution.py:130

commit v6 on v5

--- a/solution.py
+++ b/solution.py
@@ -83,12 +83,18 @@
         filtered = polyphase(part, filter_coeffs, row_gain[g * gs : (g + 1) * gs])
         local_spec = transform(filtered, cos_table, sin_table)
         send = local_spec.reshape(2, gs, nt, ndev, kc).transpose(3, 4, 0, 1, 2)
-        arrived.append(lax.all_to_all(send, AXES, split_axis=0, concat_axis=0, tiled=True))
-    recv_all = jnp.stack(arrived, axis=3).reshape(nblk, nst, kc, 2, ngr, gs, nt)
+        if g < ngr - 1:
+            arrived.append(lax.all_to_all(send, AXES, split_axis=0, concat_axis=0, tiled=True))
+        else:
+            last = [
+                lax.all_to_all(send[:, c], AXES, split_axis=0, concat_axis=0, tiled=True)
+                for c in range(kc)
+            ]
     hi = lax.Precision.HIGHEST
     got = []
     for c in range(kc):
-        recv = recv_all[:, :, c]
+        pieces = [part[:, c] for part in arrived] + [last[c]]
+        recv = jnp.stack(pieces, axis=2).reshape(nblk, nst, 2, ngr, gs, nt)
         spec = recv.transpose(2, 1, 3, 4, 0, 5).reshape(2 * stations, counted)
         gram = jnp.dot(spec, spec.T, preferred_element_type=jnp.float32)
         g00 = gram[:stations, :stations]

time: 434 us -> 417 us (0.961)
  local copies, waits for them, and re-layouts: 75.2 us -> 64.2 us
  starting transfers between devices: 26.6 us -> 36.4 us
  matrix products: 57.3 us -> 50.8 us
  waiting for transfers between devices: 107 us -> 101 us
    all_to_all x4 -> x3, waiting for transfers between devices: 81.2 us -> 49.2 us  [local(): lax.all_to_all(send, AXES, split_axis=0, concat_axis=0, tiled=True)]
    all_to_all x0 -> x4, waiting for transfers between devices: none -> 25.5 us  [local(): lax.all_to_all(send[:, c], AXES, split_axis=0, concat_axis=0, tiled=True)]
    all_to_all x0 -> x4, starting transfers between devices: none -> 12.5 us  [local(): lax.all_to_all(send[:, c], AXES, split_axis=0, concat_axis=0, tiled=True)]
    all_to_all x4 -> x0, local copies, waits for them, and re-layouts: 10.4 us -> none  [local(): lax.all_to_all(send, AXES, split_axis=0, concat_axis=0, tiled=True)]
    dot_general x16, matrix products: 21.1 us -> 12.4 us  [transform(): jnp.einsum('stc,ck->stk', a, b, preferred_element_type=jnp.float32)]
    slice x0 -> x3, local copies, waits for them, and re-layouts: none -> 8.21 us  [local(): pieces = [part[:, c] for part in arrived] + [last[c]]]
    transpose x5 -> x4, local copies, waits for them, and re-layouts: 18.2 us -> 10.8 us  [local(): spec = recv.transpose(2, 1, 3, 4, 0, 5).reshape(2 * stations, counted)]
    transpose x0 -> x4, other arithmetic: none -> 5.29 us  [local(): spec = recv.transpose(2, 1, 3, 4, 0, 5).reshape(2 * stations, counted)]
  transfers between devices with their start and end apart: 7 -> 10, of which waited for: 7 -> 10; matrix products, arithmetic and copies ran while one was open for 33% -> 39% of each run, Pallas kernels for 0% -> 0%
where the time goes in v6:
time: 417 us; the launch traced here: 409 us
  other arithmetic  134 us (32%)
  waiting for transfers between devices  101 us (24%)
  local copies, waits for them, and re-layouts  64.2 us (15%)
  matrix products  50.8 us (12%)
  starting transfers between devices  36.4 us (9%)
  blocking collectives  18.3 us (4%)
    convert_element_type x4, other arithmetic, polyphase(): return (filtered * row_gain[None, :, None, None]).astype(jnp.bfloat16)  85.4 us
    all_to_all x3, waiting for transfers between devices, local(): lax.all_to_all(send, AXES, split_axis=0, concat_axis=0, tiled=True)  49.2 us
    all_to_all x3, waiting for transfers between devices, local(): lax.all_to_all(out, AXES, split_axis=0, concat_axis=0, tiled=True)  26.2 us
    all_to_all x4, waiting for transfers between devices, local(): lax.all_to_all(send[:, c], AXES, split_axis=0, concat_axis=0, tiled=True)  25.5 us
    reshape x4, local copies, waits for them, and re-layouts, polyphase(): grid = samples.astype(jnp.float32).reshape(2, samples.shape[1], -1, width)  20.3 us
    dot_general x8, matrix products, local(): prod = jnp.dot(rows, both, precision=hi)  18.8 us
    all_to_all x1, blocking collectives, local(): lax.all_to_all(out, AXES, split_axis=0, concat_axis=0, tiled=True)  18.3 us
    all_to_all x3, starting transfers between devices, local(): lax.all_to_all(send, AXES, split_axis=0, concat_axis=0, tiled=True)  15.3 us
  transfers between devices with their start and end apart: 10, of which 10 were waited for; matrix products, arithmetic and copies ran while one was open for 39% of the time, Pallas kernels for 0%

profile of v6, /device:TPU:0, one launch (start us, length us, event | category | flops | bytes accessed | tf_op | source)
XLA Modules:
  0.0 408.8 jit_solution(2899713947732782493)
XLA Ops:
  1.0 9.9 %slice_convert_fusion.3 = (f32[2,16,34176]{2,1,0:T(8,128)}, f32[2,16,34176]{2,1,0:T(8,128)}, f32[2,16,34176]{2,1,0:T(8,128)}, f32[2,16,34176]{2,1,0:T(8,128)}) fusion(bf16[2,64,34176]{2,1,0:T(8,128)(2,1)} %bitcast.196), kind=kLoop, calls=%fused_computation.103 | loop fusion | flops 4374528 | bytes 26247168 | tf_op jit(solution)/shard_map/reshape | solution.py:26
  10.9 5.1 %reshape.174 = f32[2,16,267,128]{3,2,1,0:T(8,128)} reshape(f32[2,16,34176]{2,1,0:T(8,128)} %get-tuple-element.25) | data formatting | bytes 8749056 | tf_op jit(solution)/shard_map/reshape | solution.py:26
  16.1 21.4 %fusion.41 = bf16[2,16,256,128]{3,2,1,0:T(8,128)(2,1)S(1)} fusion(f32[2,16,267,128]{3,2,1,0:T(8,128)} %reshape.174, f32[16]{0:T(128)S(1)} %get-tuple-element.93, f32[128]{0:T(128)S(1)} %get-tuple-element.91, f32[128]{0:T(128)S(1)} %get-tuple-element.92, f32[128]{0:T(128)S(1)} %get-tuple-element.82, f32[128]{0:T(128)S(1)} %get-tuple-element.83, ...), kind=kLoop, calls=%fused_computation.78 | loop fusion | flops 26214400 | bytes 52435008 | tf_op jit(solution)/shard_map/convert_element_type | solution.py:34
  42.8 7.6 %all-to-all-start = ((bf16[32,4,2,16,256]{4,3,2,1,0:T(8,128)(2,1)}), bf16[32,4,2,16,256]{4,3,2,1,0:T(8,128)(2,1)}, u32[]{:S(2)}, u32[]{:S(2)}) async-start(bf16[32,4,2,16,256]{4,3,2,1,0:T(8,128)(2,1)} %maximum_bitcast_fusion), calls=%async_computation | async-start | bytes 4194304 | tf_op jit(solution)/shard_map/all_to_all | solution.py:87
  50.4 5.1 %reshape.176 = f32[2,16,267,128]{3,2,1,0:T(8,128)} reshape(f32[2,16,34176]{2,1,0:T(8,128)} %get-tuple-element.28) | data formatting | bytes 8749056 | tf_op jit(solution)/shard_map/reshape | solution.py:26
  55.5 21.4 %fusion.28 = bf16[2,16,256,128]{3,2,1,0:T(8,128)(2,1)S(1)} fusion(f32[2,16,267,128]{3,2,1,0:T(8,128)} %reshape.176, f32[16]{0:T(128)S(1)} %get-tuple-element.96, f32[128]{0:T(128)S(1)} %get-tuple-element.91, f32[128]{0:T(128)S(1)} %get-tuple-element.92, f32[128]{0:T(128)S(1)} %get-tuple-element.82, f32[128]{0:T(128)S(1)} %get-tuple-element.83, ...), kind=kLoop, calls=%fused_computation.53 | loop fusion | flops 26214400 | bytes 52435008 | tf_op jit(solution)/shard_map/convert_element_type | solution.py:34
  82.2 18.3 %all-to-all-done = bf16[32,4,2,16,256]{4,3,2,1,0:T(8,128)(2,1)} async-done(((bf16[32,4,2,16,256]{4,3,2,1,0:T(8,128)(2,1)}), bf16[32,4,2,16,256]{4,3,2,1,0:T(8,128)(2,1)}, u32[]{:S(2)}, u32[]{:S(2)}) %all-to-all-start) | async-done | bytes 2097184 | tf_op jit(solution)/shard_map/all_to_all | solution.py:87
  100.4 3.7 all-to-all-start.1
  104.2 5.1 %reshape.178 = f32[2,16,267,128]{3,2,1,0:T(8,128)} reshape(f32[2,16,34176]{2,1,0:T(8,128)} %get-tuple-element.27) | data formatting | bytes 8749056 | tf_op jit(solution)/shard_map/reshape | solution.py:26
  109.2 21.4 %fusion.15 = bf16[2,16,256,128]{3,2,1,0:T(8,128)(2,1)S(1)} fusion(f32[2,16,267,128]{3,2,1,0:T(8,128)} %reshape.178, f32[16]{0:T(128)S(1)} %get-tuple-element.95, f32[128]{0:T(128)S(1)} %get-tuple-element.91, f32[128]{0:T(128)S(1)} %get-tuple-element.92, f32[128]{0:T(128)S(1)} %get-tuple-element.82, f32[128]{0:T(128)S(1)} %get-tuple-element.83, ...), kind=kLoop, calls=%fused_computation.28 | loop fusion | flops 26214400 | bytes 52435008 | tf_op jit(solution)/shard_map/convert_element_type | solution.py:34
  135.9 18.3 %all-to-all-done.1 = bf16[32,4,2,16,256]{4,3,2,1,0:T(8,128)(2,1)} async-done(((bf16[32,4,2,16,256]{4,3,2,1,0:T(8,128)(2,1)}), bf16[32,4,2,16,256]{4,3,2,1,0:T(8,128)(2,1)}, u32[]{:S(2)}, u32[]{:S(2)}) %all-to-all-start.1) | async-done | bytes 2097184 | tf_op jit(solution)/shard_map/all_to_all | solution.py:87
  154.2 4.0 all-to-all-start.2
  158.2 5.1 %reshape.180 = f32[2,16,267,128]{3,2,1,0:T(8,128)} reshape(f32[2,16,34176]{2,1,0:T(8,128)} %get-tuple-element.26) | data formatting | bytes 8749056 | tf_op jit(solution)/shard_map/reshape | solution.py:26
  163.3 21.4 %fusion.2 = bf16[2,16,256,128]{3,2,1,0:T(8,128)(2,1)S(1)} fusion(f32[2,16,267,128]{3,2,1,0:T(8,128)} %reshape.180, f32[16]{0:T(128)S(1)} %get-tuple-element.94, f32[128]{0:T(128)S(1)} %get-tuple-element.91, f32[128]{0:T(128)S(1)} %get-tuple-element.92, f32[128]{0:T(128)S(1)} %get-tuple-element.82, f32[128]{0:T(128)S(1)} %get-tuple-element.83, ...), kind=kLoop, calls=%fused_computation.3 | loop fusion | flops 26214400 | bytes 52435008 | tf_op jit(solution)/shard_map/convert_element_type | solution.py:34
  195.6 12.6 %all-to-all-done.2 = bf16[32,4,2,16,256]{4,3,2,1,0:T(8,128)(2,1)} async-done(((bf16[32,4,2,16,256]{4,3,2,1,0:T(8,128)(2,1)}), bf16[32,4,2,16,256]{4,3,2,1,0:T(8,128)(2,1)}, u32[]{:S(2)}, u32[]{:S(2)}) %all-to-all-start.2) | async-done | bytes 2097184 | tf_op jit(solution)/shard_map/all_to_all | solution.py:87
  208.2 2.6 all-to-all-start.5
  211.0 2.8 fusion.380
  213.8 2.7 fusion.381
  216.5 2.7 fusion.382
  219.2 8.0 %all-to-all-done.5 = bf16[32,2,16,256]{3,2,1,0:T(8,128)(2,1)S(1)} async-done(((bf16[32,2,16,256]{3,2,1,0:T(8,128)(2,1)}), bf16[32,2,16,256]{3,2,1,0:T(8,128)(2,1)S(1)}, u32[]{:S(2)}, u32[]{:S(2)}) %all-to-all-start.5) | async-done | bytes 524320 | tf_op jit(solution)/shard_map/all_to_all | solution.py:90
  227.2 2.8 all-to-all-start.9
  230.3 2.7 copy.50
  236.9 9.5 %all-to-all-done.9 = bf16[32,2,16,256]{3,2,1,0:T(8,128)(2,1)S(1)} async-done(((bf16[32,2,16,256]{3,2,1,0:T(8,128)(2,1)}), bf16[32,2,16,256]{3,2,1,0:T(8,128)(2,1)S(1)}, u32[]{:S(2)}, u32[]{:S(2)}) %all-to-all-start.9) | async-done | bytes 524320 | tf_op jit(solution)/shard_map/all_to_all | solution.py:90
  246.3 3.3 all-to-all-start.7
  251.1 2.7 copy.62
  256.2 4.6 %fusion.387 = f32[1024,1024]{1,0:T(8,128)S(1)} fusion(bf16[1024,1024]{1,0:T(8,128)(2,1)} %bitcast.208), kind=kOutput, calls=%fused_computation.519 | convolution fusion | flops 2147483648 | bytes 6291456 | tf_op jit(solution)/shard_map/dot_general | solution.py:99
  263.5 2.5 all-to-all-done.7
  266.0 3.8 all-to-all-start.3
  271.6 2.7 copy.56
  277.2 2.4 fusion.80
  280.1 5.6 %all-to-all-done.3 = bf16[32,2,16,256]{3,2,1,0:T(8,128)(2,1)} async-done(((bf16[32,2,16,256]{3,2,1,0:T(8,128)(2,1)}), bf16[32,2,16,256]{3,2,1,0:T(8,128)(2,1)}, u32[]{:S(2)}, u32[]{:S(2)}) %all-to-all-start.3) | async-done | bytes 524320 | tf_op jit(solution)/shard_map/all_to_all | solution.py:90
  287.5 2.7 copy.44
  293.1 2.6 fusion.76
  298.6 3.6 fusion.55
  304.3 5.2 %fusion.230 = (f32[512,128]{0,1:T(8,128)S(1)}, f32[512,128]{0,1:T(8,128)S(1)}, f32[512,128]{0,1:T(8,128)S(1)}, f32[512,128]{0,1:T(8,128)S(1)}, f32[512,128]{0,1:...) fusion(f32[1024,256]{0,1:T(8,128)S(1)} %fusion.59, f32[]{:T(128)S(6)} %add.411, ...), kind=kLoop, calls=%fused_computation.355 | loop fusion | flops 6029312 | bytes 4464664 | tf_op jit(solution)/shard_map/add | solution.py:124
  320.0 4.0 fusion.368
  327.9 2.6 all-to-all-start.4
  330.6 3.0 fusion.57
  338.0 3.7 fusion.238
  343.7 3.1 all-to-all-done.4
  346.9 3.3 all-to-all-start.6
  350.3 3.3 fusion.62
  355.9 10.7 %all-to-all-done.6 = bf16[32,2,16,256]{3,2,1,0:T(8,128)(2,1)} async-done(((bf16[32,2,16,256]{3,2,1,0:T(8,128)(2,1)}), bf16[32,2,16,256]{3,2,1,0:T(8,128)(2,1)}, u32[]{:S(2)}, u32[]{:S(2)}) %all-to-all-start.6) | async-done | bytes 524320 | tf_op jit(solution)/shard_map/all_to_all | solution.py:136
  366.6 2.6 all-to-all-start.8
  369.2 2.5 fusion.63
  373.2 12.3 %all-to-all-done.8 = bf16[32,2,16,256]{3,2,1,0:T(8,128)(2,1)S(1)} async-done(((bf16[32,2,16,256]{3,2,1,0:T(8,128)(2,1)}), bf16[32,2,16,256]{3,2,1,0:T(8,128)(2,1)S(1)}, u32[]{:S(2)}, u32[]{:S(2)}) %all-to-all-start.8) | async-done | bytes 524320 | tf_op jit(solution)/shard_map/all_to_all | solution.py:136
  385.5 18.3 %all_to_all.55 = bf16[32,2,16,256]{3,2,1,0:T(8,128)(2,1)S(1)} all-to-all(bf16[32,2,16,256]{3,2,1,0:T(8,128)(2,1)S(1)} %bitcast.216), channel_id=1, replica_groups=mesh['blk'=4,'st'=8] {'blk','st'}, dimensions={0} | all-to-all | bytes 1048576 | tf_op jit(solution)/shard_map/all_to_all | solution.py:136
  405.5 2.9 copy.65
  (126 shorter events, 77.1 us)
Async XLA Ops:
  10.9 5.1 %copy-start.25 = (f32[64]{0:T(128)S(1)}, f32[64]{0:T(128)}, u32[]{:S(2)}) copy-start(f32[64]{0:T(128)} %param.7) | copy-start | bytes 772
  10.9 5.1 %copy-start.26 = (s32[1,64]{1,0:T(1,128)S(1)}, s32[1,64]{1,0:T(1,128)}, u32[]{:S(2)}) copy-start(s32[1,64]{1,0:T(1,128)} %param.8) | copy-start | bytes 772
  42.8 57.7 %all-to-all-start = ((bf16[32,4,2,16,256]{4,3,2,1,0:T(8,128)(2,1)}), bf16[32,4,2,16,256]{4,3,2,1,0:T(8,128)(2,1)}, u32[]{:S(2)}, u32[]{:S(2)}) async-start(bf16[32,4,2,16,256]{4,3,2,1,0:T(8,128)(2,1)} %maximum_bitcast_fusion), calls=%async_computation | async-start | bytes 4194304 | tf_op jit(solution)/shard_map/all_to_all | solution.py:87
  100.4 53.8 %all-to-all-start.1 = ((bf16[32,4,2,16,256]{4,3,2,1,0:T(8,128)(2,1)}), bf16[32,4,2,16,256]{4,3,2,1,0:T(8,128)(2,1)}, u32[]{:S(2)}, u32[]{:S(2)}) async-start(bf16[32,4,2,16,256]{4,3,2,1,0:T(8,128)(2,1)} %maximum_bitcast_fusion.1), calls=%async_computation.1 | async-start | bytes 4194304 | tf_op jit(solution)/shard_map/all_to_all | solution.py:87
  154.2 54.0 %all-to-all-start.2 = ((bf16[32,4,2,16,256]{4,3,2,1,0:T(8,128)(2,1)}), bf16[32,4,2,16,256]{4,3,2,1,0:T(8,128)(2,1)}, u32[]{:S(2)}, u32[]{:S(2)}) async-start(bf16[32,4,2,16,256]{4,3,2,1,0:T(8,128)(2,1)} %maximum_bitcast_fusion.2), calls=%async_computation.2 | async-start | bytes 4194304 | tf_op jit(solution)/shard_map/all_to_all | solution.py:87
  190.5 3.6 copy-start.9
  194.1 16.8 %copy-start.21 = (s32[512,128]{1,0:T(8,128)S(1)}, s32[512,128]{1,0:T(8,128)}, u32[]{:S(2)}) copy-start(s32[512,128]{1,0:T(8,128)} %param.9) | copy-start | bytes 786436
  208.2 19.0 %all-to-all-start.5 = ((bf16[32,2,16,256]{3,2,1,0:T(8,128)(2,1)}), bf16[32,2,16,256]{3,2,1,0:T(8,128)(2,1)S(1)}, u32[]{:S(2)}, u32[]{:S(2)}) async-start(bf16[32,2,16,256]{3,2,1,0:T(8,128)(2,1)} %get-tuple-element.48), calls=%async_computation.5 | async-start | bytes 1048576 | tf_op jit(solution)/shard_map/all_to_all | solution.py:90
  227.2 19.1 %all-to-all-start.9 = ((bf16[32,2,16,256]{3,2,1,0:T(8,128)(2,1)}), bf16[32,2,16,256]{3,2,1,0:T(8,128)(2,1)S(1)}, u32[]{:S(2)}, u32[]{:S(2)}) async-start(bf16[32,2,16,256]{3,2,1,0:T(8,128)(2,1)} %get-tuple-element.46), calls=%async_computation.9 | async-start | bytes 1048576 | tf_op jit(solution)/shard_map/all_to_all | solution.py:90
  233.5 2.4 copy-start.15
  246.3 19.7 %all-to-all-start.7 = ((bf16[32,2,16,256]{3,2,1,0:T(8,128)(2,1)}), bf16[32,2,16,256]{3,2,1,0:T(8,128)(2,1)}, u32[]{:S(2)}, u32[]{:S(2)}) async-start(bf16[32,2,16,256]{3,2,1,0:T(8,128)(2,1)} %get-tuple-element.47), calls=%async_computation.7 | async-start | bytes 1048576 | tf_op jit(solution)/shard_map/all_to_all | solution.py:90
  266.0 19.7 %all-to-all-start.3 = ((bf16[32,2,16,256]{3,2,1,0:T(8,128)(2,1)}), bf16[32,2,16,256]{3,2,1,0:T(8,128)(2,1)}, u32[]{:S(2)}, u32[]{:S(2)}) async-start(bf16[32,2,16,256]{3,2,1,0:T(8,128)(2,1)} %get-tuple-element.45), calls=%async_computation.3 | async-start | bytes 1048576 | tf_op jit(solution)/shard_map/all_to_all | solution.py:90
  274.8 2.4 copy-start.17
  290.7 2.4 copy-start.18
  296.4 5.8 %copy-start.3 = (f32[512,512]{1,0:T(8,128)S(1)}, f32[512,512]{1,0:T(8,128)}, u32[]{:S(2)}) copy-start(f32[512,512]{1,0:T(8,128)} %get-tuple-element.15) | copy-start | bytes 3145732
  296.4 5.8 %copy-start.4 = (f32[512,512]{1,0:T(8,128)S(1)}, f32[512,512]{1,0:T(8,128)}, u32[]{:S(2)}) copy-start(f32[512,512]{1,0:T(8,128)} %get-tuple-element.29) | copy-start | bytes 3145732
  302.2 7.3 %copy-start.1 = (f32[512,512]{1,0:T(8,128)S(1)}, f32[512,512]{1,0:T(8,128)}, u32[]{:S(2)}) copy-start(f32[512,512]{1,0:T(8,128)} %get-tuple-element.21) | copy-start | bytes 3145732
  302.2 7.3 %copy-start.2 = (f32[512,512]{1,0:T(8,128)S(1)}, f32[512,512]{1,0:T(8,128)}, u32[]{:S(2)}) copy-start(f32[512,512]{1,0:T(8,128)} %get-tuple-element.31) | copy-start | bytes 3145732
  309.5 6.2 %copy-start.10 = (f32[512,128]{0,1:T(8,128)}, f32[512,128]{0,1:T(8,128)S(1)}, u32[]{:S(2)}) copy-start(f32[512,128]{0,1:T(8,128)S(1)} %get-tuple-element.70) | copy-start | bytes 786436
  309.5 4.1 %copy-start = (f32[512,512]{1,0:T(8,128)S(1)}, f32[512,512]{1,0:T(8,128)}, u32[]{:S(2)}) copy-start(f32[512,512]{1,0:T(8,128)} %get-tuple-element.32) | copy-start | bytes 3145732
  311.5 8.5 %copy-start.5 = (f32[1024,256]{0,1:T(8,128)}, f32[1024,256]{0,1:T(8,128)S(1)}, u32[]{:S(2)}) copy-start(f32[1024,256]{0,1:T(8,128)S(1)} %fusion.54) | copy-start | bytes 3145732
  317.9 6.1 %copy-start.12 = (f32[512,128]{0,1:T(8,128)}, f32[512,128]{0,1:T(8,128)S(1)}, u32[]{:S(2)}) copy-start(f32[512,128]{0,1:T(8,128)S(1)} %get-tuple-element.56) | copy-start | bytes 786436
  317.9 6.1 %copy-start.19 = (bf16[128,8,4,256]{3,1,2,0:T(8,128)(2,1)S(1)}, bf16[128,8,4,256]{3,1,2,0:T(8,128)(2,1)}, u32[]{:S(2)}) copy-start(bf16[128,8,4,256]{3,1,2,0:T(8,128)(2,1)} %copy-done.18) | copy-start | bytes 6291460
  320.0 4.0 copy-start.7
  324.0 6.5 %copy-start.20 = (f32[512,128]{0,1:T(8,128)S(1)}, f32[512,128]{0,1:T(8,128)}, u32[]{:S(2)}) copy-start(f32[512,128]{0,1:T(8,128)} %get-tuple-element.74) | copy-start | bytes 786436
  327.9 19.0 %all-to-all-start.4 = ((bf16[32,2,16,256]{3,2,1,0:T(8,128)(2,1)}), bf16[32,2,16,256]{3,2,1,0:T(8,128)(2,1)S(1)}, u32[]{:S(2)}, u32[]{:S(2)}) async-start(bf16[32,2,16,256]{3,2,1,0:T(8,128)(2,1)} %bitcast.41), calls=%async_computation.4 | async-start | bytes 1048576 | tf_op jit(solution)/shard_map/all_to_all | solution.py:136
  333.5 4.4 %copy-start.6 = (f32[1024,256]{0,1:T(8,128)S(1)}, f32[1024,256]{0,1:T(8,128)}, u32[]{:S(2)}) copy-start(f32[1024,256]{0,1:T(8,128)} %copy-done.5) | copy-start | bytes 3145732
  333.5 4.4 %copy-start.8 = (f32[1024,256]{0,1:T(8,128)S(1)}, f32[1024,256]{0,1:T(8,128)}, u32[]{:S(2)}) copy-start(f32[1024,256]{0,1:T(8,128)} %copy-done.7) | copy-start | bytes 3145732
  333.5 4.4 %copy-start.11 = (f32[512,128]{0,1:T(8,128)S(1)}, f32[512,128]{0,1:T(8,128)}, u32[]{:S(2)}) copy-start(f32[512,128]{0,1:T(8,128)} %copy-done.10) | copy-start | bytes 786436
  333.6 4.4 %copy-start.13 = (f32[512,128]{0,1:T(8,128)S(1)}, f32[512,128]{0,1:T(8,128)}, u32[]{:S(2)}) copy-start(f32[512,128]{0,1:T(8,128)} %copy-done.12) | copy-start | bytes 786436
  334.8 6.9 %copy-start.16 = (bf16[128,8,4,256]{3,1,2,0:T(8,128)(2,1)S(1)}, bf16[128,8,4,256]{3,1,2,0:T(8,128)(2,1)}, u32[]{:S(2)}) copy-start(bf16[128,8,4,256]{3,1,2,0:T(8,128)(2,1)} %copy-done.15) | copy-start | bytes 6291460
  341.7 8.6 %copy-start.23 = (bf16[512,128]{0,1:T(8,128)(2,1)S(1)}, bf16[512,128]{0,1:T(8,128)(2,1)}, u32[]{:S(2)}) copy-start(bf16[512,128]{0,1:T(8,128)(2,1)} %get-tuple-element.67) | copy-start | bytes 393220
  341.7 8.6 %copy-start.24 = (bf16[512,128]{0,1:T(8,128)(2,1)S(1)}, bf16[512,128]{0,1:T(8,128)(2,1)}, u32[]{:S(2)}) copy-start(bf16[512,128]{0,1:T(8,128)(2,1)} %get-tuple-element.68) | copy-start | bytes 393220
  346.9 19.7 %all-to-all-start.6 = ((bf16[32,2,16,256]{3,2,1,0:T(8,128)(2,1)}), bf16[32,2,16,256]{3,2,1,0:T(8,128)(2,1)}, u32[]{:S(2)}, u32[]{:S(2)}) async-start(bf16[32,2,16,256]{3,2,1,0:T(8,128)(2,1)} %bitcast.50), calls=%async_computation.6 | async-start | bytes 1048576 | tf_op jit(solution)/shard_map/all_to_all | solution.py:136
  350.2 18.9 %copy-start.14 = (bf16[128,8,4,256]{3,1,2,0:T(8,128)(2,1)S(1)}, bf16[128,8,4,256]{3,1,2,0:T(8,128)(2,1)}, u32[]{:S(2)}) copy-start(bf16[128,8,4,256]{3,1,2,0:T(8,128)(2,1)} %copy.87) | copy-start | bytes 6291460
  350.2 18.9 %copy-start.22 = (bf16[512,128]{0,1:T(8,128)(2,1)S(1)}, bf16[512,128]{0,1:T(8,128)(2,1)}, u32[]{:S(2)}) copy-start(bf16[512,128]{0,1:T(8,128)(2,1)} %get-tuple-element.66) | copy-start | bytes 393220
  366.6 19.0 %all-to-all-start.8 = ((bf16[32,2,16,256]{3,2,1,0:T(8,128)(2,1)}), bf16[32,2,16,256]{3,2,1,0:T(8,128)(2,1)S(1)}, u32[]{:S(2)}, u32[]{:S(2)}) async-start(bf16[32,2,16,256]{3,2,1,0:T(8,128)(2,1)} %bitcast.59), calls=%async_computation.8 | async-start | bytes 1048576 | tf_op jit(solution)/shard_map/all_to_all | solution.py:136

commit v7 on v6

--- a/solution.py
+++ b/solution.py
@@ -92,8 +92,11 @@
             ]
     hi = lax.Precision.HIGHEST
     got = []
+    prev = None
     for c in range(kc):
         pieces = [part[:, c] for part in arrived] + [last[c]]
+        if prev is not None:
+            pieces, _ = lax.optimization_barrier((pieces, prev))
         recv = jnp.stack(pieces, axis=2).reshape(nblk, nst, 2, ngr, gs, nt)
         spec = recv.transpose(2, 1, 3, 4, 0, 5).reshape(2 * stations, counted)
         gram = jnp.dot(spec, spec.T, preferred_element_type=jnp.float32)
@@ -133,6 +136,7 @@
         beam = (beam * factor).astype(jnp.bfloat16)
         bc = nb // nst
         out = beam.reshape(2, nst, bc, nblk, nt).transpose(3, 1, 0, 2, 4).reshape(ndev, 2, bc, nt)
+        prev = out
         got.append(lax.all_to_all(out, AXES, split_axis=0, concat_axis=0, tiled=True))
     res = jnp.stack(got, axis=4).transpose(1, 2, 3, 0, 4).reshape(2, bc, nt, ndev * kc)
     return res[:, :, None]

time: 417 us -> 408 us (0.978)
  blocking collectives: 18.3 us -> 77.4 us
  waiting for transfers between devices: 101 us -> 56.2 us
  matrix products: 50.8 us -> 41.9 us
  local copies, waits for them, and re-layouts: 64.2 us -> 57 us
    all_to_all x1 -> x4, blocking collectives: 18.3 us -> 77.4 us  [local(): lax.all_to_all(out, AXES, split_axis=0, concat_axis=0, tiled=True)]
    all_to_all x3 -> x0, waiting for transfers between devices: 26.2 us -> none  [local(): lax.all_to_all(out, AXES, split_axis=0, concat_axis=0, tiled=True)]
    all_to_all x4, waiting for transfers between devices: 25.5 us -> 8.05 us  [local(): lax.all_to_all(send[:, c], AXES, split_axis=0, concat_axis=0, tiled=True)]
    all_to_all x3 -> x0, starting transfers between devices: 8.54 us -> none  [local(): lax.all_to_all(out, AXES, split_axis=0, concat_axis=0, tiled=True)]
    transpose x4 -> x1, local copies, waits for them, and re-layouts: 10.8 us -> 2.7 us  [local(): spec = recv.transpose(2, 1, 3, 4, 0, 5).reshape(2 * stations, counted)]
    another operation x0 -> x12, local copies, waits for them, and re-layouts: none -> 6.98 us  [local(): recv = jnp.stack(pieces, axis=2).reshape(nblk, nst, 2, ngr, gs, nt)]
    all_to_all x4, starting transfers between devices: 12.5 us -> 18 us  [local(): lax.all_to_all(send[:, c], AXES, split_axis=0, concat_axis=0, tiled=True)]
    another operation x0 -> x3, other arithmetic: none -> 5.27 us  [local(): recv = jnp.stack(pieces, axis=2).reshape(nblk, nst, 2, ngr, gs, nt)]
  transfers between devices with their start and end apart: 10 -> 7, of which waited for: 10 -> 4; matrix products, arithmetic and copies ran while one was open for 39% -> 41% of each run, Pallas kernels for 0% -> 0%
where the time goes in v7:
time: 408 us; the launch traced here: 400 us
  other arithmetic  130 us (32%)
  blocking collectives  77.4 us (19%)
  local copies, waits for them, and re-layouts  57 us (14%)
  waiting for transfers between devices  56.2 us (14%)
  matrix products  41.9 us (10%)
  starting transfers between devices  33.3 us (8%)
    convert_element_type x4, other arithmetic, polyphase(): return (filtered * row_gain[None, :, None, None]).astype(jnp.bfloat16)  86.9 us
    all_to_all x4, blocking collectives, local(): lax.all_to_all(out, AXES, split_axis=0, concat_axis=0, tiled=True)  77.4 us
    all_to_all x3, waiting for transfers between devices, local(): lax.all_to_all(send, AXES, split_axis=0, concat_axis=0, tiled=True)  48.2 us
    reshape x4, local copies, waits for them, and re-layouts, polyphase(): grid = samples.astype(jnp.float32).reshape(2, samples.shape[1], -1, width)  20.2 us
    all_to_all x4, starting transfers between devices, local(): lax.all_to_all(send[:, c], AXES, split_axis=0, concat_axis=0, tiled=True)  18 us
    dot_general x8, matrix products, local(): prod = jnp.dot(rows, both, precision=hi)  16.4 us
    all_to_all x3, starting transfers between devices, local(): lax.all_to_all(send, AXES, split_axis=0, concat_axis=0, tiled=True)  15.3 us
    dot_general x16, matrix products, transform(): jnp.einsum('stc,ck->stk', a, b, preferred_element_type=jnp.float32)  12.3 us
  transfers between devices with their start and end apart: 7, of which 4 were waited for; matrix products, arithmetic and copies ran while one was open for 41% of the time, Pallas kernels for 0%

profile of v7, /device:TPU:0, one launch (start us, length us, event | category | flops | bytes accessed | tf_op | source)
XLA Modules:
  0.0 400.1 jit_solution(3046964614113472670)
XLA Ops:
  0.0 9.9 %slice_convert_fusion = (f32[2,16,34176]{2,1,0:T(8,128)}, f32[2,16,34176]{2,1,0:T(8,128)}, f32[2,16,34176]{2,1,0:T(8,128)}, f32[2,16,34176]{2,1,0:T(8,128)}) fusion(bf16[2,64,34176]{2,1,0:T(8,128)(2,1)} %bitcast.211), kind=kLoop, calls=%fused_computation.100 | loop fusion | flops 4374528 | bytes 26247168 | tf_op jit(solution)/shard_map/reshape | solution.py:26
  9.9 5.1 %reshape.174 = f32[2,16,267,128]{3,2,1,0:T(8,128)} reshape(f32[2,16,34176]{2,1,0:T(8,128)} %get-tuple-element.52) | data formatting | bytes 8749056 | tf_op jit(solution)/shard_map/reshape | solution.py:26
  15.1 21.7 %fusion.41 = bf16[2,16,256,128]{3,2,1,0:T(8,128)(2,1)S(1)} fusion(f32[2,16,267,128]{3,2,1,0:T(8,128)} %reshape.174, f32[16]{0:T(128)S(1)} %get-tuple-element.104, f32[128]{0:T(128)S(1)} %get-tuple-element.99, f32[128]{0:T(128)S(1)} %get-tuple-element.100, f32[128]{0:T(128)S(1)} %get-tuple-element.90, f32[128]{0:T(128)S(1)} %get-tuple-element.91, ...), kind=kLoop, calls=%fused_computation.78 | loop fusion | flops 26214400 | bytes 52435008 | tf_op jit(solution)/shard_map/convert_element_type | solution.py:34
  42.2 7.6 %all-to-all-start = ((bf16[32,4,2,16,256]{4,3,2,1,0:T(8,128)(2,1)}), bf16[32,4,2,16,256]{4,3,2,1,0:T(8,128)(2,1)}, u32[]{:S(2)}, u32[]{:S(2)}) async-start(bf16[32,4,2,16,256]{4,3,2,1,0:T(8,128)(2,1)} %maximum_bitcast_fusion), calls=%async_computation | async-start | bytes 4194304 | tf_op jit(solution)/shard_map/all_to_all | solution.py:87
  49.8 5.0 %reshape.176 = f32[2,16,267,128]{3,2,1,0:T(8,128)} reshape(f32[2,16,34176]{2,1,0:T(8,128)} %get-tuple-element.51) | data formatting | bytes 8749056 | tf_op jit(solution)/shard_map/reshape | solution.py:26
  54.9 21.7 %fusion.28 = bf16[2,16,256,128]{3,2,1,0:T(8,128)(2,1)S(1)} fusion(f32[2,16,267,128]{3,2,1,0:T(8,128)} %reshape.176, f32[16]{0:T(128)S(1)} %get-tuple-element.103, f32[128]{0:T(128)S(1)} %get-tuple-element.99, f32[128]{0:T(128)S(1)} %get-tuple-element.100, f32[128]{0:T(128)S(1)} %get-tuple-element.90, f32[128]{0:T(128)S(1)} %get-tuple-element.91, ...), kind=kLoop, calls=%fused_computation.53 | loop fusion | flops 26214400 | bytes 52435008 | tf_op jit(solution)/shard_map/convert_element_type | solution.py:34
  81.9 18.0 %all-to-all-done = bf16[32,4,2,16,256]{4,3,2,1,0:T(8,128)(2,1)} async-done(((bf16[32,4,2,16,256]{4,3,2,1,0:T(8,128)(2,1)}), bf16[32,4,2,16,256]{4,3,2,1,0:T(8,128)(2,1)}, u32[]{:S(2)}, u32[]{:S(2)}) %all-to-all-start) | async-done | bytes 2097184 | tf_op jit(solution)/shard_map/all_to_all | solution.py:87
  99.9 3.7 all-to-all-start.1
  103.6 5.0 %reshape.178 = f32[2,16,267,128]{3,2,1,0:T(8,128)} reshape(f32[2,16,34176]{2,1,0:T(8,128)} %get-tuple-element.50) | data formatting | bytes 8749056 | tf_op jit(solution)/shard_map/reshape | solution.py:26
  108.7 21.7 %fusion.15 = bf16[2,16,256,128]{3,2,1,0:T(8,128)(2,1)S(1)} fusion(f32[2,16,267,128]{3,2,1,0:T(8,128)} %reshape.178, f32[16]{0:T(128)S(1)} %get-tuple-element.102, f32[128]{0:T(128)S(1)} %get-tuple-element.99, f32[128]{0:T(128)S(1)} %get-tuple-element.100, f32[128]{0:T(128)S(1)} %get-tuple-element.90, f32[128]{0:T(128)S(1)} %get-tuple-element.91, ...), kind=kLoop, calls=%fused_computation.28 | loop fusion | flops 26214400 | bytes 52435008 | tf_op jit(solution)/shard_map/convert_element_type | solution.py:34
  135.7 18.0 %all-to-all-done.1 = bf16[32,4,2,16,256]{4,3,2,1,0:T(8,128)(2,1)} async-done(((bf16[32,4,2,16,256]{4,3,2,1,0:T(8,128)(2,1)}), bf16[32,4,2,16,256]{4,3,2,1,0:T(8,128)(2,1)}, u32[]{:S(2)}, u32[]{:S(2)}) %all-to-all-start.1) | async-done | bytes 2097184 | tf_op jit(solution)/shard_map/all_to_all | solution.py:87
  153.7 3.9 all-to-all-start.2
  157.6 5.0 %reshape.180 = f32[2,16,267,128]{3,2,1,0:T(8,128)} reshape(f32[2,16,34176]{2,1,0:T(8,128)} %get-tuple-element.49) | data formatting | bytes 8749056 | tf_op jit(solution)/shard_map/reshape | solution.py:26
  162.6 21.7 %fusion.2 = bf16[2,16,256,128]{3,2,1,0:T(8,128)(2,1)S(1)} fusion(f32[2,16,267,128]{3,2,1,0:T(8,128)} %reshape.180, f32[16]{0:T(128)S(1)} %get-tuple-element.101, f32[128]{0:T(128)S(1)} %get-tuple-element.99, f32[128]{0:T(128)S(1)} %get-tuple-element.100, f32[128]{0:T(128)S(1)} %get-tuple-element.90, f32[128]{0:T(128)S(1)} %get-tuple-element.91, ...), kind=kLoop, calls=%fused_computation.3 | loop fusion | flops 26214400 | bytes 52435008 | tf_op jit(solution)/shard_map/convert_element_type | solution.py:34
  185.0 1.6 subtract_convert_fusion
  188.0 1.6 copy.52
  190.2 1.6 add_convert_fusion
  195.4 12.2 %all-to-all-done.2 = bf16[32,4,2,16,256]{4,3,2,1,0:T(8,128)(2,1)} async-done(((bf16[32,4,2,16,256]{4,3,2,1,0:T(8,128)(2,1)}), bf16[32,4,2,16,256]{4,3,2,1,0:T(8,128)(2,1)}, u32[]{:S(2)}, u32[]{:S(2)}) %all-to-all-start.2) | async-done | bytes 2097184 | tf_op jit(solution)/shard_map/all_to_all | solution.py:87
  207.7 2.6 all-to-all-start.3
  210.4 2.7 fusion.380
  213.1 2.7 fusion.381
  215.9 2.7 fusion.382
  218.6 8.0 %all-to-all-done.3 = bf16[32,2,16,256]{3,2,1,0:T(8,128)(2,1)S(1)} async-done(((bf16[32,2,16,256]{3,2,1,0:T(8,128)(2,1)}), bf16[32,2,16,256]{3,2,1,0:T(8,128)(2,1)S(1)}, u32[]{:S(2)}, u32[]{:S(2)}) %all-to-all-start.3) | async-done | bytes 524320 | tf_op jit(solution)/shard_map/all_to_all | solution.py:90
  226.6 2.8 all-to-all-start.5
  229.7 2.7 copy.53
  232.9 2.4 fusion.384
  238.0 2.0 fusion.59
  241.5 2.0 fusion.58
  246.9 6.3 %all-to-all-start.7 = ((bf16[32,2,16,256]{3,2,1,0:T(8,128)(2,1)}), bf16[32,2,16,256]{3,2,1,0:T(8,128)(2,1)}, u32[]{:S(2)}, u32[]{:S(2)}) async-start(bf16[32,2,16,256]{3,2,1,0:T(8,128)(2,1)} %get-tuple-element.71), calls=%async_computation.7 | async-start | bytes 1048576 | tf_op jit(solution)/shard_map/all_to_all | solution.py:90
  255.0 1.8 pad_maximum_fusion.1
  257.2 2.4 fusion.385
  262.5 2.0 fusion.57
  264.6 1.7 fusion.210
  266.3 2.0 fusion.56
  271.7 6.3 %all-to-all-start.9 = ((bf16[32,2,16,256]{3,2,1,0:T(8,128)(2,1)}), bf16[32,2,16,256]{3,2,1,0:T(8,128)(2,1)}, u32[]{:S(2)}, u32[]{:S(2)}) async-start(bf16[32,2,16,256]{3,2,1,0:T(8,128)(2,1)} %get-tuple-element.70), calls=%async_computation.9 | async-start | bytes 1048576 | tf_op jit(solution)/shard_map/all_to_all | solution.py:90
  280.7 1.8 pad_maximum_fusion.3
  282.9 2.4 fusion.386
  288.1 2.0 fusion.55
  291.6 2.0 fusion.54
  302.4 1.8 pad_maximum_fusion.5
  304.6 2.4 fusion.387
  310.2 2.0 fusion.53
  313.5 2.0 fusion.52
  318.8 22.1 %all_to_all.55 = bf16[32,2,16,256]{3,2,1,0:T(8,128)(2,1)S(1)} all-to-all(bf16[32,2,16,256]{3,2,1,0:T(8,128)(2,1)S(1)} %bitcast.235), channel_id=1, replica_groups=mesh['blk'=4,'st'=8] {'blk','st'}, dimensions={0} | all-to-all | bytes 1048576 | tf_op jit(solution)/shard_map/all_to_all | solution.py:140
  340.9 18.4 %all_to_all.56 = bf16[32,2,16,256]{3,2,1,0:T(8,128)(2,1)S(1)} all-to-all(bf16[32,2,16,256]{3,2,1,0:T(8,128)(2,1)S(1)} %bitcast.233), channel_id=1, replica_groups=mesh['blk'=4,'st'=8] {'blk','st'}, dimensions={0} | all-to-all | bytes 1048576 | tf_op jit(solution)/shard_map/all_to_all | solution.py:140
  359.4 18.4 %all_to_all.57 = bf16[32,2,16,256]{3,2,1,0:T(8,128)(2,1)S(1)} all-to-all(bf16[32,2,16,256]{3,2,1,0:T(8,128)(2,1)S(1)} %bitcast.232), channel_id=1, replica_groups=mesh['blk'=4,'st'=8] {'blk','st'}, dimensions={0} | all-to-all | bytes 1048576 | tf_op jit(solution)/shard_map/all_to_all | solution.py:140
  377.8 18.4 %all_to_all.58 = bf16[32,2,16,256]{3,2,1,0:T(8,128)(2,1)S(1)} all-to-all(bf16[32,2,16,256]{3,2,1,0:T(8,128)(2,1)S(1)} %bitcast.231), channel_id=1, replica_groups=mesh['blk'=4,'st'=8] {'blk','st'}, dimensions={0} | all-to-all | bytes 1048576 | tf_op jit(solution)/shard_map/all_to_all | solution.py:140
  396.8 2.9 copy.83
  (135 shorter events, 60.8 us)
Async XLA Ops:
  9.9 5.1 %copy-start.21 = (f32[64]{0:T(128)S(1)}, f32[64]{0:T(128)}, u32[]{:S(2)}) copy-start(f32[64]{0:T(128)} %param.7) | copy-start | bytes 772
  9.9 5.1 %copy-start.22 = (s32[1,64]{1,0:T(1,128)S(1)}, s32[1,64]{1,0:T(1,128)}, u32[]{:S(2)}) copy-start(s32[1,64]{1,0:T(1,128)} %param.8) | copy-start | bytes 772
  9.9 5.2 %copy-start.20 = (f32[12,128]{1,0:T(8,128)S(1)}, f32[12,128]{1,0:T(8,128)}, u32[]{:S(2)}) copy-start(f32[12,128]{1,0:T(8,128)} %param.6) | copy-start | bytes 18436
  42.2 57.7 %all-to-all-start = ((bf16[32,4,2,16,256]{4,3,2,1,0:T(8,128)(2,1)}), bf16[32,4,2,16,256]{4,3,2,1,0:T(8,128)(2,1)}, u32[]{:S(2)}, u32[]{:S(2)}) async-start(bf16[32,4,2,16,256]{4,3,2,1,0:T(8,128)(2,1)} %maximum_bitcast_fusion), calls=%async_computation | async-start | bytes 4194304 | tf_op jit(solution)/shard_map/all_to_all | solution.py:87
  99.9 53.8 %all-to-all-start.1 = ((bf16[32,4,2,16,256]{4,3,2,1,0:T(8,128)(2,1)}), bf16[32,4,2,16,256]{4,3,2,1,0:T(8,128)(2,1)}, u32[]{:S(2)}, u32[]{:S(2)}) async-start(bf16[32,4,2,16,256]{4,3,2,1,0:T(8,128)(2,1)} %maximum_bitcast_fusion.1), calls=%async_computation.1 | async-start | bytes 4194304 | tf_op jit(solution)/shard_map/all_to_all | solution.py:87
  153.7 54.0 %all-to-all-start.2 = ((bf16[32,4,2,16,256]{4,3,2,1,0:T(8,128)(2,1)}), bf16[32,4,2,16,256]{4,3,2,1,0:T(8,128)(2,1)}, u32[]{:S(2)}, u32[]{:S(2)}) async-start(bf16[32,4,2,16,256]{4,3,2,1,0:T(8,128)(2,1)} %maximum_bitcast_fusion.2), calls=%async_computation.2 | async-start | bytes 4194304 | tf_op jit(solution)/shard_map/all_to_all | solution.py:87
  190.2 3.6 copy-start
  193.8 16.5 %copy-start.19 = (s32[512,128]{1,0:T(8,128)S(1)}, s32[512,128]{1,0:T(8,128)}, u32[]{:S(2)}) copy-start(s32[512,128]{1,0:T(8,128)} %param.9) | copy-start | bytes 786436
  207.7 19.0 %all-to-all-start.3 = ((bf16[32,2,16,256]{3,2,1,0:T(8,128)(2,1)}), bf16[32,2,16,256]{3,2,1,0:T(8,128)(2,1)S(1)}, u32[]{:S(2)}, u32[]{:S(2)}) async-start(bf16[32,2,16,256]{3,2,1,0:T(8,128)(2,1)} %get-tuple-element.69), calls=%async_computation.3 | async-start | bytes 1048576 | tf_op jit(solution)/shard_map/all_to_all | solution.py:90
  226.6 20.3 %all-to-all-start.5 = ((bf16[32,2,16,256]{3,2,1,0:T(8,128)(2,1)}), bf16[32,2,16,256]{3,2,1,0:T(8,128)(2,1)S(1)}, u32[]{:S(2)}, u32[]{:S(2)}) async-start(bf16[32,2,16,256]{3,2,1,0:T(8,128)(2,1)} %get-tuple-element.72), calls=%async_computation.5 | async-start | bytes 1048576 | tf_op jit(solution)/shard_map/all_to_all | solution.py:90
  232.9 2.4 copy-start.3
  240.1 5.6 %copy-start.4 = (bf16[128,8,4,256]{3,1,2,0:T(8,128)(2,1)S(1)}, bf16[128,8,4,256]{3,1,2,0:T(8,128)(2,1)}, u32[]{:S(2)}) copy-start(bf16[128,8,4,256]{3,1,2,0:T(8,128)(2,1)} %copy-done.3) | copy-start | bytes 6291460
  245.7 8.0 %copy-start.18 = (bf16[32,2,16,256]{3,2,1,0:T(8,128)(2,1)S(1)}, bf16[32,2,16,256]{3,2,1,0:T(8,128)(2,1)}, u32[]{:S(2)}) copy-start(bf16[32,2,16,256]{3,2,1,0:T(8,128)(2,1)} %get-tuple-element.19) | copy-start | bytes 1572868
  245.7 8.4 %copy-start.17 = (bf16[32,2,16,256]{3,2,1,0:T(8,128)(2,1)S(1)}, bf16[32,2,16,256]{3,2,1,0:T(8,128)(2,1)}, u32[]{:S(2)}) copy-start(bf16[32,2,16,256]{3,2,1,0:T(8,128)(2,1)} %get-tuple-element.18) | copy-start | bytes 1572868
  246.4 8.1 %copy-start.16 = (bf16[32,2,16,256]{3,2,1,0:T(8,128)(2,1)S(1)}, bf16[32,2,16,256]{3,2,1,0:T(8,128)(2,1)}, u32[]{:S(2)}) copy-start(bf16[32,2,16,256]{3,2,1,0:T(8,128)(2,1)} %get-tuple-element.17) | copy-start | bytes 1572868
  246.9 24.7 %all-to-all-start.7 = ((bf16[32,2,16,256]{3,2,1,0:T(8,128)(2,1)}), bf16[32,2,16,256]{3,2,1,0:T(8,128)(2,1)}, u32[]{:S(2)}, u32[]{:S(2)}) async-start(bf16[32,2,16,256]{3,2,1,0:T(8,128)(2,1)} %get-tuple-element.71), calls=%async_computation.7 | async-start | bytes 1048576 | tf_op jit(solution)/shard_map/all_to_all | solution.py:90
  257.2 2.4 copy-start.5
  264.6 5.9 %copy-start.6 = (bf16[128,8,4,256]{3,1,2,0:T(8,128)(2,1)S(1)}, bf16[128,8,4,256]{3,1,2,0:T(8,128)(2,1)}, u32[]{:S(2)}) copy-start(bf16[128,8,4,256]{3,1,2,0:T(8,128)(2,1)} %copy-done.5) | copy-start | bytes 6291460
  270.4 9.0 %copy-start.15 = (bf16[32,2,16,256]{3,2,1,0:T(8,128)(2,1)S(1)}, bf16[32,2,16,256]{3,2,1,0:T(8,128)(2,1)}, u32[]{:S(2)}) copy-start(bf16[32,2,16,256]{3,2,1,0:T(8,128)(2,1)} %get-tuple-element.23) | copy-start | bytes 1572868
  270.4 9.4 %copy-start.14 = (bf16[32,2,16,256]{3,2,1,0:T(8,128)(2,1)S(1)}, bf16[32,2,16,256]{3,2,1,0:T(8,128)(2,1)}, u32[]{:S(2)}) copy-start(bf16[32,2,16,256]{3,2,1,0:T(8,128)(2,1)} %get-tuple-element.22) | copy-start | bytes 1572868
  271.2 9.1 %copy-start.13 = (bf16[32,2,16,256]{3,2,1,0:T(8,128)(2,1)S(1)}, bf16[32,2,16,256]{3,2,1,0:T(8,128)(2,1)}, u32[]{:S(2)}) copy-start(bf16[32,2,16,256]{3,2,1,0:T(8,128)(2,1)} %get-tuple-element.21) | copy-start | bytes 1572868
  271.7 28.0 %all-to-all-start.9 = ((bf16[32,2,16,256]{3,2,1,0:T(8,128)(2,1)}), bf16[32,2,16,256]{3,2,1,0:T(8,128)(2,1)}, u32[]{:S(2)}, u32[]{:S(2)}) async-start(bf16[32,2,16,256]{3,2,1,0:T(8,128)(2,1)} %get-tuple-element.70), calls=%async_computation.9 | async-start | bytes 1048576 | tf_op jit(solution)/shard_map/all_to_all | solution.py:90
  282.9 2.4 copy-start.7
  290.1 5.6 %copy-start.8 = (bf16[128,8,4,256]{3,1,2,0:T(8,128)(2,1)S(1)}, bf16[128,8,4,256]{3,1,2,0:T(8,128)(2,1)}, u32[]{:S(2)}) copy-start(bf16[128,8,4,256]{3,1,2,0:T(8,128)(2,1)} %copy-done.7) | copy-start | bytes 6291460
  295.7 5.3 %copy-start.12 = (bf16[32,2,16,256]{3,2,1,0:T(8,128)(2,1)S(1)}, bf16[32,2,16,256]{3,2,1,0:T(8,128)(2,1)}, u32[]{:S(2)}) copy-start(bf16[32,2,16,256]{3,2,1,0:T(8,128)(2,1)} %get-tuple-element.27) | copy-start | bytes 1572868
  295.8 5.8 %copy-start.11 = (bf16[32,2,16,256]{3,2,1,0:T(8,128)(2,1)S(1)}, bf16[32,2,16,256]{3,2,1,0:T(8,128)(2,1)}, u32[]{:S(2)}) copy-start(bf16[32,2,16,256]{3,2,1,0:T(8,128)(2,1)} %get-tuple-element.26) | copy-start | bytes 1572868
  295.8 6.2 %copy-start.10 = (bf16[32,2,16,256]{3,2,1,0:T(8,128)(2,1)S(1)}, bf16[32,2,16,256]{3,2,1,0:T(8,128)(2,1)}, u32[]{:S(2)}) copy-start(bf16[32,2,16,256]{3,2,1,0:T(8,128)(2,1)} %get-tuple-element.25) | copy-start | bytes 1572868
  304.6 2.4 copy-start.1
  312.2 5.4 %copy-start.2 = (bf16[128,8,4,256]{3,1,2,0:T(8,128)(2,1)S(1)}, bf16[128,8,4,256]{3,1,2,0:T(8,128)(2,1)}, u32[]{:S(2)}) copy-start(bf16[128,8,4,256]{3,1,2,0:T(8,128)(2,1)} %copy-done.1) | copy-start | bytes 6291460
  317.6 23.3 %copy-start.9 = (bf16[2,8,16,4,256]{4,2,0,1,3:T(8,128)(2,1)S(1)}, bf16[2,8,16,4,256]{4,2,0,1,3:T(8,128)(2,1)}, u32[]{:S(2)}) copy-start(bf16[2,8,16,4,256]{4,2,0,1,3:T(8,128)(2,1)} %copy.72) | copy-start | bytes 1572868

commit v8 on v7

--- a/solution.py
+++ b/solution.py
@@ -137,8 +137,9 @@
         bc = nb // nst
         out = beam.reshape(2, nst, bc, nblk, nt).transpose(3, 1, 0, 2, 4).reshape(ndev, 2, bc, nt)
         prev = out
-        got.append(lax.all_to_all(out, AXES, split_axis=0, concat_axis=0, tiled=True))
-    res = jnp.stack(got, axis=4).transpose(1, 2, 3, 0, 4).reshape(2, bc, nt, ndev * kc)
+        got.append(out)
+    sent = lax.all_to_all(jnp.stack(got, axis=1), AXES, split_axis=0, concat_axis=0, tiled=True)
+    res = sent.transpose(2, 3, 4, 0, 1).reshape(2, bc, nt, ndev * kc)
     return res[:, :, None]
 
 

time: 408 us -> 447 us (1.096)
  waiting for transfers between devices: 56.2 us -> 91.7 us
  blocking collectives: 77.4 us -> 55.8 us
  matrix products: 41.9 us -> 54.7 us
  other arithmetic: 130 us -> 140 us
  local copies, waits for them, and re-layouts: 57 us -> 63.6 us
    all_to_all x3, waiting for transfers between devices: 48.2 us -> 79.5 us  [local(): lax.all_to_all(send, AXES, split_axis=0, concat_axis=0, tiled=True)]
    all_to_all x4 -> x1, blocking collectives: 77.4 us -> 55.8 us  [local(): lax.all_to_all(jnp.stack(got, axis=1), AXES, split_axis=0, concat_axis=0,...]
  transfers between devices with their start and end apart: 7 -> 7, of which waited for: 4 -> 5; matrix products, arithmetic and copies ran while one was open for 41% -> 31% of each run, Pallas kernels for 0% -> 0%
where the time goes in v8:
time: 447 us; the launch traced here: 439 us
  other arithmetic  140 us (31%)
  waiting for transfers between devices  91.7 us (21%)
  local copies, waits for them, and re-layouts  63.6 us (14%)
  blocking collectives  55.8 us (12%)
  matrix products  54.7 us (12%)
  starting transfers between devices  29.7 us (7%)
    convert_element_type x4, other arithmetic, polyphase(): return (filtered * row_gain[None, :, None, None]).astype(jnp.bfloat16)  87.5 us
    all_to_all x3, waiting for transfers between devices, local(): lax.all_to_all(send, AXES, split_axis=0, concat_axis=0, tiled=True)  79.5 us
    all_to_all x1, blocking collectives, local(): lax.all_to_all(jnp.stack(got, axis=1), AXES, split_axis=0, concat_axis=0,...  55.8 us
    reshape x4, local copies, waits for them, and re-layouts, polyphase(): grid = samples.astype(jnp.float32).reshape(2, samples.shape[1], -1, width)  20.3 us
    dot_general x8, matrix products, local(): prod = jnp.dot(rows, both, precision=hi)  17.8 us
    all_to_all x4, starting transfers between devices, local(): lax.all_to_all(send[:, c], AXES, split_axis=0, concat_axis=0, tiled=True)  16.7 us
    dot_general x16, matrix products, transform(): jnp.einsum('stc,ck->stk', a, b, preferred_element_type=jnp.float32)  15.4 us
    dot_general x4, matrix products, local(): gram = jnp.dot(spec, spec.T, preferred_element_type=jnp.float32)  13.4 us
  transfers between devices with their start and end apart: 7, of which 5 were waited for; matrix products, arithmetic and copies ran while one was open for 31% of the time, Pallas kernels for 0%

profile of v8, /device:TPU:0, one launch (start us, length us, event | category | flops | bytes accessed | tf_op | source)
XLA Modules:
  0.0 439.3 jit_solution(12274770780418743266)
XLA Ops:
  1.0 9.8 %slice_convert_fusion = (f32[2,16,34176]{2,1,0:T(8,128)}, f32[2,16,34176]{2,1,0:T(8,128)}, f32[2,16,34176]{2,1,0:T(8,128)}, f32[2,16,34176]{2,1,0:T(8,128)}) fusion(bf16[2,64,34176]{2,1,0:T(8,128)(2,1)} %bitcast.207), kind=kLoop, calls=%fused_computation.100 | loop fusion | flops 4374528 | bytes 26247168 | tf_op jit(solution)/shard_map/reshape | solution.py:26
  10.8 5.1 %reshape.167 = f32[2,16,267,128]{3,2,1,0:T(8,128)} reshape(f32[2,16,34176]{2,1,0:T(8,128)} %get-tuple-element.49) | data formatting | bytes 8749056 | tf_op jit(solution)/shard_map/reshape | solution.py:26
  16.0 21.9 %fusion.2 = bf16[2,16,256,128]{3,2,1,0:T(8,128)(2,1)S(1)} fusion(f32[2,16,267,128]{3,2,1,0:T(8,128)} %reshape.167, f32[16]{0:T(128)S(1)} %get-tuple-element.117, f32[128]{0:T(128)S(1)} %get-tuple-element.115, f32[128]{0:T(128)S(1)} %get-tuple-element.116, f32[128]{0:T(128)S(1)} %get-tuple-element.106, f32[128]{0:T(128)S(1)} %get-tuple-element.107, ...), kind=kLoop, calls=%fused_computation.3 | loop fusion | flops 26214400 | bytes 52435008 | tf_op jit(solution)/shard_map/convert_element_type | solution.py:34
  45.0 3.3 subtract_convert_fusion
  51.8 7.6 %all-to-all-start.4 = ((bf16[32,2,16,256]{3,2,1,0:T(8,128)(2,1)}), bf16[32,2,16,256]{3,2,1,0:T(8,128)(2,1)S(1)}, u32[]{:S(2)}, u32[]{:S(2)}) async-start(bf16[32,2,16,256]{3,2,1,0:T(8,128)(2,1)} %get-tuple-element.72), calls=%async_computation.4 | async-start | bytes 1048576 | tf_op jit(solution)/shard_map/all_to_all | solution.py:90
  59.4 5.1 %reshape.165 = f32[2,16,267,128]{3,2,1,0:T(8,128)} reshape(f32[2,16,34176]{2,1,0:T(8,128)} %get-tuple-element.50) | data formatting | bytes 8749056 | tf_op jit(solution)/shard_map/reshape | solution.py:26
  64.5 21.9 %fusion.15 = bf16[2,16,256,128]{3,2,1,0:T(8,128)(2,1)S(1)} fusion(f32[2,16,267,128]{3,2,1,0:T(8,128)} %reshape.165, f32[16]{0:T(128)S(1)} %get-tuple-element.118, f32[128]{0:T(128)S(1)} %get-tuple-element.115, f32[128]{0:T(128)S(1)} %get-tuple-element.116, f32[128]{0:T(128)S(1)} %get-tuple-element.106, f32[128]{0:T(128)S(1)} %get-tuple-element.107, ...), kind=kLoop, calls=%fused_computation.28 | loop fusion | flops 26214400 | bytes 52435008 | tf_op jit(solution)/shard_map/convert_element_type | solution.py:34
  91.7 6.6 %all-to-all-start.2 = ((bf16[32,4,2,16,256]{4,3,2,1,0:T(8,128)(2,1)}), bf16[32,4,2,16,256]{4,3,2,1,0:T(8,128)(2,1)}, u32[]{:S(2)}, u32[]{:S(2)}) async-start(bf16[32,4,2,16,256]{4,3,2,1,0:T(8,128)(2,1)} %maximum_bitcast_fusion.2), calls=%async_computation.2 | async-start | bytes 4194304 | tf_op jit(solution)/shard_map/all_to_all | solution.py:87
  98.3 5.1 %reshape.163 = f32[2,16,267,128]{3,2,1,0:T(8,128)} reshape(f32[2,16,34176]{2,1,0:T(8,128)} %get-tuple-element.51) | data formatting | bytes 8749056 | tf_op jit(solution)/shard_map/reshape | solution.py:26
  103.3 21.9 %fusion.28 = bf16[2,16,256,128]{3,2,1,0:T(8,128)(2,1)S(1)} fusion(f32[2,16,267,128]{3,2,1,0:T(8,128)} %reshape.163, f32[16]{0:T(128)S(1)} %get-tuple-element.119, f32[128]{0:T(128)S(1)} %get-tuple-element.115, f32[128]{0:T(128)S(1)} %get-tuple-element.116, f32[128]{0:T(128)S(1)} %get-tuple-element.106, f32[128]{0:T(128)S(1)} %get-tuple-element.107, ...), kind=kLoop, calls=%fused_computation.53 | loop fusion | flops 26214400 | bytes 52435008 | tf_op jit(solution)/shard_map/convert_element_type | solution.py:34
  130.6 17.7 %all-to-all-done.2 = bf16[32,4,2,16,256]{4,3,2,1,0:T(8,128)(2,1)} async-done(((bf16[32,4,2,16,256]{4,3,2,1,0:T(8,128)(2,1)}), bf16[32,4,2,16,256]{4,3,2,1,0:T(8,128)(2,1)}, u32[]{:S(2)}, u32[]{:S(2)}) %all-to-all-start.2) | async-done | bytes 2097184 | tf_op jit(solution)/shard_map/all_to_all | solution.py:87
  148.3 3.6 all-to-all-start.1
  152.0 5.1 %reshape.161 = f32[2,16,267,128]{3,2,1,0:T(8,128)} reshape(f32[2,16,34176]{2,1,0:T(8,128)} %get-tuple-element.52) | data formatting | bytes 8749056 | tf_op jit(solution)/shard_map/reshape | solution.py:26
  157.0 21.9 %fusion.41 = bf16[2,16,256,128]{3,2,1,0:T(8,128)(2,1)S(1)} fusion(f32[2,16,267,128]{3,2,1,0:T(8,128)} %reshape.161, f32[16]{0:T(128)S(1)} %get-tuple-element.120, f32[128]{0:T(128)S(1)} %get-tuple-element.115, f32[128]{0:T(128)S(1)} %get-tuple-element.116, f32[128]{0:T(128)S(1)} %get-tuple-element.106, f32[128]{0:T(128)S(1)} %get-tuple-element.107, ...), kind=kLoop, calls=%fused_computation.78 | loop fusion | flops 26214400 | bytes 52435008 | tf_op jit(solution)/shard_map/convert_element_type | solution.py:34
  184.2 17.8 %all-to-all-done.1 = bf16[32,4,2,16,256]{4,3,2,1,0:T(8,128)(2,1)} async-done(((bf16[32,4,2,16,256]{4,3,2,1,0:T(8,128)(2,1)}), bf16[32,4,2,16,256]{4,3,2,1,0:T(8,128)(2,1)}, u32[]{:S(2)}, u32[]{:S(2)}) %all-to-all-start.1) | async-done | bytes 2097184 | tf_op jit(solution)/shard_map/all_to_all | solution.py:87
  202.0 2.7 all-to-all-start
  204.9 2.9 fusion.382
  207.8 2.9 fusion.381
  210.8 44.1 %all-to-all-done = bf16[32,4,2,16,256]{4,3,2,1,0:T(8,128)(2,1)S(1)} async-done(((bf16[32,4,2,16,256]{4,3,2,1,0:T(8,128)(2,1)}), bf16[32,4,2,16,256]{4,3,2,1,0:T(8,128)(2,1)S(1)}, u32[]{:S(2)}, u32[]{:S(2)}) %all-to-all-start) | async-done | bytes 2097184 | tf_op jit(solution)/shard_map/all_to_all | solution.py:87
  254.8 2.8 all-to-all-start.6
  264.2 4.3 fusion.385
  268.5 5.5 %all-to-all-done.6 = bf16[32,2,16,256]{3,2,1,0:T(8,128)(2,1)S(1)} async-done(((bf16[32,2,16,256]{3,2,1,0:T(8,128)(2,1)}), bf16[32,2,16,256]{3,2,1,0:T(8,128)(2,1)S(1)}, u32[]{:S(2)}, u32[]{:S(2)}) %all-to-all-start.6) | async-done | bytes 524320 | tf_op jit(solution)/shard_map/all_to_all | solution.py:90
  274.0 2.6 all-to-all-start.5
  281.9 4.3 fusion.387
  286.2 6.7 %all-to-all-done.5 = bf16[32,2,16,256]{3,2,1,0:T(8,128)(2,1)S(1)} async-done(((bf16[32,2,16,256]{3,2,1,0:T(8,128)(2,1)}), bf16[32,2,16,256]{3,2,1,0:T(8,128)(2,1)S(1)}, u32[]{:S(2)}, u32[]{:S(2)}) %all-to-all-start.5) | async-done | bytes 524320 | tf_op jit(solution)/shard_map/all_to_all | solution.py:90
  293.0 3.7 all-to-all-start.3
  300.6 2.8 pad_maximum_fusion.3
  303.4 2.1 fusion.82
  306.8 2.1 copy.105
  308.9 2.4 fusion.386
  311.3 2.5 fusion.80
  316.2 2.7 copy.53
  319.4 2.4 fusion.384
  321.8 2.5 fusion.76
  325.0 2.3 broadcast_divide_fusion.7
  327.3 3.6 fusion.55
  332.9 4.5 %fusion.230 = (f32[512,128]{0,1:T(8,128)S(1)}, f32[512,128]{0,1:T(8,128)S(1)}, f32[512,128]{0,1:T(8,128)S(1)}, f32[512,128]{0,1:T(8,128)S(1)}, f32[512,128]{0,1:...) fusion(f32[1024,256]{0,1:T(8,128)S(1)} %fusion.59, f32[]{:T(128)S(6)} %add.411, ...), kind=kLoop, calls=%fused_computation.364 | loop fusion | flops 6029312 | bytes 4464664 | tf_op jit(solution)/shard_map/add | solution.py:127
  337.4 2.0 fusion.57
  341.0 2.0 fusion.56
  348.8 2.0 fusion.53
  350.9 2.5 fusion.170
  353.4 2.0 fusion.52
  355.5 3.8 fusion.368
  359.3 3.7 fusion.238
  364.6 2.5 fusion.61
  369.5 3.4 fusion.62
  379.8 55.8 %all_to_all.40 = bf16[32,4,2,16,256]{4,3,2,1,0:T(8,128)(2,1)S(1)} all-to-all(bf16[32,4,2,16,256]{4,3,2,1,0:T(8,128)(2,1)S(1)} %copy.82), channel_id=1, replica_groups=mesh['blk'=4,'st'=8] {'blk','st'}, dimensions={0} | all-to-all | bytes 4194304 | tf_op jit(solution)/shard_map/all_to_all | solution.py:141
  436.0 2.9 copy.84
  (132 shorter events, 65.9 us)
Async XLA Ops:
  10.8 5.1 %copy-start.26 = (f32[64]{0:T(128)S(1)}, f32[64]{0:T(128)}, u32[]{:S(2)}) copy-start(f32[64]{0:T(128)} %param.7) | copy-start | bytes 772
  10.8 5.1 %copy-start.27 = (s32[1,64]{1,0:T(1,128)S(1)}, s32[1,64]{1,0:T(1,128)}, u32[]{:S(2)}) copy-start(s32[1,64]{1,0:T(1,128)} %param.8) | copy-start | bytes 772
  45.0 5.3 %copy-start.7 = (bf16[1,16,256,32,4]{2,1,0,3,4:T(8,128)(2,1)S(1)}, bf16[1,16,256,32,4]{2,1,0,3,4:T(8,128)(2,1)}, u32[]{:S(2)}) copy-start(bf16[1,16,256,32,4]{2,1,0,3,4:T(8,128)(2,1)} %copy.51) | copy-start | bytes 3145732
  51.8 39.9 %all-to-all-start.4 = ((bf16[32,2,16,256]{3,2,1,0:T(8,128)(2,1)}), bf16[32,2,16,256]{3,2,1,0:T(8,128)(2,1)S(1)}, u32[]{:S(2)}, u32[]{:S(2)}) async-start(bf16[32,2,16,256]{3,2,1,0:T(8,128)(2,1)} %get-tuple-element.72), calls=%async_computation.4 | async-start | bytes 1048576 | tf_op jit(solution)/shard_map/all_to_all | solution.py:90
  91.7 56.6 %all-to-all-start.2 = ((bf16[32,4,2,16,256]{4,3,2,1,0:T(8,128)(2,1)}), bf16[32,4,2,16,256]{4,3,2,1,0:T(8,128)(2,1)}, u32[]{:S(2)}, u32[]{:S(2)}) async-start(bf16[32,4,2,16,256]{4,3,2,1,0:T(8,128)(2,1)} %maximum_bitcast_fusion.2), calls=%async_computation.2 | async-start | bytes 4194304 | tf_op jit(solution)/shard_map/all_to_all | solution.py:87
  148.3 53.7 %all-to-all-start.1 = ((bf16[32,4,2,16,256]{4,3,2,1,0:T(8,128)(2,1)}), bf16[32,4,2,16,256]{4,3,2,1,0:T(8,128)(2,1)}, u32[]{:S(2)}, u32[]{:S(2)}) async-start(bf16[32,4,2,16,256]{4,3,2,1,0:T(8,128)(2,1)} %maximum_bitcast_fusion.1), calls=%async_computation.1 | async-start | bytes 4194304 | tf_op jit(solution)/shard_map/all_to_all | solution.py:87
  182.7 22.0 %copy-start.22 = (s32[512,128]{1,0:T(8,128)S(1)}, s32[512,128]{1,0:T(8,128)}, u32[]{:S(2)}) copy-start(s32[512,128]{1,0:T(8,128)} %param.9) | copy-start | bytes 786436
  202.0 52.8 %all-to-all-start = ((bf16[32,4,2,16,256]{4,3,2,1,0:T(8,128)(2,1)}), bf16[32,4,2,16,256]{4,3,2,1,0:T(8,128)(2,1)S(1)}, u32[]{:S(2)}, u32[]{:S(2)}) async-start(bf16[32,4,2,16,256]{4,3,2,1,0:T(8,128)(2,1)} %maximum_bitcast_fusion), calls=%async_computation | async-start | bytes 4194304 | tf_op jit(solution)/shard_map/all_to_all | solution.py:87
  254.8 19.2 %all-to-all-start.6 = ((bf16[32,2,16,256]{3,2,1,0:T(8,128)(2,1)}), bf16[32,2,16,256]{3,2,1,0:T(8,128)(2,1)S(1)}, u32[]{:S(2)}, u32[]{:S(2)}) async-start(bf16[32,2,16,256]{3,2,1,0:T(8,128)(2,1)} %get-tuple-element.70), calls=%async_computation.6 | async-start | bytes 1048576 | tf_op jit(solution)/shard_map/all_to_all | solution.py:90
  257.7 1.6 copy-start.20
  257.7 2.0 copy-start.18
  262.8 1.4 copy-start.8
  264.2 12.4 %copy-start.19 = (bf16[32,2,16,256]{3,2,1,0:T(8,128)(2,1)S(1)}, bf16[32,2,16,256]{3,2,1,0:T(8,128)(2,1)}, u32[]{:S(2)}) copy-start(bf16[32,2,16,256]{3,2,1,0:T(8,128)(2,1)} %get-tuple-element.25) | copy-start | bytes 1572868
  264.2 12.8 %copy-start.17 = (bf16[32,2,16,256]{3,2,1,0:T(8,128)(2,1)S(1)}, bf16[32,2,16,256]{3,2,1,0:T(8,128)(2,1)}, u32[]{:S(2)}) copy-start(bf16[32,2,16,256]{3,2,1,0:T(8,128)(2,1)} %get-tuple-element.26) | copy-start | bytes 1572868
  264.2 13.3 %copy-start.16 = (bf16[32,2,16,256]{3,2,1,0:T(8,128)(2,1)S(1)}, bf16[32,2,16,256]{3,2,1,0:T(8,128)(2,1)}, u32[]{:S(2)}) copy-start(bf16[32,2,16,256]{3,2,1,0:T(8,128)(2,1)} %get-tuple-element.27) | copy-start | bytes 1572868
  274.0 19.0 %all-to-all-start.5 = ((bf16[32,2,16,256]{3,2,1,0:T(8,128)(2,1)}), bf16[32,2,16,256]{3,2,1,0:T(8,128)(2,1)S(1)}, u32[]{:S(2)}, u32[]{:S(2)}) async-start(bf16[32,2,16,256]{3,2,1,0:T(8,128)(2,1)} %get-tuple-element.71), calls=%async_computation.5 | async-start | bytes 1048576 | tf_op jit(solution)/shard_map/all_to_all | solution.py:90
  278.3 2.3 copy-start.5
  280.6 1.3 copy-start.10
  281.9 17.9 %copy-start.15 = (bf16[32,2,16,256]{3,2,1,0:T(8,128)(2,1)S(1)}, bf16[32,2,16,256]{3,2,1,0:T(8,128)(2,1)}, u32[]{:S(2)}) copy-start(bf16[32,2,16,256]{3,2,1,0:T(8,128)(2,1)} %get-tuple-element.23) | copy-start | bytes 1572868
  293.0 21.5 %all-to-all-start.3 = ((bf16[32,2,16,256]{3,2,1,0:T(8,128)(2,1)}), bf16[32,2,16,256]{3,2,1,0:T(8,128)(2,1)}, u32[]{:S(2)}, u32[]{:S(2)}) async-start(bf16[32,2,16,256]{3,2,1,0:T(8,128)(2,1)} %get-tuple-element.69), calls=%async_computation.3 | async-start | bytes 1048576 | tf_op jit(solution)/shard_map/all_to_all | solution.py:90
  296.7 6.7 %copy-start.6 = (f32[1024,1024]{1,0:T(8,128)S(1)}, f32[1024,1024]{1,0:T(8,128)}, u32[]{:S(2)}) copy-start(f32[1024,1024]{1,0:T(8,128)} %fusion.387) | copy-start | bytes 12582916
  308.9 2.4 copy-start.12
  319.4 2.4 copy-start.13
  324.9 6.0 %copy-start.3 = (f32[512,512]{1,0:T(8,128)S(1)}, f32[512,512]{1,0:T(8,128)}, u32[]{:S(2)}) copy-start(f32[512,512]{1,0:T(8,128)} %get-tuple-element.39) | copy-start | bytes 3145732
  324.9 6.0 %copy-start.4 = (f32[512,512]{1,0:T(8,128)S(1)}, f32[512,512]{1,0:T(8,128)}, u32[]{:S(2)}) copy-start(f32[512,512]{1,0:T(8,128)} %get-tuple-element.53) | copy-start | bytes 3145732
  339.5 5.2 %copy-start.1 = (f32[512,512]{1,0:T(8,128)S(1)}, f32[512,512]{1,0:T(8,128)}, u32[]{:S(2)}) copy-start(f32[512,512]{1,0:T(8,128)} %get-tuple-element.45) | copy-start | bytes 3145732
  339.5 5.2 %copy-start.2 = (f32[512,512]{1,0:T(8,128)S(1)}, f32[512,512]{1,0:T(8,128)}, u32[]{:S(2)}) copy-start(f32[512,512]{1,0:T(8,128)} %get-tuple-element.55) | copy-start | bytes 3145732
  343.0 5.8 %copy-start = (f32[512,512]{1,0:T(8,128)S(1)}, f32[512,512]{1,0:T(8,128)}, u32[]{:S(2)}) copy-start(f32[512,512]{1,0:T(8,128)} %get-tuple-element.56) | copy-start | bytes 3145732
  353.4 9.6 %copy-start.14 = (bf16[128,8,4,256]{3,1,2,0:T(8,128)(2,1)S(1)}, bf16[128,8,4,256]{3,1,2,0:T(8,128)(2,1)}, u32[]{:S(2)}) copy-start(bf16[128,8,4,256]{3,1,2,0:T(8,128)(2,1)} %copy-done.13) | copy-start | bytes 6291460
  363.0 1.6 copy-start.9
  363.0 1.6 copy-start.23
  368.6 6.6 %copy-start.11 = (bf16[128,8,4,256]{3,1,2,0:T(8,128)(2,1)S(1)}, bf16[128,8,4,256]{3,1,2,0:T(8,128)(2,1)}, u32[]{:S(2)}) copy-start(bf16[128,8,4,256]{3,1,2,0:T(8,128)(2,1)} %copy-done.10) | copy-start | bytes 6291460
  368.6 6.6 %copy-start.24 = (bf16[512,128]{0,1:T(8,128)(2,1)S(1)}, bf16[512,128]{0,1:T(8,128)(2,1)}, u32[]{:S(2)}) copy-start(bf16[512,128]{0,1:T(8,128)(2,1)} %get-tuple-element.90) | copy-start | bytes 393220
  368.6 6.6 %copy-start.25 = (bf16[512,128]{0,1:T(8,128)(2,1)S(1)}, bf16[512,128]{0,1:T(8,128)(2,1)}, u32[]{:S(2)}) copy-start(bf16[512,128]{0,1:T(8,128)(2,1)} %get-tuple-element.103) | copy-start | bytes 393220
  375.2 3.1 copy-start.21

commit v9 on v7

--- a/solution.py
+++ b/solution.py
@@ -32,6 +32,20 @@
             + filter_coeffs[tap_no][None, None, None, :] * grid[:, :, tap_no : tap_no + count, :]
         )
     return (filtered * row_gain[None, :, None, None]).astype(jnp.bfloat16)
+
+
+def polyphase_flat(samples, filter_coeffs, row_gain):
+    ntaps = filter_coeffs.shape[0]
+    width = filter_coeffs.shape[1]
+    count = samples.shape[2] // width - ntaps + 1
+    span = count * width
+    coeffs = jnp.tile(filter_coeffs, (1, count))
+    filtered = coeffs[0][None, None, :] * samples[:, :, 0:span].astype(jnp.float32)
+    for tap_no in range(1, ntaps):
+        window = samples[:, :, tap_no * width : tap_no * width + span].astype(jnp.float32)
+        filtered = filtered + coeffs[tap_no][None, None, :] * window
+    filtered = (filtered * row_gain[None, :, None]).astype(jnp.bfloat16)
+    return filtered.reshape(samples.shape[0], samples.shape[1], count, width)
 
 
 def transform(filtered, cos_table, sin_table):
@@ -80,7 +94,7 @@
     arrived = []
     for g in range(ngr):
         part = samples[:, g * gs : (g + 1) * gs]
-        filtered = polyphase(part, filter_coeffs, row_gain[g * gs : (g + 1) * gs])
+        filtered = polyphase_flat(part, filter_coeffs, row_gain[g * gs : (g + 1) * gs])
         local_spec = transform(filtered, cos_table, sin_table)
         send = local_spec.reshape(2, gs, nt, ndev, kc).transpose(3, 4, 0, 1, 2)
         if g < ngr - 1:

time: 408 us -> 384 us (0.941)
  other arithmetic: 130 us -> 87.7 us
  waiting for transfers between devices: 56.2 us -> 97.4 us
  local copies, waits for them, and re-layouts: 57 us -> 38.3 us
    all_to_all x3, waiting for transfers between devices: 48.2 us -> 88.2 us  [local(): lax.all_to_all(send, AXES, split_axis=0, concat_axis=0, tiled=True)]
    convert_element_type x4, other arithmetic: 86.9 us -> 53.4 us  [polyphase_flat(): filtered = (filtered * row_gain[None, :, None]).astype(jnp.bfloat16)]
    reshape x4 -> x0, local copies, waits for them, and re-layouts: 20.2 us -> none  [polyphase(): grid = samples.astype(jnp.float32).reshape(2, samples.shape[1], -1, width)]
    reshape x1 -> x0, other arithmetic: 9.94 us -> none  [polyphase(): grid = samples.astype(jnp.float32).reshape(2, samples.shape[1], -1, width)]
  transfers between devices with their start and end apart: 7 -> 7, of which waited for: 4 -> 4; matrix products, arithmetic and copies ran while one was open for 41% -> 32% of each run, Pallas kernels for 0% -> 0%
where the time goes in v9:
time: 384 us; the launch traced here: 378 us
  waiting for transfers between devices  97.4 us (25%)
  other arithmetic  87.7 us (23%)
  blocking collectives  77.3 us (20%)
  matrix products  40.1 us (10%)
  local copies, waits for them, and re-layouts  38.3 us (10%)
  starting transfers between devices  33.1 us (9%)
  between operations  4.14 us (1%)
    all_to_all x3, waiting for transfers between devices, local(): lax.all_to_all(send, AXES, split_axis=0, concat_axis=0, tiled=True)  88.2 us
    all_to_all x4, blocking collectives, local(): lax.all_to_all(out, AXES, split_axis=0, concat_axis=0, tiled=True)  77.3 us
    convert_element_type x4, other arithmetic, polyphase_flat(): filtered = (filtered * row_gain[None, :, None]).astype(jnp.bfloat16)  53.4 us
    all_to_all x4, starting transfers between devices, local(): lax.all_to_all(send[:, c], AXES, split_axis=0, concat_axis=0, tiled=True)  18 us
    dot_general x8, matrix products, local(): prod = jnp.dot(rows, both, precision=hi)  16.4 us
    all_to_all x3, starting transfers between devices, local(): lax.all_to_all(send, AXES, split_axis=0, concat_axis=0, tiled=True)  15.2 us
    dot_general x16, matrix products, transform(): jnp.einsum('stc,ck->stk', a, b, preferred_element_type=jnp.float32)  11.4 us
    dot_general x4, matrix products, local(): gram = jnp.dot(spec, spec.T, preferred_element_type=jnp.float32)  9.47 us
  transfers between devices with their start and end apart: 7, of which 4 were waited for; matrix products, arithmetic and copies ran while one was open for 32% of the time, Pallas kernels for 0%

profile of v9, /device:TPU:0, one launch (start us, length us, event | category | flops | bytes accessed | tf_op | source)
XLA Modules:
  0.0 378.2 jit_solution(5678853529440243631)
XLA Ops:
  1.9 13.1 %multiply_convert_fusion.3 = bf16[2,16,32768]{2,1,0:T(8,128)(2,1)S(1)} fusion(bf16[2,64,34176]{2,1,0:T(8,128)(2,1)} %bitcast.251, f32[16]{0:T(128)S(1)} %get-tuple-element.108, f32[32768]{0:T(1024)S(1)} %get-tuple-element.109, f32[32768]{0:T(1024)S(1)} %get-tuple-element.110, f32[32768]{0:T(1024)S(1)} %get-tuple-element.111, ...), kind=kLoop, calls=%fused_computation.3 | loop fusion | flops 38797312 | bytes 28835904 | tf_op jit(solution)/shard_map/convert_element_type | solution.py:47
  19.4 1.5 maximum_bitcast_fusion
  20.9 7.5 %all-to-all-start = ((bf16[32,4,2,16,256]{4,3,2,1,0:T(8,128)(2,1)}), bf16[32,4,2,16,256]{4,3,2,1,0:T(8,128)(2,1)S(1)}, u32[]{:S(2)}, u32[]{:S(2)}) async-start(bf16[32,4,2,16,256]{4,3,2,1,0:T(8,128)(2,1)} %maximum_bitcast_fusion), calls=%async_computation | async-start | bytes 4194304 | tf_op jit(solution)/shard_map/all_to_all | solution.py:101
  28.5 13.6 %multiply_convert_fusion.2 = bf16[2,16,32768]{2,1,0:T(8,128)(2,1)S(1)} fusion(bf16[2,64,34176]{2,1,0:T(8,128)(2,1)} %bitcast.252, f32[16]{0:T(128)S(1)} %get-tuple-element.107, f32[32768]{0:T(1024)S(1)} %get-tuple-element.109, f32[32768]{0:T(1024)S(1)} %get-tuple-element.110, f32[32768]{0:T(1024)S(1)} %get-tuple-element.111, ...), kind=kLoop, calls=%fused_computation.2 | loop fusion | flops 38797312 | bytes 28835904 | tf_op jit(solution)/shard_map/convert_element_type | solution.py:47
  46.4 1.5 maximum_bitcast_fusion.1
  47.9 30.6 %all-to-all-done = bf16[32,4,2,16,256]{4,3,2,1,0:T(8,128)(2,1)S(1)} async-done(((bf16[32,4,2,16,256]{4,3,2,1,0:T(8,128)(2,1)}), bf16[32,4,2,16,256]{4,3,2,1,0:T(8,128)(2,1)S(1)}, u32[]{:S(2)}, u32[]{:S(2)}) %all-to-all-start) | async-done | bytes 2097184 | tf_op jit(solution)/shard_map/all_to_all | solution.py:101
  79.9 3.7 all-to-all-start.1
  83.6 13.3 %multiply_convert_fusion.1 = bf16[2,16,32768]{2,1,0:T(8,128)(2,1)S(1)} fusion(bf16[2,64,34176]{2,1,0:T(8,128)(2,1)} %bitcast.253, f32[16]{0:T(128)S(1)} %get-tuple-element.106, f32[32768]{0:T(1024)S(1)} %get-tuple-element.109, f32[32768]{0:T(1024)S(1)} %get-tuple-element.110, f32[32768]{0:T(1024)S(1)} %get-tuple-element.111, ...), kind=kLoop, calls=%fused_computation.1 | loop fusion | flops 38797312 | bytes 28835904 | tf_op jit(solution)/shard_map/convert_element_type | solution.py:47
  101.2 1.5 maximum_bitcast_fusion.2
  102.7 30.9 %all-to-all-done.1 = bf16[32,4,2,16,256]{4,3,2,1,0:T(8,128)(2,1)} async-done(((bf16[32,4,2,16,256]{4,3,2,1,0:T(8,128)(2,1)}), bf16[32,4,2,16,256]{4,3,2,1,0:T(8,128)(2,1)}, u32[]{:S(2)}, u32[]{:S(2)}) %all-to-all-start.1) | async-done | bytes 2097184 | tf_op jit(solution)/shard_map/all_to_all | solution.py:101
  133.7 3.9 %all-to-all-start.2 = ((bf16[32,4,2,16,256]{4,3,2,1,0:T(8,128)(2,1)}), bf16[32,4,2,16,256]{4,3,2,1,0:T(8,128)(2,1)}, u32[]{:S(2)}, u32[]{:S(2)}) async-start(bf16[32,4,2,16,256]{4,3,2,1,0:T(8,128)(2,1)} %maximum_bitcast_fusion.2), calls=%async_computation.2 | async-start | bytes 4194304 | tf_op jit(solution)/shard_map/all_to_all | solution.py:101
  137.6 13.5 %multiply_convert_fusion = bf16[2,16,32768]{2,1,0:T(8,128)(2,1)S(1)} fusion(bf16[2,64,34176]{2,1,0:T(8,128)(2,1)} %bitcast.254, f32[16]{0:T(128)S(1)} %get-tuple-element.105, f32[32768]{0:T(1024)S(1)} %get-tuple-element.109, f32[32768]{0:T(1024)S(1)} %get-tuple-element.110, f32[32768]{0:T(1024)S(1)} %get-tuple-element.111, f32[32768]{0:T(1024)S(1)} %get-tuple-element.112, ...), kind=kLoop, calls=%fused_computation | loop fusion | flops 38797312 | bytes 28835904 | tf_op jit(solution)/shard_map/convert_element_type | solution.py:47
  152.3 1.6 subtract_convert_fusion
  155.2 1.5 copy.52
  161.0 26.7 %all-to-all-done.2 = bf16[32,4,2,16,256]{4,3,2,1,0:T(8,128)(2,1)} async-done(((bf16[32,4,2,16,256]{4,3,2,1,0:T(8,128)(2,1)}), bf16[32,4,2,16,256]{4,3,2,1,0:T(8,128)(2,1)}, u32[]{:S(2)}, u32[]{:S(2)}) %all-to-all-start.2) | async-done | bytes 2097184 | tf_op jit(solution)/shard_map/all_to_all | solution.py:101
  187.7 2.6 all-to-all-start.3
  191.8 2.8 fusion.329
  194.6 2.8 fusion.330
  197.4 9.2 %all-to-all-done.3 = bf16[32,2,16,256]{3,2,1,0:T(8,128)(2,1)S(1)} async-done(((bf16[32,2,16,256]{3,2,1,0:T(8,128)(2,1)}), bf16[32,2,16,256]{3,2,1,0:T(8,128)(2,1)S(1)}, u32[]{:S(2)}, u32[]{:S(2)}) %all-to-all-start.3) | async-done | bytes 524320 | tf_op jit(solution)/shard_map/all_to_all | solution.py:104
  206.6 2.8 all-to-all-start.5
  209.7 2.7 copy.53
  212.9 2.4 fusion.332
  218.2 2.0 fusion.7
  220.2 1.4 fusion.170
  221.7 2.0 fusion.6
  227.1 6.3 %all-to-all-start.7 = ((bf16[32,2,16,256]{3,2,1,0:T(8,128)(2,1)}), bf16[32,2,16,256]{3,2,1,0:T(8,128)(2,1)}, u32[]{:S(2)}, u32[]{:S(2)}) async-start(bf16[32,2,16,256]{3,2,1,0:T(8,128)(2,1)} %get-tuple-element.67), calls=%async_computation.7 | async-start | bytes 1048576 | tf_op jit(solution)/shard_map/all_to_all | solution.py:104
  235.1 1.8 pad_maximum_fusion.1
  237.4 2.4 fusion.333
  242.5 2.0 fusion.5
  244.5 1.7 fusion.150
  246.2 2.0 fusion.4
  251.6 6.3 %all-to-all-start.9 = ((bf16[32,2,16,256]{3,2,1,0:T(8,128)(2,1)}), bf16[32,2,16,256]{3,2,1,0:T(8,128)(2,1)}, u32[]{:S(2)}, u32[]{:S(2)}) async-start(bf16[32,2,16,256]{3,2,1,0:T(8,128)(2,1)} %get-tuple-element.66), calls=%async_computation.9 | async-start | bytes 1048576 | tf_op jit(solution)/shard_map/all_to_all | solution.py:104
  257.9 1.4 copy.71
  260.6 1.8 pad_maximum_fusion.3
  262.9 2.4 fusion.334
  268.1 2.0 fusion.3
  270.1 1.4 fusion.130
  271.6 2.0 fusion.2
  277.8 1.4 copy.80
  280.5 1.8 pad_maximum_fusion.5
  282.8 2.4 fusion.335
  288.2 2.0 fusion.1
  291.5 2.0 fusion
  296.9 22.1 %all_to_all.55 = bf16[32,2,16,256]{3,2,1,0:T(8,128)(2,1)S(1)} all-to-all(bf16[32,2,16,256]{3,2,1,0:T(8,128)(2,1)S(1)} %bitcast.294), channel_id=1, replica_groups=mesh['blk'=4,'st'=8] {'blk','st'}, dimensions={0} | all-to-all | bytes 1048576 | tf_op jit(solution)/shard_map/all_to_all | solution.py:154
  319.0 18.4 %all_to_all.56 = bf16[32,2,16,256]{3,2,1,0:T(8,128)(2,1)S(1)} all-to-all(bf16[32,2,16,256]{3,2,1,0:T(8,128)(2,1)S(1)} %bitcast.292), channel_id=1, replica_groups=mesh['blk'=4,'st'=8] {'blk','st'}, dimensions={0} | all-to-all | bytes 1048576 | tf_op jit(solution)/shard_map/all_to_all | solution.py:154
  337.4 18.4 %all_to_all.57 = bf16[32,2,16,256]{3,2,1,0:T(8,128)(2,1)S(1)} all-to-all(bf16[32,2,16,256]{3,2,1,0:T(8,128)(2,1)S(1)} %bitcast.291), channel_id=1, replica_groups=mesh['blk'=4,'st'=8] {'blk','st'}, dimensions={0} | all-to-all | bytes 1048576 | tf_op jit(solution)/shard_map/all_to_all | solution.py:154
  355.9 18.4 %all_to_all.58 = bf16[32,2,16,256]{3,2,1,0:T(8,128)(2,1)S(1)} all-to-all(bf16[32,2,16,256]{3,2,1,0:T(8,128)(2,1)S(1)} %bitcast.290), channel_id=1, replica_groups=mesh['blk'=4,'st'=8] {'blk','st'}, dimensions={0} | all-to-all | bytes 1048576 | tf_op jit(solution)/shard_map/all_to_all | solution.py:154
  374.8 2.9 copy.83
  (152 shorter events, 55.2 us)
Async XLA Ops:
  1.9 13.2 %copy-start.3 = (f32[32768]{0:T(1024)}, f32[32768]{0:T(1024)S(1)}, u32[]{:S(2)}) copy-start(f32[32768]{0:T(1024)S(1)} %get-tuple-element.120) | copy-start | bytes 393220
  20.9 57.6 %all-to-all-start = ((bf16[32,4,2,16,256]{4,3,2,1,0:T(8,128)(2,1)}), bf16[32,4,2,16,256]{4,3,2,1,0:T(8,128)(2,1)S(1)}, u32[]{:S(2)}, u32[]{:S(2)}) async-start(bf16[32,4,2,16,256]{4,3,2,1,0:T(8,128)(2,1)} %maximum_bitcast_fusion), calls=%async_computation | async-start | bytes 4194304 | tf_op jit(solution)/shard_map/all_to_all | solution.py:101
  78.5 1.4 copy-start
  79.9 53.8 %all-to-all-start.1 = ((bf16[32,4,2,16,256]{4,3,2,1,0:T(8,128)(2,1)}), bf16[32,4,2,16,256]{4,3,2,1,0:T(8,128)(2,1)}, u32[]{:S(2)}, u32[]{:S(2)}) async-start(bf16[32,4,2,16,256]{4,3,2,1,0:T(8,128)(2,1)} %maximum_bitcast_fusion.1), calls=%async_computation.1 | async-start | bytes 4194304 | tf_op jit(solution)/shard_map/all_to_all | solution.py:101
  102.7 34.9 %copy-start.4 = (f32[32768]{0:T(1024)S(1)}, f32[32768]{0:T(1024)}, u32[]{:S(2)}) copy-start(f32[32768]{0:T(1024)} %copy-done.3) | copy-start | bytes 393220
  133.7 54.0 %all-to-all-start.2 = ((bf16[32,4,2,16,256]{4,3,2,1,0:T(8,128)(2,1)}), bf16[32,4,2,16,256]{4,3,2,1,0:T(8,128)(2,1)}, u32[]{:S(2)}, u32[]{:S(2)}) async-start(bf16[32,4,2,16,256]{4,3,2,1,0:T(8,128)(2,1)} %maximum_bitcast_fusion.2), calls=%async_computation.2 | async-start | bytes 4194304 | tf_op jit(solution)/shard_map/all_to_all | solution.py:101
  158.1 1.2 copy-start.2
  159.6 30.7 %copy-start.24 = (s32[512,128]{1,0:T(8,128)S(1)}, s32[512,128]{1,0:T(8,128)}, u32[]{:S(2)}) copy-start(s32[512,128]{1,0:T(8,128)} %param.9) | copy-start | bytes 786436
  159.6 30.8 %copy-start.1 = (bf16[32,4,2,16,256]{4,3,2,1,0:T(8,128)(2,1)S(1)}, bf16[32,4,2,16,256]{4,3,2,1,0:T(8,128)(2,1)}, u32[]{:S(2)}) copy-start(bf16[32,4,2,16,256]{4,3,2,1,0:T(8,128)(2,1)} %copy-done) | copy-start | bytes 6291460
  187.7 19.0 %all-to-all-start.3 = ((bf16[32,2,16,256]{3,2,1,0:T(8,128)(2,1)}), bf16[32,2,16,256]{3,2,1,0:T(8,128)(2,1)S(1)}, u32[]{:S(2)}, u32[]{:S(2)}) async-start(bf16[32,2,16,256]{3,2,1,0:T(8,128)(2,1)} %get-tuple-element.65), calls=%async_computation.3 | async-start | bytes 1048576 | tf_op jit(solution)/shard_map/all_to_all | solution.py:104
  194.6 14.8 %copy-start.23 = (bf16[32,1,2,16,256]{4,3,2,1,0:T(8,128)(2,1)S(1)}, bf16[32,1,2,16,256]{4,3,2,1,0:T(8,128)(2,1)}, u32[]{:S(2)}) copy-start(bf16[32,1,2,16,256]{4,3,2,1,0:T(8,128)(2,1)} %get-tuple-element.53) | copy-start | bytes 1572868
  206.6 20.4 %all-to-all-start.5 = ((bf16[32,2,16,256]{3,2,1,0:T(8,128)(2,1)}), bf16[32,2,16,256]{3,2,1,0:T(8,128)(2,1)S(1)}, u32[]{:S(2)}, u32[]{:S(2)}) async-start(bf16[32,2,16,256]{3,2,1,0:T(8,128)(2,1)} %get-tuple-element.68), calls=%async_computation.5 | async-start | bytes 1048576 | tf_op jit(solution)/shard_map/all_to_all | solution.py:104
  212.9 2.4 copy-start.7
  223.7 2.1 copy-start.8
  226.6 7.3 %copy-start.22 = (bf16[32,2,16,256]{3,2,1,0:T(8,128)(2,1)S(1)}, bf16[32,2,16,256]{3,2,1,0:T(8,128)(2,1)}, u32[]{:S(2)}) copy-start(bf16[32,2,16,256]{3,2,1,0:T(8,128)(2,1)} %get-tuple-element.19) | copy-start | bytes 1572868
  227.0 7.3 %copy-start.21 = (bf16[32,2,16,256]{3,2,1,0:T(8,128)(2,1)S(1)}, bf16[32,2,16,256]{3,2,1,0:T(8,128)(2,1)}, u32[]{:S(2)}) copy-start(bf16[32,2,16,256]{3,2,1,0:T(8,128)(2,1)} %get-tuple-element.18) | copy-start | bytes 1572868
  227.1 7.6 %copy-start.20 = (bf16[32,2,16,256]{3,2,1,0:T(8,128)(2,1)S(1)}, bf16[32,2,16,256]{3,2,1,0:T(8,128)(2,1)}, u32[]{:S(2)}) copy-start(bf16[32,2,16,256]{3,2,1,0:T(8,128)(2,1)} %get-tuple-element.17) | copy-start | bytes 1572868
  227.1 24.5 %all-to-all-start.7 = ((bf16[32,2,16,256]{3,2,1,0:T(8,128)(2,1)}), bf16[32,2,16,256]{3,2,1,0:T(8,128)(2,1)}, u32[]{:S(2)}, u32[]{:S(2)}) async-start(bf16[32,2,16,256]{3,2,1,0:T(8,128)(2,1)} %get-tuple-element.67), calls=%async_computation.7 | async-start | bytes 1048576 | tf_op jit(solution)/shard_map/all_to_all | solution.py:104
  237.4 2.4 copy-start.9
  248.3 2.1 copy-start.10
  251.1 8.2 %copy-start.19 = (bf16[32,2,16,256]{3,2,1,0:T(8,128)(2,1)S(1)}, bf16[32,2,16,256]{3,2,1,0:T(8,128)(2,1)}, u32[]{:S(2)}) copy-start(bf16[32,2,16,256]{3,2,1,0:T(8,128)(2,1)} %get-tuple-element.23) | copy-start | bytes 1572868
  251.5 8.3 %copy-start.18 = (bf16[32,2,16,256]{3,2,1,0:T(8,128)(2,1)S(1)}, bf16[32,2,16,256]{3,2,1,0:T(8,128)(2,1)}, u32[]{:S(2)}) copy-start(bf16[32,2,16,256]{3,2,1,0:T(8,128)(2,1)} %get-tuple-element.22) | copy-start | bytes 1572868
  251.6 8.6 %copy-start.17 = (bf16[32,2,16,256]{3,2,1,0:T(8,128)(2,1)S(1)}, bf16[32,2,16,256]{3,2,1,0:T(8,128)(2,1)}, u32[]{:S(2)}) copy-start(bf16[32,2,16,256]{3,2,1,0:T(8,128)(2,1)} %get-tuple-element.21) | copy-start | bytes 1572868
  251.6 26.1 %all-to-all-start.9 = ((bf16[32,2,16,256]{3,2,1,0:T(8,128)(2,1)}), bf16[32,2,16,256]{3,2,1,0:T(8,128)(2,1)}, u32[]{:S(2)}, u32[]{:S(2)}) async-start(bf16[32,2,16,256]{3,2,1,0:T(8,128)(2,1)} %get-tuple-element.66), calls=%async_computation.9 | async-start | bytes 1048576 | tf_op jit(solution)/shard_map/all_to_all | solution.py:104
  262.9 2.4 copy-start.11
  273.6 2.1 copy-start.12
  276.5 2.8 copy-start.16
  276.5 3.2 copy-start.15
  276.9 3.2 copy-start.14
  282.8 2.4 copy-start.5
  293.6 2.1 copy-start.6
  296.4 22.6 %copy-start.13 = (bf16[2,8,16,4,256]{4,2,0,1,3:T(8,128)(2,1)S(1)}, bf16[2,8,16,4,256]{4,2,0,1,3:T(8,128)(2,1)}, u32[]{:S(2)}) copy-start(bf16[2,8,16,4,256]{4,2,0,1,3:T(8,128)(2,1)} %copy.72) | copy-start | bytes 1572868
